TPU v7x, 512 devices: a whole 4x4x16 slice. The times are simulated.
512 devices in a mesh: span: 32 (over x, z_lo, core), chord: 16 (over z_hi, y).
Axes of the slice: x: 4, y: 4, z: 16 (z_hi: 4, z_lo: 4; z = z_hi * 4 + z_lo), core: 2. Of those that a mesh axis runs over, the one named last changes fastest.
Arguments:
- adj_rhs: bfloat16 [64, 64, 320, 128], P('span', 'chord'), may hold values from -6 to 6
- diag_inv: bfloat16 [64, 64, 320, 320], P('span', 'chord'), may hold values from -0.3125 to 0.3125
- face_jac: bfloat16 [64, 64, 4, 80, 320], P('span', 'chord'), may hold values from -0.15625 to 0.15625
- face_mask: int32 [64, 64, 4], P('span', 'chord'), may hold values 0 or 1
- wall_map: int32 [64, 64, 16], P('span', 'chord'), may hold values from 0 to 1023
- couple: float32 [6, 5], replicated, may hold values from -3 to 3
- shell_rhs: bfloat16 [32768, 6, 128], P(('span', 'chord')), may hold values from -6 to 6
- shell_inv: float32 [32768, 6, 6], P(('span', 'chord')), may hold values from -2.5 to 2.5
Outputs:
- fluid_adjoint: bfloat16 [64, 64, 320, 128], P('span', 'chord')
- shell_adjoint: bfloat16 [32768, 6, 128], P(('span', 'chord'))
All inputs are finite; a program needn't handle non-finite values. No bound on the sum of `face_mask` on one device may be relied on, other than what follows from the above.
Results may differ from a plain program's by a relative error of at most 0.0063.
Values may be sent and summed in bfloat16 or wider, within the bound.
No kernel may reach another device: no remote copies, remote signals or barrier semaphores. Data moves between devices by JAX's collectives and lax.ppermute only.
A program may use at most 64 MiB of HBM per device.

v0:
```python
import jax
import jax.numpy as jnp
from jax import lax
from jax.sharding import PartitionSpec as P

NV = 5
ITERS = 3


def passed_along(block, axis, distance):
    devices = range(lax.axis_size(axis))
    route = [(i - distance, i) for i in devices if i - distance in devices]
    return lax.ppermute(block, axis, route)


def assemble(adj_rhs, low_span, high_span, low_chord, high_chord, wall_in):
    rows, cols, blk, width = adj_rhs.shape
    resid = adj_rhs.astype(jnp.float32).reshape(rows, cols, 4, 4, 4, NV, width)
    resid = resid.at[:, :, 0].add(
        -low_span.astype(jnp.float32).reshape(rows, cols, 4, 4, NV, width)
    )
    resid = resid.at[:, :, 3].add(
        -high_span.astype(jnp.float32).reshape(rows, cols, 4, 4, NV, width)
    )
    resid = resid.at[:, :, :, 0].add(
        -low_chord.astype(jnp.float32).reshape(rows, cols, 4, 4, NV, width)
    )
    resid = resid.at[:, :, :, 3].add(
        -high_chord.astype(jnp.float32).reshape(rows, cols, 4, 4, NV, width)
    )
    resid = resid.at[:, :, :, :, 0].add(-wall_in.reshape(rows, cols, 4, 4, NV, width))
    return resid.reshape(rows, cols, blk, width).astype(jnp.bfloat16)


def pass_span(moving, offset):
    rim_row = moving[-1:] if offset == 1 else moving[:1]
    arrived = passed_along(rim_row, "span", offset)
    if offset == 1:
        return jnp.concatenate([arrived, moving[:-1]], 0)
    return jnp.concatenate([moving[1:], arrived], 0)


def pass_chord(moving, offset):
    rim_col = moving[:, -1:] if offset == 1 else moving[:, :1]
    arrived = passed_along(rim_col, "chord", offset)
    if offset == 1:
        return jnp.concatenate([arrived, moving[:, :-1]], 1)
    return jnp.concatenate([moving[:, 1:], arrived], 1)


def face_terms(sent):
    low_span = pass_span(sent[:, :, 0], 1)
    high_span = pass_span(sent[:, :, 1], -1)
    low_chord = pass_chord(sent[:, :, 2], 1)
    high_chord = pass_chord(sent[:, :, 3], -1)
    return (low_span, high_span, low_chord, high_chord)


def per_device(adj_rhs, diag_inv, face_jac, face_mask, wall_map, couple, shell_rhs, shell_inv):
    high = lax.Precision.HIGHEST
    rows, cols, blk, width = adj_rhs.shape
    shell_count = shell_rhs.shape[0]
    chord_pos = lax.axis_index("chord")
    my_nodes = chord_pos * shell_count + lax.iota(jnp.int32, shell_count)
    wall_local = wall_map.reshape(-1)
    wall_count = wall_local.shape[0]
    strip_ids = lax.all_gather(wall_local, "chord", axis=0, tiled=True)
    fluid = jnp.einsum(
        "abmn,abnr->abmr", diag_inv, adj_rhs, preferred_element_type=jnp.float32
    ).astype(jnp.bfloat16)
    shell = jnp.einsum(
        "nst,ntr->nsr", shell_inv, shell_rhs.astype(jnp.float32), precision=high
    ).astype(jnp.bfloat16)
    weights = face_mask.astype(jnp.float32)[:, :, :, None, None]
    for step in range(1, ITERS):
        sent = jnp.einsum("abdmn,abnr->abdmr", face_jac, fluid, preferred_element_type=jnp.float32)
        sent = (sent * weights).astype(jnp.bfloat16)
        low_span, high_span, low_chord, high_chord = face_terms(sent)
        pick_piece = lax.all_gather(shell, "chord", axis=0, tiled=True)
        pick_count = pick_piece.shape[0]
        pick_hit = (wall_local[:, None] == lax.iota(jnp.int32, pick_count)[None, :]).astype(
            jnp.float32
        )
        picked = jnp.einsum("wn,nsr->wsr", pick_hit, pick_piece.astype(jnp.float32), precision=high)
        wall_in = jnp.einsum("sv,wsr->wvr", couple, picked, precision=high)
        wall_rows = fluid.reshape(rows, cols, 4, 4, 4, NV, width)[:, :, :, :, 0].reshape(
            wall_count, NV, width
        )
        piece = lax.all_gather(wall_rows, "chord", axis=0, tiled=True)
        hit = (my_nodes[:, None] == strip_ids[None, :]).astype(jnp.float32)
        summed = jnp.einsum("nw,wvr->nvr", hit, piece.astype(jnp.float32), precision=high)
        shell_load = jnp.einsum("sv,nvr->nsr", couple, summed, precision=high)
        wall_in, shell_load = (wall_in, shell_load)
        resid = assemble(adj_rhs, low_span, high_span, low_chord, high_chord, wall_in)
        fluid = jnp.einsum(
            "abmn,abnr->abmr", diag_inv, resid, preferred_element_type=jnp.float32
        ).astype(jnp.bfloat16)
        shell = jnp.einsum(
            "nst,ntr->nsr", shell_inv, shell_rhs.astype(jnp.float32) - shell_load, precision=high
        ).astype(jnp.bfloat16)
    return (fluid, shell)


def solution(mesh):
    return jax.shard_map(
        per_device,
        mesh=mesh,
        in_specs=(
            P("span", "chord", None, None),
            P("span", "chord", None, None),
            P("span", "chord", None, None, None),
            P("span", "chord", None),
            P("span", "chord", None),
            P(),
            P(("span", "chord"), None, None),
            P(("span", "chord"), None, None),
        ),
        out_specs=(P("span", "chord", None, None), P(("span", "chord"), None, None)),
        check_vma=False,
    )
```

profile of v0, /device:TPU:1, one launch (start us, length us, event | category | flops | bytes accessed | tf_op | source)
XLA Modules:
  0.0 407.1 jit_solution(17927677500699481471)
XLA Ops:
  7.2 1.5 copy-done
  8.7 1.7 convolution_convert_fusion.2
  10.5 0.5 copy.150
  11.1 0.7 copy.151
  11.9 0.2 copy.130
  12.1 0.4 convolution_convert_fusion.5
  12.5 0.7 copy.132
  13.3 53.3 %all-gather = s32[16,1,128]{2,1,0:T(1,128)S(1)} all-gather(s32[1,1,128]{2,1,0:T(1,128)S(1)} %reshape.757), channel_id=1, replica_groups=mesh['span'=32,'chord'=16] {'chord'}, dimensions={0}, use_global_device_ids=true | all-gather | bytes 8704 | tf_op jit(solution)/shard_map/all_gather | solution.py:67
  66.6 55.7 %all-gather.8.cloned.1.call-done = bf16[2048,5,128]{2,0,1:T(8,128)(2,1)} async-done(((bf16[128,5,128]{2,0,1:T(8,128)(2,1)}), bf16[2048,5,128]{2,0,1:T(8,128)(2,1)}) %all-gather.8.cloned.1.call-update) | async-done | bytes 2621456 | tf_op jit(solution)/shard_map/all_gather | solution.py:89
  122.3 2.4 fusion.22
  124.7 0.5 fusion.6
  125.2 0.6 fusion.7
  125.7 0.6 copy.154
  126.5 2.2 fusion.4
  128.7 0.8 fusion.48
  129.4 1.9 collective-permute-start
  131.3 3.2 collective-permute-start.1
  134.6 0.6 slice.554
  135.2 3.7 collective-permute-start.2
  138.9 0.6 slice.559
  139.5 1.3 collective-permute-start.3
  140.8 0.5 copy.117
  141.4 0.7 slice.555
  142.0 0.6 slice.558
  142.7 1.3 eq.14
  144.0 0.9 copy.119
  144.9 1.1 copy.193
  146.5 0.8 copy.122
  147.4 0.8 copy.127
  148.3 0.9 copy.118
  149.2 0.9 copy.121
  150.1 0.1 add_dynamic-update-slice_fusion.1
  150.3 0.1 fusion.33
  150.4 0.3 fusion.32
  150.8 0.3 fusion.31
  151.1 56.3 %all-gather.6.cloned.1.call-done = bf16[1024,6,128]{2,0,1:T(8,128)(2,1)} async-done(((bf16[64,6,128]{2,0,1:T(8,128)(2,1)}), bf16[1024,6,128]{2,0,1:T(8,128)(2,1)}) %all-gather.6.cloned.1.call-update) | async-done | bytes 1572880 | tf_op jit(solution)/shard_map/all_gather | solution.py:79
  207.4 1.8 fusion.18
  209.2 0.8 convolution_negate_fusion.1
  210.0 0.4 fusion.30
  210.4 0.2 convert_element_type.153
  210.7 0.7 convolution_convert_fusion.1
  211.3 0.5 copy.159
  211.9 0.7 copy.160
  212.7 2.2 fusion.3
  214.9 1.9 collective-permute-start.4
  216.8 4.2 %collective-permute-start.5 = (bf16[1,4,80,128]{3,2,1,0:T(8,128)(2,1)S(1)}, bf16[1,4,80,128]{3,2,1,0:T(8,128)(2,1)S(1)}, u32[]{:S(2)}, u32[]{:S(2)}) collective-permute-start(bf16[1,4,80,128]{3,2,1,0:T(8,128)(2,1)S(1)} %get-tuple-element.133), channel_id=1, source_target_pairs={{16,0},{32,16},{48,32},{64,48},{80,64},{96,80},{112,96},{128,112},... | collective-permute-start | bytes 245768 | tf_op jit(solution)/shard_map/ppermute | solution.py:13
  221.1 1.9 collective-permute-start.6
  223.0 1.6 collective-permute-start.7
  225.2 3.7 collective-permute-done.7
  229.1 0.1 add_dynamic-update-slice_fusion
  229.3 0.1 fusion.29
  229.4 0.3 fusion.28
  229.8 0.3 fusion.27
  230.1 62.3 %all-gather.10.cloned.1.call-done = bf16[1024,6,128]{2,0,1:T(8,128)(2,1)} async-done(((bf16[64,6,128]{2,0,1:T(8,128)(2,1)}), bf16[1024,6,128]{2,0,1:T(8,128)(2,1)}) %all-gather.10.cloned.1.call-update) | async-done | bytes 1572880 | tf_op jit(solution)/shard_map/all_gather | solution.py:79
  292.3 1.8 fusion.16
  294.2 0.8 convolution_negate_fusion
  295.0 0.4 fusion.26
  295.4 0.2 convert_element_type.165
  295.6 1.5 fusion.2
  297.1 99.4 %all-gather.12.cloned.1.call-done = bf16[2048,5,128]{2,0,1:T(8,128)(2,1)} async-done(((bf16[128,5,128]{2,0,1:T(8,128)(2,1)}), bf16[2048,5,128]{2,0,1:T(8,128)(2,1)}) %all-gather.12.cloned.1.call-update) | async-done | bytes 2621456 | tf_op jit(solution)/shard_map/all_gather | solution.py:89
  396.5 2.4 fusion.20
  398.9 0.5 fusion.5
  399.4 0.6 fusion.8
  399.9 0.7 copy.163
  (75 shorter events, 1.9 us)
Async XLA Ops:
  7.2 1.6 copy-start
  7.2 115.1 %all-gather.8.cloned.1.call-start = ((), (), s32[]{:S(2)}) async-start(), calls=%async_computation.1 | async-start | bytes 2785280 | tf_op jit(solution)/shard_map/all_gather | solution.py:89
  10.5 1.4 copy-start.9
  10.5 1.6 copy-start.3
  11.0 2.2 copy-start.10
  11.8 195.6 %all-gather.6.cloned.1.call-start = ((), (), s32[]{:S(2)}) async-start(), calls=%async_computation | async-start | bytes 1671168 | tf_op jit(solution)/shard_map/all_gather | solution.py:79
  13.1 279.2 %all-gather.10.cloned.1.call-start = ((), (), s32[]{:S(2)}) async-start(), calls=%async_computation.2 | async-start | bytes 1671168 | tf_op jit(solution)/shard_map/all_gather | solution.py:79
  66.6 55.7 %copy-start.13 = (s32[64]{0:T(128)}, s32[64]{0:T(128)S(1)}, u32[]{:S(2)}) copy-start(s32[64]{0:T(128)S(1)} %iota_add_fusion) | copy-start | bytes 772
  122.3 2.4 copy-start.8
  124.7 1.8 copy-start.12
  126.4 270.1 %all-gather.12.cloned.1.call-start = ((), (), s32[]{:S(2)}) async-start(), calls=%async_computation.3 | async-start | bytes 2785280 | tf_op jit(solution)/shard_map/all_gather | solution.py:89
  128.7 12.2 %copy-start.2 = (bf16[2,4,320,128]{3,2,1,0:T(8,128)(2,1)S(1)}, bf16[2,4,320,128]{3,2,1,0:T(8,128)(2,1)}, u32[]{:S(2)}) copy-start(bf16[2,4,320,128]{3,2,1,0:T(8,128)(2,1)} %param.28) | copy-start | bytes 1966084
  129.4 18.8 %collective-permute-start = (bf16[1,4,80,128]{3,2,1,0:T(8,128)(2,1)}, bf16[1,4,80,128]{3,2,1,0:T(8,128)(2,1)}, u32[]{:S(2)}, u32[]{:S(2)}) collective-permute-start(bf16[1,4,80,128]{3,2,1,0:T(8,128)(2,1)} %get-tuple-element.141), channel_id=1, source_target_pairs={{0,16},{16,32},{32,48},{48,64},{64,80},{80,96},{96,112},{112,128},... | collective-permute-start | bytes 245768 | tf_op jit(solution)/shard_map/ppermute | solution.py:13
  131.3 17.8 %collective-permute-start.1 = (bf16[1,4,80,128]{3,2,1,0:T(8,128)(2,1)}, bf16[1,4,80,128]{3,2,1,0:T(8,128)(2,1)}, u32[]{:S(2)}, u32[]{:S(2)}) collective-permute-start(bf16[1,4,80,128]{3,2,1,0:T(8,128)(2,1)} %get-tuple-element.139), channel_id=1, source_target_pairs={{16,0},{32,16},{48,32},{64,48},{80,64},{96,80},{112,96},{128,112},... | collective-permute-start | bytes 245768 | tf_op jit(solution)/shard_map/ppermute | solution.py:13
  135.2 11.3 %collective-permute-start.2 = (bf16[2,1,80,128]{3,2,1,0:T(8,128)(2,1)}, bf16[2,1,80,128]{3,2,1,0:T(8,128)(2,1)}, u32[]{:S(2)}, u32[]{:S(2)}) collective-permute-start(bf16[2,1,80,128]{3,2,1,0:T(8,128)(2,1)} %slice.554), channel_id=1, source_target_pairs={{0,1},{1,2},{2,3},{3,4},{4,5},{5,6},{6,7},{7,8},{8,9},{9,10},{10,1... | collective-permute-start | bytes 122888 | tf_op jit(solution)/shard_map/ppermute | solution.py:13
  139.5 7.8 %collective-permute-start.3 = (bf16[2,1,80,128]{3,2,1,0:T(8,128)(2,1)}, bf16[2,1,80,128]{3,2,1,0:T(8,128)(2,1)}, u32[]{:S(2)}, u32[]{:S(2)}) collective-permute-start(bf16[2,1,80,128]{3,2,1,0:T(8,128)(2,1)} %slice.559), channel_id=1, source_target_pairs={{1,0},{2,1},{3,2},{4,3},{5,4},{6,5},{7,6},{8,7},{9,8},{10,9},{11,1... | collective-permute-start | bytes 122888 | tf_op jit(solution)/shard_map/ppermute | solution.py:13
  144.9 1.1 copy-start.7
  144.9 1.1 copy-start.6
  144.9 1.3 copy-start.5
  214.9 14.1 %collective-permute-start.4 = (bf16[1,4,80,128]{3,2,1,0:T(8,128)(2,1)S(1)}, bf16[1,4,80,128]{3,2,1,0:T(8,128)(2,1)S(1)}, u32[]{:S(2)}, u32[]{:S(2)}) collective-permute-start(bf16[1,4,80,128]{3,2,1,0:T(8,128)(2,1)S(1)} %get-tuple-element.135), channel_id=1, source_target_pairs={{0,16},{16,32},{32,48},{48,64},{64,80},{80,96},{96,112},{112,128},... | collective-permute-start | bytes 245768 | tf_op jit(solution)/shard_map/ppermute | solution.py:13
  216.8 12.2 %collective-permute-start.5 = (bf16[1,4,80,128]{3,2,1,0:T(8,128)(2,1)S(1)}, bf16[1,4,80,128]{3,2,1,0:T(8,128)(2,1)S(1)}, u32[]{:S(2)}, u32[]{:S(2)}) collective-permute-start(bf16[1,4,80,128]{3,2,1,0:T(8,128)(2,1)S(1)} %get-tuple-element.133), channel_id=1, source_target_pairs={{16,0},{32,16},{48,32},{64,48},{80,64},{96,80},{112,96},{128,112},... | collective-permute-start | bytes 245768 | tf_op jit(solution)/shard_map/ppermute | solution.py:13
  221.1 4.0 collective-permute-start.6
  222.9 6.2 %copy-start.1 = (f32[2,4,4,4,4,5,128]{6,1,5,4,3,2,0:T(4,128)S(1)}, f32[2,4,4,4,4,5,128]{6,1,5,4,3,2,0:T(4,128)}, u32[]{:S(2)}) copy-start(f32[2,4,4,4,4,5,128]{6,1,5,4,3,2,0:T(4,128)} %copy.193) | copy-start | bytes 3932164
  223.0 5.9 %collective-permute-start.7 = (bf16[2,1,80,128]{3,2,1,0:T(8,128)(2,1)S(1)}, bf16[2,1,80,128]{3,2,1,0:T(8,128)(2,1)S(1)}, u32[]{:S(2)}, u32[]{:S(2)}) collective-permute-start(bf16[2,1,80,128]{3,2,1,0:T(8,128)(2,1)S(1)} %slice.573), channel_id=1, source_target_pairs={{1,0},{2,1},{3,2},{4,3},{5,4},{6,5},{7,6},{8,7},{9,8},{10,9},{11,1... | collective-permute-start | bytes 122888 | tf_op jit(solution)/shard_map/ppermute | solution.py:13
  229.3 63.1 %copy-start.11 = (s32[128]{0:T(128)S(1)}, s32[128]{0:T(128)}, u32[]{:S(2)}) copy-start(s32[128]{0:T(128)} %eq.14) | copy-start | bytes 1540
  295.6 100.9 %copy-start.14 = (s32[64]{0:T(128)S(1)}, s32[64]{0:T(128)}, u32[]{:S(2)}) copy-start(s32[64]{0:T(128)} %copy-done.13) | copy-start | bytes 772
  297.1 101.8 %copy-start.4 = (bf16[64,6,128]{2,0,1:T(8,128)(2,1)S(1)}, bf16[64,6,128]{2,0,1:T(8,128)(2,1)}, u32[]{:S(2)}) copy-start(bf16[64,6,128]{2,0,1:T(8,128)(2,1)} %param.34) | copy-start | bytes 294916
Sparse Core Ops, SparseCore 0:
  12.0 110.2 all-gather.7
  125.9 81.4 all-gather.5
  210.4 81.8 all-gather.9
  295.2 101.2 all-gather.11
where the time goes:
time: 408 us; the launch traced here: 407 us
  waiting for transfers between devices  277 us (68%)
  blocking collectives  53.3 us (13%)
  matrix products  20.6 us (5%)
  starting transfers between devices  19.8 us (5%)
  local copies, waits for them, and re-layouts  18.3 us (4%)
  between operations  14.5 us (4%)
    all_gather x2, waiting for transfers between devices, per_device(): piece = lax.all_gather(wall_rows, 'chord', axis=0, tiled=True)  155 us
    all_gather x2, waiting for transfers between devices, per_device(): pick_piece = lax.all_gather(shell, 'chord', axis=0, tiled=True)  119 us
    all_gather x1, blocking collectives, per_device(): strip_ids = lax.all_gather(wall_local, 'chord', axis=0, tiled=True)  53.3 us
    ppermute x8, starting transfers between devices, passed_along(): return lax.ppermute(block, axis, route)  19.6 us
  transfers between devices with their start and end apart: 12, of which 5 were waited for; matrix products, arithmetic and copies ran while one was open for 8% of the time, Pallas kernels for 0%

commit v1 on v0

--- a/solution.py
+++ b/solution.py
@@ -5,12 +5,22 @@
 
 NV = 5
 ITERS = 3
+CY = 4
 
 
 def passed_along(block, axis, distance):
     devices = range(lax.axis_size(axis))
     route = [(i - distance, i) for i in devices if i - distance in devices]
     return lax.ppermute(block, axis, route)
+
+
+def chord_shift(block, dz, dy):
+    size = lax.axis_size("chord")
+    cz = size // CY
+    route = [
+        (c, ((c // CY + dz) % cz) * CY + (c % CY + dy) % CY) for c in range(size)
+    ]
+    return lax.ppermute(block, "chord", route)
 
 
 def assemble(adj_rhs, low_span, high_span, low_chord, high_chord, wall_in):
@@ -56,15 +66,41 @@
     return (low_span, high_span, low_chord, high_chord)
 
 
+def gather_strip(shell):
+    cz = lax.axis_size("chord") // CY
+    first = jnp.stack([shell] + [chord_shift(shell, k, 0) for k in range(1, cz)])
+    return jnp.stack([first] + [chord_shift(first, 0, k) for k in range(1, CY)])
+
+
+def reduce_strip(partial):
+    cz = partial.shape[1]
+    part = partial[0]
+    for k in range(1, CY):
+        part = part + chord_shift(partial[k], 0, k)
+    total = part[0]
+    for k in range(1, cz):
+        total = total + chord_shift(part[k], k, 0)
+    return total
+
+
 def per_device(adj_rhs, diag_inv, face_jac, face_mask, wall_map, couple, shell_rhs, shell_inv):
     high = lax.Precision.HIGHEST
     rows, cols, blk, width = adj_rhs.shape
     shell_count = shell_rhs.shape[0]
+    size = lax.axis_size("chord")
+    cz = size // CY
     chord_pos = lax.axis_index("chord")
-    my_nodes = chord_pos * shell_count + lax.iota(jnp.int32, shell_count)
+    zpos = chord_pos // CY
+    ypos = chord_pos % CY
     wall_local = wall_map.reshape(-1)
     wall_count = wall_local.shape[0]
-    strip_ids = lax.all_gather(wall_local, "chord", axis=0, tiled=True)
+    node = lax.iota(jnp.int32, shell_count)
+    ky = lax.iota(jnp.int32, CY)[:, None, None]
+    kz = lax.iota(jnp.int32, cz)[None, :, None]
+    got_ids = ((((zpos - kz) % cz) * CY + (ypos - ky) % CY) * shell_count + node).reshape(-1)
+    out_ids = ((((zpos + kz) % cz) * CY + (ypos + ky) % CY) * shell_count + node).reshape(-1)
+    pick_hit = (wall_local[:, None] == got_ids[None, :]).astype(jnp.bfloat16)
+    load_hit = (out_ids[:, None] == wall_local[None, :]).astype(jnp.bfloat16)
     fluid = jnp.einsum(
         "abmn,abnr->abmr", diag_inv, adj_rhs, preferred_element_type=jnp.float32
     ).astype(jnp.bfloat16)
@@ -72,25 +108,22 @@
         "nst,ntr->nsr", shell_inv, shell_rhs.astype(jnp.float32), precision=high
     ).astype(jnp.bfloat16)
     weights = face_mask.astype(jnp.float32)[:, :, :, None, None]
+    sdof = shell.shape[1]
     for step in range(1, ITERS):
         sent = jnp.einsum("abdmn,abnr->abdmr", face_jac, fluid, preferred_element_type=jnp.float32)
         sent = (sent * weights).astype(jnp.bfloat16)
         low_span, high_span, low_chord, high_chord = face_terms(sent)
-        pick_piece = lax.all_gather(shell, "chord", axis=0, tiled=True)
-        pick_count = pick_piece.shape[0]
-        pick_hit = (wall_local[:, None] == lax.iota(jnp.int32, pick_count)[None, :]).astype(
-            jnp.float32
+        strip = gather_strip(shell).reshape(size * shell_count, sdof * width)
+        picked = jnp.dot(pick_hit, strip, preferred_element_type=jnp.float32)
+        wall_in = jnp.einsum(
+            "sv,wsr->wvr", couple, picked.reshape(wall_count, sdof, width), precision=high
         )
-        picked = jnp.einsum("wn,nsr->wsr", pick_hit, pick_piece.astype(jnp.float32), precision=high)
-        wall_in = jnp.einsum("sv,wsr->wvr", couple, picked, precision=high)
         wall_rows = fluid.reshape(rows, cols, 4, 4, 4, NV, width)[:, :, :, :, 0].reshape(
-            wall_count, NV, width
+            wall_count, NV * width
         )
-        piece = lax.all_gather(wall_rows, "chord", axis=0, tiled=True)
-        hit = (my_nodes[:, None] == strip_ids[None, :]).astype(jnp.float32)
-        summed = jnp.einsum("nw,wvr->nvr", hit, piece.astype(jnp.float32), precision=high)
+        partial = jnp.dot(load_hit, wall_rows, preferred_element_type=jnp.float32)
+        summed = reduce_strip(partial.reshape(CY, cz, shell_count, NV, width))
         shell_load = jnp.einsum("sv,nvr->nsr", couple, summed, precision=high)
-        wall_in, shell_load = (wall_in, shell_load)
         resid = assemble(adj_rhs, low_span, high_span, low_chord, high_chord, wall_in)
         fluid = jnp.einsum(
             "abmn,abnr->abmr", diag_inv, resid, preferred_element_type=jnp.float32

time: 408 us -> 359 us (0.88)
  the two profiles are of different devices: /device:TPU:1 before, /device:TPU:126 now
where the time goes in v1:
time: 359 us; the launch traced here: 357 us
  starting transfers between devices  138 us (38%)
  waiting for transfers between devices  127 us (35%)
  local copies, waits for them, and re-layouts  61.9 us (17%)
  matrix products  16 us (4%)
  other arithmetic  12.8 us (4%)
    ppermute x24, waiting for transfers between devices, chord_shift(): return lax.ppermute(block, 'chord', route)  120 us
    ppermute x24, starting transfers between devices, chord_shift(): return lax.ppermute(block, 'chord', route)  115 us
    ppermute x8, starting transfers between devices, passed_along(): return lax.ppermute(block, axis, route)  22.9 us
    squeeze x12, local copies, waits for them, and re-layouts, reduce_strip(): part = part + chord_shift(partial[k], 0, k)  19.6 us
  transfers between devices with their start and end apart: 32, of which 8 were waited for; matrix products, arithmetic and copies ran while one was open for 22% of the time, Pallas kernels for 0%

profile of v1, /device:TPU:126, one launch (start us, length us, event | category | flops | bytes accessed | tf_op | source)
XLA Modules:
  0.0 356.9 jit_solution(12080233605711414978)
XLA Ops:
  1.7 1.9 convolution_convert_fusion.5
  3.6 10.0 %collective-permute-start.6 = (bf16[64,6,128]{2,1,0:T(8,128)(2,1)}, bf16[64,6,128]{2,1,0:T(8,128)(2,1)}, u32[]{:S(2)}, u32[]{:S(2)}) collective-permute-start(bf16[64,6,128]{2,1,0:T(8,128)(2,1)} %convolution_convert_fusion.5), channel_id=1, source_target_pairs={{0,12},{1,13},{2,14},{3,15},{4,0},{5,1},{6,2},{7,3},{8,4},{9,5},{1... | collective-permute-start | bytes 294920 | tf_op jit(solution)/shard_map/ppermute | solution.py:23
  13.6 6.3 %collective-permute-start.5 = (bf16[64,6,128]{2,1,0:T(8,128)(2,1)}, bf16[64,6,128]{2,1,0:T(8,128)(2,1)}, u32[]{:S(2)}, u32[]{:S(2)}) collective-permute-start(bf16[64,6,128]{2,1,0:T(8,128)(2,1)} %convolution_convert_fusion.5), channel_id=1, source_target_pairs={{0,8},{1,9},{2,10},{3,11},{4,12},{5,13},{6,14},{7,15},{8,0},{9,1},... | collective-permute-start | bytes 294920 | tf_op jit(solution)/shard_map/ppermute | solution.py:23
  20.7 1.9 convolution_convert_fusion.2
  24.0 6.1 %collective-permute-start.2 = (bf16[2,1,80,128]{3,2,1,0:T(8,128)(2,1)}, bf16[2,1,80,128]{3,2,1,0:T(8,128)(2,1)}, u32[]{:S(2)}, u32[]{:S(2)}) collective-permute-start(bf16[2,1,80,128]{3,2,1,0:T(8,128)(2,1)} %slice.626), channel_id=1, source_target_pairs={{0,1},{1,2},{2,3},{3,4},{4,5},{5,6},{6,7},{7,8},{8,9},{9,10},{10,1... | collective-permute-start | bytes 122888 | tf_op jit(solution)/shard_map/ppermute | solution.py:14
  30.6 1.9 collective-permute-start.3
  33.3 1.9 collective-permute-start
  36.8 1.5 fusion.66
  41.7 1.6 copy.85
  46.8 1.6 copy.84
  49.4 2.2 squeeze.69
  51.6 2.2 copy.117
  53.8 2.2 squeeze.71
  56.0 2.2 copy.121
  58.2 2.2 squeeze.70
  60.4 2.2 copy.119
  62.6 2.2 squeeze.68
  64.8 4.4 %collective-permute-start.4 = (bf16[64,6,128]{2,1,0:T(8,128)(2,1)}, bf16[64,6,128]{2,1,0:T(8,128)(2,1)S(1)}, u32[]{:S(2)}, u32[]{:S(2)}) collective-permute-start(bf16[64,6,128]{2,1,0:T(8,128)(2,1)} %convolution_convert_fusion.5), channel_id=1, source_target_pairs={{0,4},{1,5},{2,6},{3,7},{4,8},{5,9},{6,10},{7,11},{8,12},{9,13},{1... | collective-permute-start | bytes 294920 | tf_op jit(solution)/shard_map/ppermute | solution.py:23
  70.1 3.4 collective-permute-start.1
  74.4 8.1 %collective-permute-start.14 = (f32[4,64,5,128]{3,1,2,0:T(8,128)}, f32[4,64,5,128]{3,1,2,0:T(8,128)}, u32[]{:S(2)}, u32[]{:S(2)}) collective-permute-start(f32[4,64,5,128]{3,1,2,0:T(8,128)} %copy.117), channel_id=1, source_target_pairs={{0,1},{1,2},{2,3},{3,0},{4,5},{5,6},{6,7},{7,4},{8,9},{9,10},{10,1... | collective-permute-start | bytes 1966088 | tf_op jit(solution)/shard_map/ppermute | solution.py:23
  84.5 1.9 collective-permute-start.16
  86.7 1.2 fusion.64
  87.9 3.4 collective-permute-start.8
  91.3 3.7 %collective-permute-start.7 = (bf16[4,64,6,128]{3,2,1,0:T(8,128)(2,1)S(1)}, bf16[4,64,6,128]{3,2,1,0:T(8,128)(2,1)S(1)}, u32[]{:S(2)}, u32[]{:S(2)}) collective-permute-start(bf16[4,64,6,128]{3,2,1,0:T(8,128)(2,1)S(1)} %get-tuple-element.157), channel_id=1, source_target_pairs={{0,1},{1,2},{2,3},{3,0},{4,5},{5,6},{6,7},{7,4},{8,9},{9,10},{10,1... | collective-permute-start | bytes 1179656 | tf_op jit(solution)/shard_map/ppermute | solution.py:23
  95.0 2.8 collective-permute-start.9
  98.4 16.6 %collective-permute-done.8 = bf16[4,64,6,128]{3,2,1,0:T(8,128)(2,1)S(1)} collective-permute-done((bf16[4,64,6,128]{3,2,1,0:T(8,128)(2,1)S(1)}, bf16[4,64,6,128]{3,2,1,0:T(8,128)(2,1)S(1)}, u32[]{:S(2)}, u32[]{:S(2)}) %collective-permute-start.8) | collective-permute-done | bytes 393248 | tf_op jit(solution)/shard_map/ppermute | solution.py:23
  115.0 4.1 %collective-permute-start.15 = (f32[4,64,5,128]{3,1,2,0:T(8,128)}, f32[4,64,5,128]{3,1,2,0:T(8,128)}, u32[]{:S(2)}, u32[]{:S(2)}) collective-permute-start(f32[4,64,5,128]{3,1,2,0:T(8,128)} %copy.119), channel_id=1, source_target_pairs={{0,2},{1,3},{2,0},{3,1},{4,6},{5,7},{6,4},{7,5},{8,10},{9,11},{10,... | collective-permute-start | bytes 1966088 | tf_op jit(solution)/shard_map/ppermute | solution.py:23
  119.1 13.3 %collective-permute-done.7 = bf16[4,64,6,128]{3,2,1,0:T(8,128)(2,1)S(1)} collective-permute-done((bf16[4,64,6,128]{3,2,1,0:T(8,128)(2,1)S(1)}, bf16[4,64,6,128]{3,2,1,0:T(8,128)(2,1)S(1)}, u32[]{:S(2)}, u32[]{:S(2)}) %collective-permute-start.7) | collective-permute-done | bytes 393248 | tf_op jit(solution)/shard_map/ppermute | solution.py:23
  132.4 7.3 %collective-permute-done.9 = bf16[4,64,6,128]{3,2,1,0:T(8,128)(2,1)S(1)} collective-permute-done((bf16[4,64,6,128]{3,2,1,0:T(8,128)(2,1)S(1)}, bf16[4,64,6,128]{3,2,1,0:T(8,128)(2,1)S(1)}, u32[]{:S(2)}, u32[]{:S(2)}) %collective-permute-start.9) | collective-permute-done | bytes 393248 | tf_op jit(solution)/shard_map/ppermute | solution.py:23
  140.3 1.5 copy.188
  141.8 2.6 copy.97
  144.4 2.1 fusion.20
  150.2 3.3 collective-permute-start.12
  153.5 2.6 collective-permute-start.13
  158.0 1.9 collective-permute-start.11
  159.9 6.3 %collective-permute-done.13 = bf16[2,1,80,128]{3,2,1,0:T(8,128)(2,1)} collective-permute-done((bf16[2,1,80,128]{3,2,1,0:T(8,128)(2,1)S(1)}, bf16[2,1,80,128]{3,2,1,0:T(8,128)(2,1)}, u32[]{:S(2)}, u32[]{:S(2)}) %collective-permute-start.13) | collective-permute-done | bytes 40992 | tf_op jit(solution)/shard_map/ppermute | solution.py:14
  166.2 1.9 collective-permute-start.10
  168.1 1.5 fusion.65
  177.0 1.2 squeeze.78
  179.1 2.3 squeeze.76
  183.3 1.9 collective-permute-start.26
  186.2 3.9 %collective-permute-start.28 = (f32[4,64,5,128]{3,1,2,0:T(8,128)}, f32[4,64,5,128]{3,1,2,0:T(8,128)S(1)}, u32[]{:S(2)}, u32[]{:S(2)}) collective-permute-start(f32[4,64,5,128]{3,1,2,0:T(8,128)} %copy.135), channel_id=1, source_target_pairs={{0,3},{1,0},{2,1},{3,2},{4,7},{5,4},{6,5},{7,6},{8,11},{9,8},{10,9... | collective-permute-start | bytes 1966088 | tf_op jit(solution)/shard_map/ppermute | solution.py:23
  192.1 1.9 collective-permute-start.27
  194.1 2.7 copy_add_fusion.3
  196.8 4.2 %collective-permute-start.17 = (f32[64,5,128]{2,1,0:T(8,128)S(1)}, f32[64,5,128]{2,1,0:T(8,128)S(1)}, u32[]{:S(2)}, u32[]{:S(2)}) collective-permute-start(f32[64,5,128]{2,1,0:T(8,128)S(1)} %get-tuple-element.139), channel_id=1, source_target_pairs={{0,4},{1,5},{2,6},{3,7},{4,8},{5,9},{6,10},{7,11},{8,12},{9,13},{1... | collective-permute-start | bytes 491528 | tf_op jit(solution)/shard_map/ppermute | solution.py:23
  201.2 5.8 %collective-permute-start.19 = (f32[64,5,128]{2,1,0:T(8,128)S(1)}, f32[64,5,128]{2,1,0:T(8,128)S(1)}, u32[]{:S(2)}, u32[]{:S(2)}) collective-permute-start(f32[64,5,128]{2,1,0:T(8,128)S(1)} %get-tuple-element.140), channel_id=1, source_target_pairs={{0,12},{1,13},{2,14},{3,15},{4,0},{5,1},{6,2},{7,3},{8,4},{9,5},{1... | collective-permute-start | bytes 491528 | tf_op jit(solution)/shard_map/ppermute | solution.py:23
  207.0 15.4 %collective-permute-done.17 = f32[64,5,128]{2,1,0:T(8,128)S(1)} collective-permute-done((f32[64,5,128]{2,1,0:T(8,128)S(1)}, f32[64,5,128]{2,1,0:T(8,128)S(1)}, u32[]{:S(2)}, u32[]{:S(2)}) %collective-permute-start.17) | collective-permute-done | bytes 163872 | tf_op jit(solution)/shard_map/ppermute | solution.py:23
  222.5 8.8 %collective-permute-start.18 = (f32[64,5,128]{2,1,0:T(8,128)S(1)}, f32[64,5,128]{2,1,0:T(8,128)S(1)}, u32[]{:S(2)}, u32[]{:S(2)}) collective-permute-start(f32[64,5,128]{2,1,0:T(8,128)S(1)} %get-tuple-element.141), channel_id=1, source_target_pairs={{0,8},{1,9},{2,10},{3,11},{4,12},{5,13},{6,14},{7,15},{8,0},{9,1},... | collective-permute-start | bytes 491528 | tf_op jit(solution)/shard_map/ppermute | solution.py:23
  231.6 22.3 %collective-permute-done.18 = f32[64,5,128]{2,1,0:T(8,128)S(1)} collective-permute-done((f32[64,5,128]{2,1,0:T(8,128)S(1)}, f32[64,5,128]{2,1,0:T(8,128)S(1)}, u32[]{:S(2)}, u32[]{:S(2)}) %collective-permute-start.18) | collective-permute-done | bytes 163872 | tf_op jit(solution)/shard_map/ppermute | solution.py:23
  254.8 6.9 %collective-permute-start.21 = (bf16[64,6,128]{2,1,0:T(8,128)(2,1)S(1)}, bf16[64,6,128]{2,1,0:T(8,128)(2,1)S(1)}, u32[]{:S(2)}, u32[]{:S(2)}) collective-permute-start(bf16[64,6,128]{2,1,0:T(8,128)(2,1)S(1)} %bitcast.196), channel_id=1, source_target_pairs={{0,8},{1,9},{2,10},{3,11},{4,12},{5,13},{6,14},{7,15},{8,0},{9,1},... | collective-permute-start | bytes 294920 | tf_op jit(solution)/shard_map/ppermute | solution.py:23
  261.8 1.9 collective-permute-start.20
  263.7 8.1 %collective-permute-start.22 = (bf16[64,6,128]{2,1,0:T(8,128)(2,1)S(1)}, bf16[64,6,128]{2,1,0:T(8,128)(2,1)S(1)}, u32[]{:S(2)}, u32[]{:S(2)}) collective-permute-start(bf16[64,6,128]{2,1,0:T(8,128)(2,1)S(1)} %bitcast.198), channel_id=1, source_target_pairs={{0,12},{1,13},{2,14},{3,15},{4,0},{5,1},{6,2},{7,3},{8,4},{9,5},{1... | collective-permute-start | bytes 294920 | tf_op jit(solution)/shard_map/ppermute | solution.py:23
  273.0 2.3 collective-permute-start.29
  275.3 7.5 %collective-permute-start.31 = (f32[64,5,128]{2,1,0:T(8,128)S(1)}, f32[64,5,128]{2,1,0:T(8,128)S(1)}, u32[]{:S(2)}, u32[]{:S(2)}) collective-permute-start(f32[64,5,128]{2,1,0:T(8,128)S(1)} %get-tuple-element.137), channel_id=1, source_target_pairs={{0,12},{1,13},{2,14},{3,15},{4,0},{5,1},{6,2},{7,3},{8,4},{9,5},{1... | collective-permute-start | bytes 491528 | tf_op jit(solution)/shard_map/ppermute | solution.py:23
  282.8 7.6 %collective-permute-start.30 = (f32[64,5,128]{2,1,0:T(8,128)S(1)}, f32[64,5,128]{2,1,0:T(8,128)S(1)}, u32[]{:S(2)}, u32[]{:S(2)}) collective-permute-start(f32[64,5,128]{2,1,0:T(8,128)S(1)} %get-tuple-element.138), channel_id=1, source_target_pairs={{0,8},{1,9},{2,10},{3,11},{4,12},{5,13},{6,14},{7,15},{8,0},{9,1},... | collective-permute-start | bytes 491528 | tf_op jit(solution)/shard_map/ppermute | solution.py:23
  291.0 1.9 collective-permute-start.24
  292.9 5.6 %collective-permute-start.23 = (bf16[4,64,6,128]{3,2,1,0:T(8,128)(2,1)S(1)}, bf16[4,64,6,128]{3,2,1,0:T(8,128)(2,1)S(1)}, u32[]{:S(2)}, u32[]{:S(2)}) collective-permute-start(bf16[4,64,6,128]{3,2,1,0:T(8,128)(2,1)S(1)} %get-tuple-element.155), channel_id=1, source_target_pairs={{0,1},{1,2},{2,3},{3,0},{4,5},{5,6},{6,7},{7,4},{8,9},{9,10},{10,1... | collective-permute-start | bytes 1179656 | tf_op jit(solution)/shard_map/ppermute | solution.py:23
  298.5 31.9 %collective-permute-done.29 = f32[64,5,128]{2,1,0:T(8,128)S(1)} collective-permute-done((f32[64,5,128]{2,1,0:T(8,128)S(1)}, f32[64,5,128]{2,1,0:T(8,128)S(1)}, u32[]{:S(2)}, u32[]{:S(2)}) %collective-permute-start.29) | collective-permute-done | bytes 163872 | tf_op jit(solution)/shard_map/ppermute | solution.py:23
  330.4 1.9 collective-permute-start.25
  334.0 13.3 %collective-permute-done.25 = bf16[4,64,6,128]{3,2,1,0:T(8,128)(2,1)S(1)} collective-permute-done((bf16[4,64,6,128]{3,2,1,0:T(8,128)(2,1)S(1)}, bf16[4,64,6,128]{3,2,1,0:T(8,128)(2,1)S(1)}, u32[]{:S(2)}, u32[]{:S(2)}) %collective-permute-start.25) | collective-permute-done | bytes 393248 | tf_op jit(solution)/shard_map/ppermute | solution.py:23
  347.8 1.5 copy.187
  349.3 2.6 copy.124
  351.9 2.1 fusion.18
  355.4 1.5 fusion.2
  (156 shorter events, 44.3 us)
Async XLA Ops:
  0.6 20.1 %copy-start = (bf16[2,4,320,320]{3,2,1,0:T(8,128)(2,1)S(1)}, bf16[2,4,320,320]{3,2,1,0:T(8,128)(2,1)}, u32[]{:S(2)}) copy-start(bf16[2,4,320,320]{3,2,1,0:T(8,128)(2,1)} %param.29) | copy-start | bytes 4915204
  3.6 83.1 %collective-permute-start.6 = (bf16[64,6,128]{2,1,0:T(8,128)(2,1)}, bf16[64,6,128]{2,1,0:T(8,128)(2,1)}, u32[]{:S(2)}, u32[]{:S(2)}) collective-permute-start(bf16[64,6,128]{2,1,0:T(8,128)(2,1)} %convolution_convert_fusion.5), channel_id=1, source_target_pairs={{0,12},{1,13},{2,14},{3,15},{4,0},{5,1},{6,2},{7,3},{8,4},{9,5},{1... | collective-permute-start | bytes 294920 | tf_op jit(solution)/shard_map/ppermute | solution.py:23
  13.6 73.0 %collective-permute-start.5 = (bf16[64,6,128]{2,1,0:T(8,128)(2,1)}, bf16[64,6,128]{2,1,0:T(8,128)(2,1)}, u32[]{:S(2)}, u32[]{:S(2)}) collective-permute-start(bf16[64,6,128]{2,1,0:T(8,128)(2,1)} %convolution_convert_fusion.5), channel_id=1, source_target_pairs={{0,8},{1,9},{2,10},{3,11},{4,12},{5,13},{6,14},{7,15},{8,0},{9,1},... | collective-permute-start | bytes 294920 | tf_op jit(solution)/shard_map/ppermute | solution.py:23
  20.7 1.9 copy-start.2
  23.2 12.5 %copy-start.21 = (s32[2,4,16]{2,1,0:T(4,128)S(1)}, s32[2,4,16]{2,1,0:T(4,128)}, u32[]{:S(2)}) copy-start(s32[2,4,16]{2,1,0:T(4,128)} %param.32) | copy-start | bytes 1540
  23.3 10.0 %copy-start.9 = (bf16[2,4,80,128]{3,2,1,0:T(8,128)(2,1)}, bf16[2,4,80,128]{3,2,1,0:T(8,128)(2,1)S(1)}, u32[]{:S(2)}) copy-start(bf16[2,4,80,128]{3,2,1,0:T(8,128)(2,1)S(1)} %get-tuple-element.149) | copy-start | bytes 491524
  23.3 10.0 %copy-start.11 = (bf16[2,4,80,128]{3,2,1,0:T(8,128)(2,1)}, bf16[2,4,80,128]{3,2,1,0:T(8,128)(2,1)S(1)}, u32[]{:S(2)}) copy-start(bf16[2,4,80,128]{3,2,1,0:T(8,128)(2,1)S(1)} %get-tuple-element.148) | copy-start | bytes 491524
  24.0 40.8 %collective-permute-start.2 = (bf16[2,1,80,128]{3,2,1,0:T(8,128)(2,1)}, bf16[2,1,80,128]{3,2,1,0:T(8,128)(2,1)}, u32[]{:S(2)}, u32[]{:S(2)}) collective-permute-start(bf16[2,1,80,128]{3,2,1,0:T(8,128)(2,1)} %slice.626), channel_id=1, source_target_pairs={{0,1},{1,2},{2,3},{3,4},{4,5},{5,6},{6,7},{7,8},{8,9},{9,10},{10,1... | collective-permute-start | bytes 122888 | tf_op jit(solution)/shard_map/ppermute | solution.py:14
  30.6 39.5 %collective-permute-start.3 = (bf16[2,1,80,128]{3,2,1,0:T(8,128)(2,1)}, bf16[2,1,80,128]{3,2,1,0:T(8,128)(2,1)}, u32[]{:S(2)}, u32[]{:S(2)}) collective-permute-start(bf16[2,1,80,128]{3,2,1,0:T(8,128)(2,1)} %slice.631), channel_id=1, source_target_pairs={{1,0},{2,1},{3,2},{4,3},{5,4},{6,5},{7,6},{8,7},{9,8},{10,9},{11,1... | collective-permute-start | bytes 122888 | tf_op jit(solution)/shard_map/ppermute | solution.py:14
  33.3 41.1 %collective-permute-start = (bf16[1,4,80,128]{3,2,1,0:T(8,128)(2,1)}, bf16[1,4,80,128]{3,2,1,0:T(8,128)(2,1)}, u32[]{:S(2)}, u32[]{:S(2)}) collective-permute-start(bf16[1,4,80,128]{3,2,1,0:T(8,128)(2,1)} %get-tuple-element.153), channel_id=1, source_target_pairs={{0,16},{16,32},{32,48},{48,64},{64,80},{80,96},{96,112},{112,128},... | collective-permute-start | bytes 245768 | tf_op jit(solution)/shard_map/ppermute | solution.py:14
  35.8 1.0 copy-start.19
  36.8 2.3 copy-start.12
  36.8 3.0 copy-start.10
  36.8 3.6 %copy-start.6 = (bf16[2,4,320,128]{3,2,1,0:T(8,128)(2,1)S(1)}, bf16[2,4,320,128]{3,2,1,0:T(8,128)(2,1)}, u32[]{:S(2)}) copy-start(bf16[2,4,320,128]{3,2,1,0:T(8,128)(2,1)} %param.28) | copy-start | bytes 1966084
  64.8 21.7 %copy-start.17 = (bf16[1,4,1,80,128]{4,1,3,2,0:T(4,128)(2,1)S(1)}, bf16[1,4,1,80,128]{4,1,3,2,0:T(4,128)(2,1)}, u32[]{:S(2)}) copy-start(bf16[1,4,1,80,128]{4,1,3,2,0:T(4,128)(2,1)} %copy.85) | copy-start | bytes 245764
  64.8 21.9 %collective-permute-start.4 = (bf16[64,6,128]{2,1,0:T(8,128)(2,1)}, bf16[64,6,128]{2,1,0:T(8,128)(2,1)S(1)}, u32[]{:S(2)}, u32[]{:S(2)}) collective-permute-start(bf16[64,6,128]{2,1,0:T(8,128)(2,1)} %convolution_convert_fusion.5), channel_id=1, source_target_pairs={{0,4},{1,5},{2,6},{3,7},{4,8},{5,9},{6,10},{7,11},{8,12},{9,13},{1... | collective-permute-start | bytes 294920 | tf_op jit(solution)/shard_map/ppermute | solution.py:23
  70.1 14.4 %collective-permute-start.1 = (bf16[1,4,80,128]{3,2,1,0:T(8,128)(2,1)}, bf16[1,4,80,128]{3,2,1,0:T(8,128)(2,1)S(1)}, u32[]{:S(2)}, u32[]{:S(2)}) collective-permute-start(bf16[1,4,80,128]{3,2,1,0:T(8,128)(2,1)} %get-tuple-element.151), channel_id=1, source_target_pairs={{16,0},{32,16},{48,32},{64,48},{80,64},{96,80},{112,96},{128,112},... | collective-permute-start | bytes 245768 | tf_op jit(solution)/shard_map/ppermute | solution.py:14
  74.4 117.7 %collective-permute-start.14 = (f32[4,64,5,128]{3,1,2,0:T(8,128)}, f32[4,64,5,128]{3,1,2,0:T(8,128)}, u32[]{:S(2)}, u32[]{:S(2)}) collective-permute-start(f32[4,64,5,128]{3,1,2,0:T(8,128)} %copy.117), channel_id=1, source_target_pairs={{0,1},{1,2},{2,3},{3,0},{4,5},{5,6},{6,7},{7,4},{8,9},{9,10},{10,1... | collective-permute-start | bytes 1966088 | tf_op jit(solution)/shard_map/ppermute | solution.py:23
  83.4 14.3 %copy-start.14 = (bf16[2,3,4,1,4,5,128]{6,1,5,4,3,2,0:T(4,128)(2,1)S(1)}, bf16[2,3,4,1,4,5,128]{6,1,5,4,3,2,0:T(4,128)(2,1)}, u32[]{:S(2)}) copy-start(bf16[2,3,4,1,4,5,128]{6,1,5,4,3,2,0:T(4,128)(2,1)} %copy.90) | copy-start | bytes 368644
  84.5 109.5 %collective-permute-start.16 = (f32[4,64,5,128]{3,1,2,0:T(8,128)}, f32[4,64,5,128]{3,1,2,0:T(8,128)}, u32[]{:S(2)}, u32[]{:S(2)}) collective-permute-start(f32[4,64,5,128]{3,1,2,0:T(8,128)} %copy.121), channel_id=1, source_target_pairs={{0,3},{1,0},{2,1},{3,2},{4,7},{5,4},{6,5},{7,6},{8,11},{9,8},{10,9... | collective-permute-start | bytes 1966088 | tf_op jit(solution)/shard_map/ppermute | solution.py:23
  86.5 11.6 %copy-start.13 = (bf16[2,3,4,1,4,5,128]{6,1,5,4,3,2,0:T(4,128)(2,1)S(1)}, bf16[2,3,4,1,4,5,128]{6,1,5,4,3,2,0:T(4,128)(2,1)}, u32[]{:S(2)}) copy-start(bf16[2,3,4,1,4,5,128]{6,1,5,4,3,2,0:T(4,128)(2,1)} %copy.93) | copy-start | bytes 368644
  87.9 27.1 %collective-permute-start.8 = (bf16[4,64,6,128]{3,2,1,0:T(8,128)(2,1)S(1)}, bf16[4,64,6,128]{3,2,1,0:T(8,128)(2,1)S(1)}, u32[]{:S(2)}, u32[]{:S(2)}) collective-permute-start(bf16[4,64,6,128]{3,2,1,0:T(8,128)(2,1)S(1)} %get-tuple-element.157), channel_id=1, source_target_pairs={{0,2},{1,3},{2,0},{3,1},{4,6},{5,7},{6,4},{7,5},{8,10},{9,11},{10,... | collective-permute-start | bytes 1179656 | tf_op jit(solution)/shard_map/ppermute | solution.py:23
  91.3 41.1 %collective-permute-start.7 = (bf16[4,64,6,128]{3,2,1,0:T(8,128)(2,1)S(1)}, bf16[4,64,6,128]{3,2,1,0:T(8,128)(2,1)S(1)}, u32[]{:S(2)}, u32[]{:S(2)}) collective-permute-start(bf16[4,64,6,128]{3,2,1,0:T(8,128)(2,1)S(1)} %get-tuple-element.157), channel_id=1, source_target_pairs={{0,1},{1,2},{2,3},{3,0},{4,5},{5,6},{6,7},{7,4},{8,9},{9,10},{10,1... | collective-permute-start | bytes 1179656 | tf_op jit(solution)/shard_map/ppermute | solution.py:23
  95.0 44.8 %collective-permute-start.9 = (bf16[4,64,6,128]{3,2,1,0:T(8,128)(2,1)S(1)}, bf16[4,64,6,128]{3,2,1,0:T(8,128)(2,1)S(1)}, u32[]{:S(2)}, u32[]{:S(2)}) collective-permute-start(bf16[4,64,6,128]{3,2,1,0:T(8,128)(2,1)S(1)} %get-tuple-element.157), channel_id=1, source_target_pairs={{0,3},{1,0},{2,1},{3,2},{4,7},{5,4},{6,5},{7,6},{8,11},{9,8},{10,9... | collective-permute-start | bytes 1179656 | tf_op jit(solution)/shard_map/ppermute | solution.py:23
  115.0 79.1 %collective-permute-start.15 = (f32[4,64,5,128]{3,1,2,0:T(8,128)}, f32[4,64,5,128]{3,1,2,0:T(8,128)}, u32[]{:S(2)}, u32[]{:S(2)}) collective-permute-start(f32[4,64,5,128]{3,1,2,0:T(8,128)} %copy.119), channel_id=1, source_target_pairs={{0,2},{1,3},{2,0},{3,1},{4,6},{5,7},{6,4},{7,5},{8,10},{9,11},{10,... | collective-permute-start | bytes 1966088 | tf_op jit(solution)/shard_map/ppermute | solution.py:23
  144.4 2.1 copy-start.18
  147.9 1.5 copy-start.3
  150.1 6.6 %copy-start.20 = (s32[128]{0:T(128)S(1)}, s32[128]{0:T(128)}, u32[]{:S(2)}) copy-start(s32[128]{0:T(128)} %copy-done.19) | copy-start | bytes 1540
  150.2 7.8 %collective-permute-start.12 = (bf16[2,1,80,128]{3,2,1,0:T(8,128)(2,1)S(1)}, bf16[2,1,80,128]{3,2,1,0:T(8,128)(2,1)}, u32[]{:S(2)}, u32[]{:S(2)}) collective-permute-start(bf16[2,1,80,128]{3,2,1,0:T(8,128)(2,1)S(1)} %slice.640), channel_id=1, source_target_pairs={{0,1},{1,2},{2,3},{3,4},{4,5},{5,6},{6,7},{7,8},{8,9},{9,10},{10,1... | collective-permute-start | bytes 122888 | tf_op jit(solution)/shard_map/ppermute | solution.py:14
  153.5 12.7 %collective-permute-start.13 = (bf16[2,1,80,128]{3,2,1,0:T(8,128)(2,1)S(1)}, bf16[2,1,80,128]{3,2,1,0:T(8,128)(2,1)}, u32[]{:S(2)}, u32[]{:S(2)}) collective-permute-start(bf16[2,1,80,128]{3,2,1,0:T(8,128)(2,1)S(1)} %slice.645), channel_id=1, source_target_pairs={{1,0},{2,1},{3,2},{4,3},{5,4},{6,5},{7,6},{8,7},{9,8},{10,9},{11,1... | collective-permute-start | bytes 122888 | tf_op jit(solution)/shard_map/ppermute | solution.py:14
  158.0 25.4 %collective-permute-start.11 = (bf16[1,4,80,128]{3,2,1,0:T(8,128)(2,1)}, bf16[1,4,80,128]{3,2,1,0:T(8,128)(2,1)}, u32[]{:S(2)}, u32[]{:S(2)}) collective-permute-start(bf16[1,4,80,128]{3,2,1,0:T(8,128)(2,1)} %get-tuple-element.145), channel_id=1, source_target_pairs={{16,0},{32,16},{48,32},{64,48},{80,64},{96,80},{112,96},{128,112},... | collective-permute-start | bytes 245768 | tf_op jit(solution)/shard_map/ppermute | solution.py:14
  166.2 20.0 %collective-permute-start.10 = (bf16[1,4,80,128]{3,2,1,0:T(8,128)(2,1)}, bf16[1,4,80,128]{3,2,1,0:T(8,128)(2,1)}, u32[]{:S(2)}, u32[]{:S(2)}) collective-permute-start(bf16[1,4,80,128]{3,2,1,0:T(8,128)(2,1)} %get-tuple-element.147), channel_id=1, source_target_pairs={{0,16},{16,32},{32,48},{48,64},{64,80},{80,96},{96,112},{112,128},... | collective-permute-start | bytes 245768 | tf_op jit(solution)/shard_map/ppermute | solution.py:14
  179.1 11.9 %copy-start.1 = (f32[2,4,4,4,4,5,128]{6,1,5,4,3,2,0:T(4,128)S(1)}, f32[2,4,4,4,4,5,128]{6,1,5,4,3,2,0:T(4,128)}, u32[]{:S(2)}) copy-start(f32[2,4,4,4,4,5,128]{6,1,5,4,3,2,0:T(4,128)} %copy.194) | copy-start | bytes 3932164
  181.5 12.6 %copy-start.4 = (f32[4,64,5,128]{3,2,1,0:T(8,128)S(1)}, f32[4,64,5,128]{3,2,1,0:T(8,128)}, u32[]{:S(2)}) copy-start(f32[4,64,5,128]{3,2,1,0:T(8,128)} %squeeze.68) | copy-start | bytes 1966084
  183.3 80.4 %collective-permute-start.26 = (f32[4,64,5,128]{3,1,2,0:T(8,128)}, f32[4,64,5,128]{3,1,2,0:T(8,128)S(1)}, u32[]{:S(2)}, u32[]{:S(2)}) collective-permute-start(f32[4,64,5,128]{3,1,2,0:T(8,128)} %copy.131), channel_id=1, source_target_pairs={{0,1},{1,2},{2,3},{3,0},{4,5},{5,6},{6,7},{7,4},{8,9},{9,10},{10,1... | collective-permute-start | bytes 1966088 | tf_op jit(solution)/shard_map/ppermute | solution.py:23
  186.2 85.6 %collective-permute-start.28 = (f32[4,64,5,128]{3,1,2,0:T(8,128)}, f32[4,64,5,128]{3,1,2,0:T(8,128)S(1)}, u32[]{:S(2)}, u32[]{:S(2)}) collective-permute-start(f32[4,64,5,128]{3,1,2,0:T(8,128)} %copy.135), channel_id=1, source_target_pairs={{0,3},{1,0},{2,1},{3,2},{4,7},{5,4},{6,5},{7,6},{8,11},{9,8},{10,9... | collective-permute-start | bytes 1966088 | tf_op jit(solution)/shard_map/ppermute | solution.py:23
  192.1 79.7 %collective-permute-start.27 = (f32[4,64,5,128]{3,1,2,0:T(8,128)}, f32[4,64,5,128]{3,1,2,0:T(8,128)S(1)}, u32[]{:S(2)}, u32[]{:S(2)}) collective-permute-start(f32[4,64,5,128]{3,1,2,0:T(8,128)} %copy.133), channel_id=1, source_target_pairs={{0,2},{1,3},{2,0},{3,1},{4,6},{5,7},{6,4},{7,5},{8,10},{9,11},{10,... | collective-permute-start | bytes 1966088 | tf_op jit(solution)/shard_map/ppermute | solution.py:23
  196.7 4.3 %copy-start.16 = (bf16[1,4,1,80,128]{4,1,3,2,0:T(4,128)(2,1)S(1)}, bf16[1,4,1,80,128]{4,1,3,2,0:T(4,128)(2,1)}, u32[]{:S(2)}) copy-start(bf16[1,4,1,80,128]{4,1,3,2,0:T(4,128)(2,1)} %copy.104) | copy-start | bytes 245764
  196.7 34.5 %copy-start.15 = (bf16[2,3,4,1,4,5,128]{6,1,5,4,3,2,0:T(4,128)(2,1)S(1)}, bf16[2,3,4,1,4,5,128]{6,1,5,4,3,2,0:T(4,128)(2,1)}, u32[]{:S(2)}) copy-start(bf16[2,3,4,1,4,5,128]{6,1,5,4,3,2,0:T(4,128)(2,1)} %copy.109) | copy-start | bytes 368644
  196.7 57.1 %copy-start.7 = (bf16[64,6,128]{2,0,1:T(8,128)(2,1)S(1)}, bf16[64,6,128]{2,0,1:T(8,128)(2,1)}, u32[]{:S(2)}) copy-start(bf16[64,6,128]{2,0,1:T(8,128)(2,1)} %param.34) | copy-start | bytes 294916
  196.8 25.6 %collective-permute-start.17 = (f32[64,5,128]{2,1,0:T(8,128)S(1)}, f32[64,5,128]{2,1,0:T(8,128)S(1)}, u32[]{:S(2)}, u32[]{:S(2)}) collective-permute-start(f32[64,5,128]{2,1,0:T(8,128)S(1)} %get-tuple-element.139), channel_id=1, source_target_pairs={{0,4},{1,5},{2,6},{3,7},{4,8},{5,9},{6,10},{7,11},{8,12},{9,13},{1... | collective-permute-start | bytes 491528 | tf_op jit(solution)/shard_map/ppermute | solution.py:23
  201.2 70.6 %copy-start.5 = (f32[4,64,5,128]{3,2,1,0:T(8,128)S(1)}, f32[4,64,5,128]{3,2,1,0:T(8,128)}, u32[]{:S(2)}) copy-start(f32[4,64,5,128]{3,2,1,0:T(8,128)} %squeeze.76) | copy-start | bytes 1966084
  201.2 30.4 %collective-permute-start.19 = (f32[64,5,128]{2,1,0:T(8,128)S(1)}, f32[64,5,128]{2,1,0:T(8,128)S(1)}, u32[]{:S(2)}, u32[]{:S(2)}) collective-permute-start(f32[64,5,128]{2,1,0:T(8,128)S(1)} %get-tuple-element.140), channel_id=1, source_target_pairs={{0,12},{1,13},{2,14},{3,15},{4,0},{5,1},{6,2},{7,3},{8,4},{9,5},{1... | collective-permute-start | bytes 491528 | tf_op jit(solution)/shard_map/ppermute | solution.py:23
  222.5 31.4 %collective-permute-start.18 = (f32[64,5,128]{2,1,0:T(8,128)S(1)}, f32[64,5,128]{2,1,0:T(8,128)S(1)}, u32[]{:S(2)}, u32[]{:S(2)}) collective-permute-start(f32[64,5,128]{2,1,0:T(8,128)S(1)} %get-tuple-element.141), channel_id=1, source_target_pairs={{0,8},{1,9},{2,10},{3,11},{4,12},{5,13},{6,14},{7,15},{8,0},{9,1},... | collective-permute-start | bytes 491528 | tf_op jit(solution)/shard_map/ppermute | solution.py:23
  254.8 28.0 %collective-permute-start.21 = (bf16[64,6,128]{2,1,0:T(8,128)(2,1)S(1)}, bf16[64,6,128]{2,1,0:T(8,128)(2,1)S(1)}, u32[]{:S(2)}, u32[]{:S(2)}) collective-permute-start(bf16[64,6,128]{2,1,0:T(8,128)(2,1)S(1)} %bitcast.196), channel_id=1, source_target_pairs={{0,8},{1,9},{2,10},{3,11},{4,12},{5,13},{6,14},{7,15},{8,0},{9,1},... | collective-permute-start | bytes 294920 | tf_op jit(solution)/shard_map/ppermute | solution.py:23
  261.8 29.0 %collective-permute-start.20 = (bf16[64,6,128]{2,1,0:T(8,128)(2,1)S(1)}, bf16[64,6,128]{2,1,0:T(8,128)(2,1)S(1)}, u32[]{:S(2)}, u32[]{:S(2)}) collective-permute-start(bf16[64,6,128]{2,1,0:T(8,128)(2,1)S(1)} %bitcast.197), channel_id=1, source_target_pairs={{0,4},{1,5},{2,6},{3,7},{4,8},{5,9},{6,10},{7,11},{8,12},{9,13},{1... | collective-permute-start | bytes 294920 | tf_op jit(solution)/shard_map/ppermute | solution.py:23
  263.7 27.1 %collective-permute-start.22 = (bf16[64,6,128]{2,1,0:T(8,128)(2,1)S(1)}, bf16[64,6,128]{2,1,0:T(8,128)(2,1)S(1)}, u32[]{:S(2)}, u32[]{:S(2)}) collective-permute-start(bf16[64,6,128]{2,1,0:T(8,128)(2,1)S(1)} %bitcast.198), channel_id=1, source_target_pairs={{0,12},{1,13},{2,14},{3,15},{4,0},{5,1},{6,2},{7,3},{8,4},{9,5},{1... | collective-permute-start | bytes 294920 | tf_op jit(solution)/shard_map/ppermute | solution.py:23
  273.0 17.5 %copy-start.8 = (bf16[2,3,4,1,4,5,128]{6,1,5,4,3,2,0:T(4,128)(2,1)S(1)}, bf16[2,3,4,1,4,5,128]{6,1,5,4,3,2,0:T(4,128)(2,1)}, u32[]{:S(2)}) copy-start(bf16[2,3,4,1,4,5,128]{6,1,5,4,3,2,0:T(4,128)(2,1)} %copy.112) | copy-start | bytes 368644
  273.0 57.4 %collective-permute-start.29 = (f32[64,5,128]{2,1,0:T(8,128)S(1)}, f32[64,5,128]{2,1,0:T(8,128)S(1)}, u32[]{:S(2)}, u32[]{:S(2)}) collective-permute-start(f32[64,5,128]{2,1,0:T(8,128)S(1)} %get-tuple-element.136), channel_id=1, source_target_pairs={{0,4},{1,5},{2,6},{3,7},{4,8},{5,9},{6,10},{7,11},{8,12},{9,13},{1... | collective-permute-start | bytes 491528 | tf_op jit(solution)/shard_map/ppermute | solution.py:23
  275.3 57.0 %collective-permute-start.31 = (f32[64,5,128]{2,1,0:T(8,128)S(1)}, f32[64,5,128]{2,1,0:T(8,128)S(1)}, u32[]{:S(2)}, u32[]{:S(2)}) collective-permute-start(f32[64,5,128]{2,1,0:T(8,128)S(1)} %get-tuple-element.137), channel_id=1, source_target_pairs={{0,12},{1,13},{2,14},{3,15},{4,0},{5,1},{6,2},{7,3},{8,4},{9,5},{1... | collective-permute-start | bytes 491528 | tf_op jit(solution)/shard_map/ppermute | solution.py:23
  282.8 49.5 %collective-permute-start.30 = (f32[64,5,128]{2,1,0:T(8,128)S(1)}, f32[64,5,128]{2,1,0:T(8,128)S(1)}, u32[]{:S(2)}, u32[]{:S(2)}) collective-permute-start(f32[64,5,128]{2,1,0:T(8,128)S(1)} %get-tuple-element.138), channel_id=1, source_target_pairs={{0,8},{1,9},{2,10},{3,11},{4,12},{5,13},{6,14},{7,15},{8,0},{9,1},... | collective-permute-start | bytes 491528 | tf_op jit(solution)/shard_map/ppermute | solution.py:23
  291.0 43.0 %collective-permute-start.24 = (bf16[4,64,6,128]{3,2,1,0:T(8,128)(2,1)S(1)}, bf16[4,64,6,128]{3,2,1,0:T(8,128)(2,1)S(1)}, u32[]{:S(2)}, u32[]{:S(2)}) collective-permute-start(bf16[4,64,6,128]{3,2,1,0:T(8,128)(2,1)S(1)} %get-tuple-element.155), channel_id=1, source_target_pairs={{0,2},{1,3},{2,0},{3,1},{4,6},{5,7},{6,4},{7,5},{8,10},{9,11},{10,... | collective-permute-start | bytes 1179656 | tf_op jit(solution)/shard_map/ppermute | solution.py:23
  292.9 41.1 %collective-permute-start.23 = (bf16[4,64,6,128]{3,2,1,0:T(8,128)(2,1)S(1)}, bf16[4,64,6,128]{3,2,1,0:T(8,128)(2,1)S(1)}, u32[]{:S(2)}, u32[]{:S(2)}) collective-permute-start(bf16[4,64,6,128]{3,2,1,0:T(8,128)(2,1)S(1)} %get-tuple-element.155), channel_id=1, source_target_pairs={{0,1},{1,2},{2,3},{3,0},{4,5},{5,6},{6,7},{7,4},{8,9},{9,10},{10,1... | collective-permute-start | bytes 1179656 | tf_op jit(solution)/shard_map/ppermute | solution.py:23
  330.4 16.9 %collective-permute-start.25 = (bf16[4,64,6,128]{3,2,1,0:T(8,128)(2,1)S(1)}, bf16[4,64,6,128]{3,2,1,0:T(8,128)(2,1)S(1)}, u32[]{:S(2)}, u32[]{:S(2)}) collective-permute-start(bf16[4,64,6,128]{3,2,1,0:T(8,128)(2,1)S(1)} %get-tuple-element.155), channel_id=1, source_target_pairs={{0,3},{1,0},{2,1},{3,2},{4,7},{5,4},{6,5},{7,6},{8,11},{9,8},{10,9... | collective-permute-start | bytes 1179656 | tf_op jit(solution)/shard_map/ppermute | solution.py:23

commit v2 on v1

--- a/solution.py
+++ b/solution.py
@@ -113,7 +113,8 @@
         sent = jnp.einsum("abdmn,abnr->abdmr", face_jac, fluid, preferred_element_type=jnp.float32)
         sent = (sent * weights).astype(jnp.bfloat16)
         low_span, high_span, low_chord, high_chord = face_terms(sent)
-        strip = gather_strip(shell).reshape(size * shell_count, sdof * width)
+        strip = gather_strip(shell.reshape(shell_count, sdof * width))
+        strip = strip.reshape(size * shell_count, sdof * width)
         picked = jnp.dot(pick_hit, strip, preferred_element_type=jnp.float32)
         wall_in = jnp.einsum(
             "sv,wsr->wvr", couple, picked.reshape(wall_count, sdof, width), precision=high
@@ -122,8 +123,10 @@
             wall_count, NV * width
         )
         partial = jnp.dot(load_hit, wall_rows, preferred_element_type=jnp.float32)
-        summed = reduce_strip(partial.reshape(CY, cz, shell_count, NV, width))
-        shell_load = jnp.einsum("sv,nvr->nsr", couple, summed, precision=high)
+        summed = reduce_strip(partial.reshape(CY, cz, shell_count, NV * width))
+        shell_load = jnp.einsum(
+            "sv,nvr->nsr", couple, summed.reshape(shell_count, NV, width), precision=high
+        )
         resid = assemble(adj_rhs, low_span, high_span, low_chord, high_chord, wall_in)
         fluid = jnp.einsum(
             "abmn,abnr->abmr", diag_inv, resid, preferred_element_type=jnp.float32

time: 359 us -> 319 us (0.89)
  the two profiles are of different devices: /device:TPU:126 before, /device:TPU:45 now
where the time goes in v2:
time: 319 us; the launch traced here: 317 us
  starting transfers between devices  176 us (55%)
  waiting for transfers between devices  68.5 us (21%)
  local copies, waits for them, and re-layouts  36.6 us (11%)
  other arithmetic  17.4 us (5%)
  matrix products  17.2 us (5%)
    ppermute x24, starting transfers between devices, chord_shift(): return lax.ppermute(block, 'chord', route)  138 us
    ppermute x24, waiting for transfers between devices, chord_shift(): return lax.ppermute(block, 'chord', route)  68.4 us
    ppermute x8, starting transfers between devices, passed_along(): return lax.ppermute(block, axis, route)  37.8 us
  transfers between devices with their start and end apart: 32, of which 9 were waited for; matrix products, arithmetic and copies ran while one was open for 15% of the time, Pallas kernels for 0%

profile of v2, /device:TPU:45, one launch (start us, length us, event | category | flops | bytes accessed | tf_op | source)
XLA Modules:
  0.0 317.2 jit_solution(13922745401918396050)
XLA Ops:
  1.7 1.3 convolution_convert_fusion.5
  3.6 11.5 %collective-permute-start.6 = (bf16[64,768]{1,0:T(8,128)(2,1)}, bf16[64,768]{1,0:T(8,128)(2,1)}, u32[]{:S(2)}, u32[]{:S(2)}) collective-permute-start(bf16[64,768]{1,0:T(8,128)(2,1)} %bitcast.175), channel_id=1, source_target_pairs={{0,12},{1,13},{2,14},{3,15},{4,0},{5,1},{6,2},{7,3},{8,4},{9,5},{1... | collective-permute-start | bytes 294920 | tf_op jit(solution)/shard_map/ppermute | solution.py:23
  15.2 4.9 %collective-permute-start.5 = (bf16[64,768]{1,0:T(8,128)(2,1)}, bf16[64,768]{1,0:T(8,128)(2,1)}, u32[]{:S(2)}, u32[]{:S(2)}) collective-permute-start(bf16[64,768]{1,0:T(8,128)(2,1)} %bitcast.175), channel_id=1, source_target_pairs={{0,8},{1,9},{2,10},{3,11},{4,12},{5,13},{6,14},{7,15},{8,0},{9,1},... | collective-permute-start | bytes 294920 | tf_op jit(solution)/shard_map/ppermute | solution.py:23
  20.8 1.9 convolution_convert_fusion.2
  24.1 3.2 %collective-permute-start.2 = (bf16[2,1,80,128]{3,2,1,0:T(8,128)(2,1)}, bf16[2,1,80,128]{3,2,1,0:T(8,128)(2,1)}, u32[]{:S(2)}, u32[]{:S(2)}) collective-permute-start(bf16[2,1,80,128]{3,2,1,0:T(8,128)(2,1)} %slice.626), channel_id=1, source_target_pairs={{0,1},{1,2},{2,3},{3,4},{4,5},{5,6},{6,7},{7,8},{8,9},{9,10},{10,1... | collective-permute-start | bytes 122888 | tf_op jit(solution)/shard_map/ppermute | solution.py:14
  27.9 2.7 collective-permute-start.3
  31.4 4.6 %collective-permute-start = (bf16[1,4,80,128]{3,2,1,0:T(8,128)(2,1)}, bf16[1,4,80,128]{3,2,1,0:T(8,128)(2,1)}, u32[]{:S(2)}, u32[]{:S(2)}) collective-permute-start(bf16[1,4,80,128]{3,2,1,0:T(8,128)(2,1)} %get-tuple-element.151), channel_id=1, source_target_pairs={{0,16},{16,32},{32,48},{48,64},{64,80},{80,96},{96,112},{112,128},... | collective-permute-start | bytes 245768 | tf_op jit(solution)/shard_map/ppermute | solution.py:14
  37.8 1.5 fusion.66
  42.1 1.6 copy.38
  48.6 1.1 copy.131
  49.6 6.5 %collective-permute-start.4 = (bf16[64,768]{1,0:T(8,128)(2,1)}, bf16[64,768]{1,0:T(8,128)(2,1)S(1)}, u32[]{:S(2)}, u32[]{:S(2)}) collective-permute-start(bf16[64,768]{1,0:T(8,128)(2,1)} %bitcast.175), channel_id=1, source_target_pairs={{0,4},{1,5},{2,6},{3,7},{4,8},{5,9},{6,10},{7,11},{8,12},{9,13},{1... | collective-permute-start | bytes 294920 | tf_op jit(solution)/shard_map/ppermute | solution.py:23
  57.1 1.9 collective-permute-start.1
  59.9 8.1 %collective-permute-start.16 = (f32[4,64,640]{2,1,0:T(8,128)}, f32[4,64,640]{2,1,0:T(8,128)}, u32[]{:S(2)}, u32[]{:S(2)}) collective-permute-start(f32[4,64,640]{2,1,0:T(8,128)} %bitcast.50), channel_id=1, source_target_pairs={{0,3},{1,0},{2,1},{3,2},{4,7},{5,4},{6,5},{7,6},{8,11},{9,8},{10,9... | collective-permute-start | bytes 1966088 | tf_op jit(solution)/shard_map/ppermute | solution.py:23
  69.1 1.9 collective-permute-start.14
  72.3 3.7 %collective-permute-start.8 = (bf16[4,64,768]{2,1,0:T(8,128)(2,1)S(1)}, bf16[4,64,768]{2,1,0:T(8,128)(2,1)S(1)}, u32[]{:S(2)}, u32[]{:S(2)}) collective-permute-start(bf16[4,64,768]{2,1,0:T(8,128)(2,1)S(1)} %get-tuple-element.155), channel_id=1, source_target_pairs={{0,2},{1,3},{2,0},{3,1},{4,6},{5,7},{6,4},{7,5},{8,10},{9,11},{10,... | collective-permute-start | bytes 1179656 | tf_op jit(solution)/shard_map/ppermute | solution.py:23
  76.0 2.8 collective-permute-start.7
  78.8 2.5 collective-permute-start.9
  81.9 7.7 %collective-permute-done.8 = bf16[4,64,768]{2,1,0:T(8,128)(2,1)S(1)} collective-permute-done((bf16[4,64,768]{2,1,0:T(8,128)(2,1)S(1)}, bf16[4,64,768]{2,1,0:T(8,128)(2,1)S(1)}, u32[]{:S(2)}, u32[]{:S(2)}) %collective-permute-start.8) | collective-permute-done | bytes 393248 | tf_op jit(solution)/shard_map/ppermute | solution.py:23
  89.7 5.6 %collective-permute-start.15 = (f32[4,64,640]{2,1,0:T(8,128)}, f32[4,64,640]{2,1,0:T(8,128)}, u32[]{:S(2)}, u32[]{:S(2)}) collective-permute-start(f32[4,64,640]{2,1,0:T(8,128)} %bitcast.49), channel_id=1, source_target_pairs={{0,2},{1,3},{2,0},{3,1},{4,6},{5,7},{6,4},{7,5},{8,10},{9,11},{10,... | collective-permute-start | bytes 1966088 | tf_op jit(solution)/shard_map/ppermute | solution.py:23
  95.3 7.8 %collective-permute-done.7 = bf16[4,64,768]{2,1,0:T(8,128)(2,1)S(1)} collective-permute-done((bf16[4,64,768]{2,1,0:T(8,128)(2,1)S(1)}, bf16[4,64,768]{2,1,0:T(8,128)(2,1)S(1)}, u32[]{:S(2)}, u32[]{:S(2)}) %collective-permute-start.7) | collective-permute-done | bytes 393248 | tf_op jit(solution)/shard_map/ppermute | solution.py:23
  103.1 1.4 pad_maximum_fusion
  104.6 2.6 copy.53
  107.2 2.1 fusion.18
  113.0 2.0 collective-permute-start.12
  115.0 16.7 %collective-permute-start.13 = (bf16[2,1,80,128]{3,2,1,0:T(8,128)(2,1)S(1)}, bf16[2,1,80,128]{3,2,1,0:T(8,128)(2,1)S(1)}, u32[]{:S(2)}, u32[]{:S(2)}) collective-permute-start(bf16[2,1,80,128]{3,2,1,0:T(8,128)(2,1)S(1)} %slice.645), channel_id=1, source_target_pairs={{1,0},{2,1},{3,2},{4,3},{5,4},{6,5},{7,6},{8,7},{9,8},{10,9},{11,1... | collective-permute-start | bytes 122888 | tf_op jit(solution)/shard_map/ppermute | solution.py:14
  133.0 4.2 %collective-permute-start.11 = (bf16[1,4,80,128]{3,2,1,0:T(8,128)(2,1)S(1)}, bf16[1,4,80,128]{3,2,1,0:T(8,128)(2,1)S(1)}, u32[]{:S(2)}, u32[]{:S(2)}) collective-permute-start(bf16[1,4,80,128]{3,2,1,0:T(8,128)(2,1)S(1)} %get-tuple-element.143), channel_id=1, source_target_pairs={{16,0},{32,16},{48,32},{64,48},{80,64},{96,80},{112,96},{128,112},... | collective-permute-start | bytes 245768 | tf_op jit(solution)/shard_map/ppermute | solution.py:14
  137.2 2.5 collective-permute-start.10
  139.7 1.6 fusion.65
  144.6 2.2 collective-permute-start.28
  146.9 5.2 %collective-permute-start.26 = (f32[4,64,640]{2,1,0:T(8,128)}, f32[4,64,640]{2,1,0:T(8,128)}, u32[]{:S(2)}, u32[]{:S(2)}) collective-permute-start(f32[4,64,640]{2,1,0:T(8,128)} %bitcast.76), channel_id=1, source_target_pairs={{0,1},{1,2},{2,3},{3,0},{4,5},{5,6},{6,7},{7,4},{8,9},{9,10},{10,1... | collective-permute-start | bytes 1966088 | tf_op jit(solution)/shard_map/ppermute | solution.py:23
  152.1 12.1 %collective-permute-start.27 = (f32[4,64,640]{2,1,0:T(8,128)}, f32[4,64,640]{2,1,0:T(8,128)}, u32[]{:S(2)}, u32[]{:S(2)}) collective-permute-start(f32[4,64,640]{2,1,0:T(8,128)} %bitcast.77), channel_id=1, source_target_pairs={{0,2},{1,3},{2,0},{3,1},{4,6},{5,7},{6,4},{7,5},{8,10},{9,11},{10,... | collective-permute-start | bytes 1966088 | tf_op jit(solution)/shard_map/ppermute | solution.py:23
  164.3 1.7 add_add_fusion.1
  166.1 1.9 collective-permute-start.17
  168.2 7.3 %collective-permute-start.19 = (f32[64,640]{1,0:T(8,128)S(1)}, f32[64,640]{1,0:T(8,128)S(1)}, u32[]{:S(2)}, u32[]{:S(2)}) collective-permute-start(f32[64,640]{1,0:T(8,128)S(1)} %get-tuple-element.138), channel_id=1, source_target_pairs={{0,12},{1,13},{2,14},{3,15},{4,0},{5,1},{6,2},{7,3},{8,4},{9,5},{1... | collective-permute-start | bytes 491528 | tf_op jit(solution)/shard_map/ppermute | solution.py:23
  175.4 6.9 %collective-permute-done.17 = f32[64,640]{1,0:T(8,128)S(1)} collective-permute-done((f32[64,640]{1,0:T(8,128)S(1)}, f32[64,640]{1,0:T(8,128)S(1)}, u32[]{:S(2)}, u32[]{:S(2)}) %collective-permute-start.17) | collective-permute-done | bytes 163872 | tf_op jit(solution)/shard_map/ppermute | solution.py:23
  182.3 9.7 %collective-permute-start.18 = (f32[64,640]{1,0:T(8,128)S(1)}, f32[64,640]{1,0:T(8,128)S(1)}, u32[]{:S(2)}, u32[]{:S(2)}) collective-permute-start(f32[64,640]{1,0:T(8,128)S(1)} %get-tuple-element.139), channel_id=1, source_target_pairs={{0,8},{1,9},{2,10},{3,11},{4,12},{5,13},{6,14},{7,15},{8,0},{9,1},... | collective-permute-start | bytes 491528 | tf_op jit(solution)/shard_map/ppermute | solution.py:23
  192.2 11.5 %collective-permute-done.18 = f32[64,640]{1,0:T(8,128)S(1)} collective-permute-done((f32[64,640]{1,0:T(8,128)S(1)}, f32[64,640]{1,0:T(8,128)S(1)}, u32[]{:S(2)}, u32[]{:S(2)}) %collective-permute-start.18) | collective-permute-done | bytes 163872 | tf_op jit(solution)/shard_map/ppermute | solution.py:23
  204.5 1.6 reshape.979
  206.1 1.8 add_add_fusion
  208.0 1.9 collective-permute-start.29
  209.9 7.3 %collective-permute-start.31 = (f32[64,640]{1,0:T(8,128)S(1)}, f32[64,640]{1,0:T(8,128)S(1)}, u32[]{:S(2)}, u32[]{:S(2)}) collective-permute-start(f32[64,640]{1,0:T(8,128)S(1)} %get-tuple-element.135), channel_id=1, source_target_pairs={{0,12},{1,13},{2,14},{3,15},{4,0},{5,1},{6,2},{7,3},{8,4},{9,5},{1... | collective-permute-start | bytes 491528 | tf_op jit(solution)/shard_map/ppermute | solution.py:23
  217.2 12.8 %collective-permute-start.30 = (f32[64,640]{1,0:T(8,128)S(1)}, f32[64,640]{1,0:T(8,128)S(1)}, u32[]{:S(2)}, u32[]{:S(2)}) collective-permute-start(f32[64,640]{1,0:T(8,128)S(1)} %get-tuple-element.136), channel_id=1, source_target_pairs={{0,8},{1,9},{2,10},{3,11},{4,12},{5,13},{6,14},{7,15},{8,0},{9,1},... | collective-permute-start | bytes 491528 | tf_op jit(solution)/shard_map/ppermute | solution.py:23
  230.1 1.0 fusion.54
  231.1 11.5 %collective-permute-done.30 = f32[64,640]{1,0:T(8,128)S(1)} collective-permute-done((f32[64,640]{1,0:T(8,128)S(1)}, f32[64,640]{1,0:T(8,128)S(1)}, u32[]{:S(2)}, u32[]{:S(2)}) %collective-permute-start.30) | collective-permute-done | bytes 163872 | tf_op jit(solution)/shard_map/ppermute | solution.py:23
  243.3 1.6 reshape.983
  245.0 1.3 fusion.52
  246.3 1.8 convert_subtract_fusion
  249.4 6.9 %collective-permute-start.22 = (bf16[64,768]{1,0:T(8,128)(2,1)}, bf16[64,768]{1,0:T(8,128)(2,1)}, u32[]{:S(2)}, u32[]{:S(2)}) collective-permute-start(bf16[64,768]{1,0:T(8,128)(2,1)} %bitcast.174), channel_id=1, source_target_pairs={{0,12},{1,13},{2,14},{3,15},{4,0},{5,1},{6,2},{7,3},{8,4},{9,5},{1... | collective-permute-start | bytes 294920 | tf_op jit(solution)/shard_map/ppermute | solution.py:23
  256.3 11.1 %collective-permute-start.21 = (bf16[64,768]{1,0:T(8,128)(2,1)}, bf16[64,768]{1,0:T(8,128)(2,1)}, u32[]{:S(2)}, u32[]{:S(2)}) collective-permute-start(bf16[64,768]{1,0:T(8,128)(2,1)} %bitcast.174), channel_id=1, source_target_pairs={{0,8},{1,9},{2,10},{3,11},{4,12},{5,13},{6,14},{7,15},{8,0},{9,1},... | collective-permute-start | bytes 294920 | tf_op jit(solution)/shard_map/ppermute | solution.py:23
  267.4 4.9 %collective-permute-start.20 = (bf16[64,768]{1,0:T(8,128)(2,1)}, bf16[64,768]{1,0:T(8,128)(2,1)}, u32[]{:S(2)}, u32[]{:S(2)}) collective-permute-start(bf16[64,768]{1,0:T(8,128)(2,1)} %bitcast.174), channel_id=1, source_target_pairs={{0,4},{1,5},{2,6},{3,7},{4,8},{5,9},{6,10},{7,11},{8,12},{9,13},{1... | collective-permute-start | bytes 294920 | tf_op jit(solution)/shard_map/ppermute | solution.py:23
  272.6 1.7 stack_reshape.7
  274.3 10.0 %collective-permute-done.20 = bf16[64,768]{1,0:T(8,128)(2,1)} collective-permute-done((bf16[64,768]{1,0:T(8,128)(2,1)}, bf16[64,768]{1,0:T(8,128)(2,1)}, u32[]{:S(2)}, u32[]{:S(2)}) %collective-permute-start.20) | collective-permute-done | bytes 98336 | tf_op jit(solution)/shard_map/ppermute | solution.py:23
  284.3 1.1 fusion.63
  285.4 1.9 collective-permute-start.24
  287.3 2.1 collective-permute-start.23
  289.4 3.2 %collective-permute-start.25 = (bf16[4,64,768]{2,1,0:T(8,128)(2,1)S(1)}, bf16[4,64,768]{2,1,0:T(8,128)(2,1)S(1)}, u32[]{:S(2)}, u32[]{:S(2)}) collective-permute-start(bf16[4,64,768]{2,1,0:T(8,128)(2,1)S(1)} %get-tuple-element.153), channel_id=1, source_target_pairs={{0,3},{1,0},{2,1},{3,2},{4,7},{5,4},{6,5},{7,6},{8,11},{9,8},{10,9... | collective-permute-start | bytes 1179656 | tf_op jit(solution)/shard_map/ppermute | solution.py:23
  292.6 1.3 fusion.23
  295.3 3.3 %collective-permute-done.24 = bf16[4,64,768]{2,1,0:T(8,128)(2,1)S(1)} collective-permute-done((bf16[4,64,768]{2,1,0:T(8,128)(2,1)S(1)}, bf16[4,64,768]{2,1,0:T(8,128)(2,1)S(1)}, u32[]{:S(2)}, u32[]{:S(2)}) %collective-permute-start.24) | collective-permute-done | bytes 393248 | tf_op jit(solution)/shard_map/ppermute | solution.py:23
  298.6 3.6 %collective-permute-done.23 = bf16[4,64,768]{2,1,0:T(8,128)(2,1)S(1)} collective-permute-done((bf16[4,64,768]{2,1,0:T(8,128)(2,1)S(1)}, bf16[4,64,768]{2,1,0:T(8,128)(2,1)S(1)}, u32[]{:S(2)}, u32[]{:S(2)}) %collective-permute-start.23) | collective-permute-done | bytes 393248 | tf_op jit(solution)/shard_map/ppermute | solution.py:23
  302.2 6.1 %collective-permute-done.25 = bf16[4,64,768]{2,1,0:T(8,128)(2,1)S(1)} collective-permute-done((bf16[4,64,768]{2,1,0:T(8,128)(2,1)S(1)}, bf16[4,64,768]{2,1,0:T(8,128)(2,1)S(1)}, u32[]{:S(2)}, u32[]{:S(2)}) %collective-permute-start.25) | collective-permute-done | bytes 393248 | tf_op jit(solution)/shard_map/ppermute | solution.py:23
  308.3 1.4 pad_maximum_fusion.1
  309.6 2.6 copy.73
  312.2 2.1 fusion.16
  315.7 1.5 fusion.2
  (149 shorter events, 33.5 us)
Async XLA Ops:
  0.6 20.2 %copy-start = (bf16[2,4,320,320]{3,2,1,0:T(8,128)(2,1)S(1)}, bf16[2,4,320,320]{3,2,1,0:T(8,128)(2,1)}, u32[]{:S(2)}) copy-start(bf16[2,4,320,320]{3,2,1,0:T(8,128)(2,1)} %param.29) | copy-start | bytes 4915204
  3.0 17.2 %copy-start.6 = (bf16[64,6,128]{2,1,0:T(8,128)(2,1)}, bf16[64,6,128]{2,1,0:T(8,128)(2,1)S(1)}, u32[]{:S(2)}) copy-start(bf16[64,6,128]{2,1,0:T(8,128)(2,1)S(1)} %convolution_convert_fusion.5) | copy-start | bytes 294916
  3.6 67.6 %collective-permute-start.6 = (bf16[64,768]{1,0:T(8,128)(2,1)}, bf16[64,768]{1,0:T(8,128)(2,1)}, u32[]{:S(2)}, u32[]{:S(2)}) collective-permute-start(bf16[64,768]{1,0:T(8,128)(2,1)} %bitcast.175), channel_id=1, source_target_pairs={{0,12},{1,13},{2,14},{3,15},{4,0},{5,1},{6,2},{7,3},{8,4},{9,5},{1... | collective-permute-start | bytes 294920 | tf_op jit(solution)/shard_map/ppermute | solution.py:23
  15.2 56.0 %collective-permute-start.5 = (bf16[64,768]{1,0:T(8,128)(2,1)}, bf16[64,768]{1,0:T(8,128)(2,1)}, u32[]{:S(2)}, u32[]{:S(2)}) collective-permute-start(bf16[64,768]{1,0:T(8,128)(2,1)} %bitcast.175), channel_id=1, source_target_pairs={{0,8},{1,9},{2,10},{3,11},{4,12},{5,13},{6,14},{7,15},{8,0},{9,1},... | collective-permute-start | bytes 294920 | tf_op jit(solution)/shard_map/ppermute | solution.py:23
  20.8 1.9 copy-start.2
  23.4 13.1 %copy-start.21 = (s32[2,4,16]{2,1,0:T(4,128)S(1)}, s32[2,4,16]{2,1,0:T(4,128)}, u32[]{:S(2)}) copy-start(s32[2,4,16]{2,1,0:T(4,128)} %param.32) | copy-start | bytes 1540
  23.4 7.9 %copy-start.11 = (bf16[2,4,80,128]{3,2,1,0:T(8,128)(2,1)}, bf16[2,4,80,128]{3,2,1,0:T(8,128)(2,1)S(1)}, u32[]{:S(2)}) copy-start(bf16[2,4,80,128]{3,2,1,0:T(8,128)(2,1)S(1)} %get-tuple-element.147) | copy-start | bytes 491524
  23.4 7.9 %copy-start.13 = (bf16[2,4,80,128]{3,2,1,0:T(8,128)(2,1)}, bf16[2,4,80,128]{3,2,1,0:T(8,128)(2,1)S(1)}, u32[]{:S(2)}) copy-start(bf16[2,4,80,128]{3,2,1,0:T(8,128)(2,1)S(1)} %get-tuple-element.146) | copy-start | bytes 491524
  24.1 25.5 %collective-permute-start.2 = (bf16[2,1,80,128]{3,2,1,0:T(8,128)(2,1)}, bf16[2,1,80,128]{3,2,1,0:T(8,128)(2,1)}, u32[]{:S(2)}, u32[]{:S(2)}) collective-permute-start(bf16[2,1,80,128]{3,2,1,0:T(8,128)(2,1)} %slice.626), channel_id=1, source_target_pairs={{0,1},{1,2},{2,3},{3,4},{4,5},{5,6},{6,7},{7,8},{8,9},{9,10},{10,1... | collective-permute-start | bytes 122888 | tf_op jit(solution)/shard_map/ppermute | solution.py:14
  27.9 29.1 %collective-permute-start.3 = (bf16[2,1,80,128]{3,2,1,0:T(8,128)(2,1)}, bf16[2,1,80,128]{3,2,1,0:T(8,128)(2,1)}, u32[]{:S(2)}, u32[]{:S(2)}) collective-permute-start(bf16[2,1,80,128]{3,2,1,0:T(8,128)(2,1)} %slice.631), channel_id=1, source_target_pairs={{1,0},{2,1},{3,2},{4,3},{5,4},{6,5},{7,6},{8,7},{9,8},{10,9},{11,1... | collective-permute-start | bytes 122888 | tf_op jit(solution)/shard_map/ppermute | solution.py:14
  31.4 28.5 %collective-permute-start = (bf16[1,4,80,128]{3,2,1,0:T(8,128)(2,1)}, bf16[1,4,80,128]{3,2,1,0:T(8,128)(2,1)}, u32[]{:S(2)}, u32[]{:S(2)}) collective-permute-start(bf16[1,4,80,128]{3,2,1,0:T(8,128)(2,1)} %get-tuple-element.151), channel_id=1, source_target_pairs={{0,16},{16,32},{32,48},{48,64},{64,80},{80,96},{96,112},{112,128},... | collective-permute-start | bytes 245768 | tf_op jit(solution)/shard_map/ppermute | solution.py:14
  36.6 0.6 copy-start.19
  37.7 2.3 copy-start.7
  37.7 3.1 copy-start.14
  37.7 3.7 %copy-start.12 = (bf16[2,4,80,128]{3,2,1,0:T(8,128)(2,1)S(1)}, bf16[2,4,80,128]{3,2,1,0:T(8,128)(2,1)}, u32[]{:S(2)}) copy-start(bf16[2,4,80,128]{3,2,1,0:T(8,128)(2,1)} %copy-done.11) | copy-start | bytes 491524
  47.5 9.6 %copy-start.17 = (bf16[1,4,80,128]{3,2,1,0:T(8,128)(2,1)S(1)}, bf16[1,4,80,128]{3,2,1,0:T(8,128)(2,1)}, u32[]{:S(2)}) copy-start(bf16[1,4,80,128]{3,2,1,0:T(8,128)(2,1)} %get-tuple-element.149) | copy-start | bytes 245764
  49.6 21.6 %copy-start.15 = (bf16[1,64,768]{2,1,0:T(8,128)(2,1)S(1)}, bf16[1,64,768]{2,1,0:T(8,128)(2,1)}, u32[]{:S(2)}) copy-start(bf16[1,64,768]{2,1,0:T(8,128)(2,1)} %stack_reshape.6) | copy-start | bytes 294916
  49.6 21.6 %collective-permute-start.4 = (bf16[64,768]{1,0:T(8,128)(2,1)}, bf16[64,768]{1,0:T(8,128)(2,1)S(1)}, u32[]{:S(2)}, u32[]{:S(2)}) collective-permute-start(bf16[64,768]{1,0:T(8,128)(2,1)} %bitcast.175), channel_id=1, source_target_pairs={{0,4},{1,5},{2,6},{3,7},{4,8},{5,9},{6,10},{7,11},{8,12},{9,13},{1... | collective-permute-start | bytes 294920 | tf_op jit(solution)/shard_map/ppermute | solution.py:23
  57.1 12.0 %collective-permute-start.1 = (bf16[1,4,80,128]{3,2,1,0:T(8,128)(2,1)S(1)}, bf16[1,4,80,128]{3,2,1,0:T(8,128)(2,1)S(1)}, u32[]{:S(2)}, u32[]{:S(2)}) collective-permute-start(bf16[1,4,80,128]{3,2,1,0:T(8,128)(2,1)S(1)} %copy-done.17), channel_id=1, source_target_pairs={{16,0},{32,16},{48,32},{64,48},{80,64},{96,80},{112,96},{128,112},... | collective-permute-start | bytes 245768 | tf_op jit(solution)/shard_map/ppermute | solution.py:14
  59.9 92.2 %collective-permute-start.16 = (f32[4,64,640]{2,1,0:T(8,128)}, f32[4,64,640]{2,1,0:T(8,128)}, u32[]{:S(2)}, u32[]{:S(2)}) collective-permute-start(f32[4,64,640]{2,1,0:T(8,128)} %bitcast.50), channel_id=1, source_target_pairs={{0,3},{1,0},{2,1},{3,2},{4,7},{5,4},{6,5},{7,6},{8,11},{9,8},{10,9... | collective-permute-start | bytes 1966088 | tf_op jit(solution)/shard_map/ppermute | solution.py:23
  69.1 95.1 %collective-permute-start.14 = (f32[4,64,640]{2,1,0:T(8,128)}, f32[4,64,640]{2,1,0:T(8,128)}, u32[]{:S(2)}, u32[]{:S(2)}) collective-permute-start(f32[4,64,640]{2,1,0:T(8,128)} %bitcast.48), channel_id=1, source_target_pairs={{0,1},{1,2},{2,3},{3,0},{4,5},{5,6},{6,7},{7,4},{8,9},{9,10},{10,1... | collective-permute-start | bytes 1966088 | tf_op jit(solution)/shard_map/ppermute | solution.py:23
  72.3 17.4 %collective-permute-start.8 = (bf16[4,64,768]{2,1,0:T(8,128)(2,1)S(1)}, bf16[4,64,768]{2,1,0:T(8,128)(2,1)S(1)}, u32[]{:S(2)}, u32[]{:S(2)}) collective-permute-start(bf16[4,64,768]{2,1,0:T(8,128)(2,1)S(1)} %get-tuple-element.155), channel_id=1, source_target_pairs={{0,2},{1,3},{2,0},{3,1},{4,6},{5,7},{6,4},{7,5},{8,10},{9,11},{10,... | collective-permute-start | bytes 1179656 | tf_op jit(solution)/shard_map/ppermute | solution.py:23
  76.0 27.1 %collective-permute-start.7 = (bf16[4,64,768]{2,1,0:T(8,128)(2,1)S(1)}, bf16[4,64,768]{2,1,0:T(8,128)(2,1)S(1)}, u32[]{:S(2)}, u32[]{:S(2)}) collective-permute-start(bf16[4,64,768]{2,1,0:T(8,128)(2,1)S(1)} %get-tuple-element.155), channel_id=1, source_target_pairs={{0,1},{1,2},{2,3},{3,0},{4,5},{5,6},{6,7},{7,4},{8,9},{9,10},{10,1... | collective-permute-start | bytes 1179656 | tf_op jit(solution)/shard_map/ppermute | solution.py:23
  78.8 24.4 %collective-permute-start.9 = (bf16[4,64,768]{2,1,0:T(8,128)(2,1)S(1)}, bf16[4,64,768]{2,1,0:T(8,128)(2,1)S(1)}, u32[]{:S(2)}, u32[]{:S(2)}) collective-permute-start(bf16[4,64,768]{2,1,0:T(8,128)(2,1)S(1)} %get-tuple-element.155), channel_id=1, source_target_pairs={{0,3},{1,0},{2,1},{3,2},{4,7},{5,4},{6,5},{7,6},{8,11},{9,8},{10,9... | collective-permute-start | bytes 1179656 | tf_op jit(solution)/shard_map/ppermute | solution.py:23
  89.7 74.6 %collective-permute-start.15 = (f32[4,64,640]{2,1,0:T(8,128)}, f32[4,64,640]{2,1,0:T(8,128)}, u32[]{:S(2)}, u32[]{:S(2)}) collective-permute-start(f32[4,64,640]{2,1,0:T(8,128)} %bitcast.49), channel_id=1, source_target_pairs={{0,2},{1,3},{2,0},{3,1},{4,6},{5,7},{6,4},{7,5},{8,10},{9,11},{10,... | collective-permute-start | bytes 1966088 | tf_op jit(solution)/shard_map/ppermute | solution.py:23
  107.2 2.1 copy-start.18
  110.7 1.5 copy-start.3
  112.9 19.5 %copy-start.20 = (s32[128]{0:T(128)S(1)}, s32[128]{0:T(128)}, u32[]{:S(2)}) copy-start(s32[128]{0:T(128)} %copy-done.19) | copy-start | bytes 1540
  113.0 20.0 %collective-permute-start.12 = (bf16[2,1,80,128]{3,2,1,0:T(8,128)(2,1)S(1)}, bf16[2,1,80,128]{3,2,1,0:T(8,128)(2,1)S(1)}, u32[]{:S(2)}, u32[]{:S(2)}) collective-permute-start(bf16[2,1,80,128]{3,2,1,0:T(8,128)(2,1)S(1)} %slice.640), channel_id=1, source_target_pairs={{0,1},{1,2},{2,3},{3,4},{4,5},{5,6},{6,7},{7,8},{8,9},{9,10},{10,1... | collective-permute-start | bytes 122888 | tf_op jit(solution)/shard_map/ppermute | solution.py:14
  115.0 22.2 %collective-permute-start.13 = (bf16[2,1,80,128]{3,2,1,0:T(8,128)(2,1)S(1)}, bf16[2,1,80,128]{3,2,1,0:T(8,128)(2,1)S(1)}, u32[]{:S(2)}, u32[]{:S(2)}) collective-permute-start(bf16[2,1,80,128]{3,2,1,0:T(8,128)(2,1)S(1)} %slice.645), channel_id=1, source_target_pairs={{1,0},{2,1},{3,2},{4,3},{5,4},{6,5},{7,6},{8,7},{9,8},{10,9},{11,1... | collective-permute-start | bytes 122888 | tf_op jit(solution)/shard_map/ppermute | solution.py:14
  133.0 11.6 %collective-permute-start.11 = (bf16[1,4,80,128]{3,2,1,0:T(8,128)(2,1)S(1)}, bf16[1,4,80,128]{3,2,1,0:T(8,128)(2,1)S(1)}, u32[]{:S(2)}, u32[]{:S(2)}) collective-permute-start(bf16[1,4,80,128]{3,2,1,0:T(8,128)(2,1)S(1)} %get-tuple-element.143), channel_id=1, source_target_pairs={{16,0},{32,16},{48,32},{64,48},{80,64},{96,80},{112,96},{128,112},... | collective-permute-start | bytes 245768 | tf_op jit(solution)/shard_map/ppermute | solution.py:14
  137.2 9.7 %collective-permute-start.10 = (bf16[1,4,80,128]{3,2,1,0:T(8,128)(2,1)S(1)}, bf16[1,4,80,128]{3,2,1,0:T(8,128)(2,1)S(1)}, u32[]{:S(2)}, u32[]{:S(2)}) collective-permute-start(bf16[1,4,80,128]{3,2,1,0:T(8,128)(2,1)S(1)} %get-tuple-element.145), channel_id=1, source_target_pairs={{0,16},{16,32},{32,48},{48,64},{64,80},{80,96},{96,112},{112,128},... | collective-permute-start | bytes 245768 | tf_op jit(solution)/shard_map/ppermute | solution.py:14
  141.3 22.9 %copy-start.4 = (f32[256,640]{1,0:T(8,128)S(1)}, f32[256,640]{1,0:T(8,128)}, u32[]{:S(2)}) copy-start(f32[256,640]{1,0:T(8,128)} %get-tuple-element.133) | copy-start | bytes 1966084
  144.6 61.5 %collective-permute-start.28 = (f32[4,64,640]{2,1,0:T(8,128)}, f32[4,64,640]{2,1,0:T(8,128)}, u32[]{:S(2)}, u32[]{:S(2)}) collective-permute-start(f32[4,64,640]{2,1,0:T(8,128)} %bitcast.78), channel_id=1, source_target_pairs={{0,3},{1,0},{2,1},{3,2},{4,7},{5,4},{6,5},{7,6},{8,11},{9,8},{10,9... | collective-permute-start | bytes 1966088 | tf_op jit(solution)/shard_map/ppermute | solution.py:23
  146.9 59.2 %collective-permute-start.26 = (f32[4,64,640]{2,1,0:T(8,128)}, f32[4,64,640]{2,1,0:T(8,128)}, u32[]{:S(2)}, u32[]{:S(2)}) collective-permute-start(f32[4,64,640]{2,1,0:T(8,128)} %bitcast.76), channel_id=1, source_target_pairs={{0,1},{1,2},{2,3},{3,0},{4,5},{5,6},{6,7},{7,4},{8,9},{9,10},{10,1... | collective-permute-start | bytes 1966088 | tf_op jit(solution)/shard_map/ppermute | solution.py:23
  152.1 54.0 %collective-permute-start.27 = (f32[4,64,640]{2,1,0:T(8,128)}, f32[4,64,640]{2,1,0:T(8,128)}, u32[]{:S(2)}, u32[]{:S(2)}) collective-permute-start(f32[4,64,640]{2,1,0:T(8,128)} %bitcast.77), channel_id=1, source_target_pairs={{0,2},{1,3},{2,0},{3,1},{4,6},{5,7},{6,4},{7,5},{8,10},{9,11},{10,... | collective-permute-start | bytes 1966088 | tf_op jit(solution)/shard_map/ppermute | solution.py:23
  164.3 3.7 %copy-start.1 = (f32[2,4,4,4,4,5,128]{6,1,5,4,3,2,0:T(4,128)S(1)}, f32[2,4,4,4,4,5,128]{6,1,5,4,3,2,0:T(4,128)}, u32[]{:S(2)}) copy-start(f32[2,4,4,4,4,5,128]{6,1,5,4,3,2,0:T(4,128)} %copy.131) | copy-start | bytes 3932164
  166.1 16.2 %collective-permute-start.17 = (f32[64,640]{1,0:T(8,128)S(1)}, f32[64,640]{1,0:T(8,128)S(1)}, u32[]{:S(2)}, u32[]{:S(2)}) collective-permute-start(f32[64,640]{1,0:T(8,128)S(1)} %get-tuple-element.137), channel_id=1, source_target_pairs={{0,4},{1,5},{2,6},{3,7},{4,8},{5,9},{6,10},{7,11},{8,12},{9,13},{1... | collective-permute-start | bytes 491528 | tf_op jit(solution)/shard_map/ppermute | solution.py:23
  168.2 24.1 %collective-permute-start.19 = (f32[64,640]{1,0:T(8,128)S(1)}, f32[64,640]{1,0:T(8,128)S(1)}, u32[]{:S(2)}, u32[]{:S(2)}) collective-permute-start(f32[64,640]{1,0:T(8,128)S(1)} %get-tuple-element.138), channel_id=1, source_target_pairs={{0,12},{1,13},{2,14},{3,15},{4,0},{5,1},{6,2},{7,3},{8,4},{9,5},{1... | collective-permute-start | bytes 491528 | tf_op jit(solution)/shard_map/ppermute | solution.py:23
  182.3 21.4 %collective-permute-start.18 = (f32[64,640]{1,0:T(8,128)S(1)}, f32[64,640]{1,0:T(8,128)S(1)}, u32[]{:S(2)}, u32[]{:S(2)}) collective-permute-start(f32[64,640]{1,0:T(8,128)S(1)} %get-tuple-element.139), channel_id=1, source_target_pairs={{0,8},{1,9},{2,10},{3,11},{4,12},{5,13},{6,14},{7,15},{8,0},{9,1},... | collective-permute-start | bytes 491528 | tf_op jit(solution)/shard_map/ppermute | solution.py:23
  206.1 23.9 %copy-start.9 = (f32[64,5,128]{2,1,0:T(8,128)S(1)}, f32[64,5,128]{2,1,0:T(8,128)}, u32[]{:S(2)}) copy-start(f32[64,5,128]{2,1,0:T(8,128)} %reshape.979) | copy-start | bytes 491524
  208.0 23.1 %collective-permute-start.29 = (f32[64,640]{1,0:T(8,128)S(1)}, f32[64,640]{1,0:T(8,128)S(1)}, u32[]{:S(2)}, u32[]{:S(2)}) collective-permute-start(f32[64,640]{1,0:T(8,128)S(1)} %get-tuple-element.134), channel_id=1, source_target_pairs={{0,4},{1,5},{2,6},{3,7},{4,8},{5,9},{6,10},{7,11},{8,12},{9,13},{1... | collective-permute-start | bytes 491528 | tf_op jit(solution)/shard_map/ppermute | solution.py:23
  209.9 21.2 %collective-permute-start.31 = (f32[64,640]{1,0:T(8,128)S(1)}, f32[64,640]{1,0:T(8,128)S(1)}, u32[]{:S(2)}, u32[]{:S(2)}) collective-permute-start(f32[64,640]{1,0:T(8,128)S(1)} %get-tuple-element.135), channel_id=1, source_target_pairs={{0,12},{1,13},{2,14},{3,15},{4,0},{5,1},{6,2},{7,3},{8,4},{9,5},{1... | collective-permute-start | bytes 491528 | tf_op jit(solution)/shard_map/ppermute | solution.py:23
  217.2 25.4 %collective-permute-start.30 = (f32[64,640]{1,0:T(8,128)S(1)}, f32[64,640]{1,0:T(8,128)S(1)}, u32[]{:S(2)}, u32[]{:S(2)}) collective-permute-start(f32[64,640]{1,0:T(8,128)S(1)} %get-tuple-element.136), channel_id=1, source_target_pairs={{0,8},{1,9},{2,10},{3,11},{4,12},{5,13},{6,14},{7,15},{8,0},{9,1},... | collective-permute-start | bytes 491528 | tf_op jit(solution)/shard_map/ppermute | solution.py:23
  245.0 27.3 %copy-start.10 = (bf16[2,3,4,1,4,5,128]{6,1,5,4,3,2,0:T(4,128)(2,1)S(1)}, bf16[2,3,4,1,4,5,128]{6,1,5,4,3,2,0:T(4,128)(2,1)}, u32[]{:S(2)}) copy-start(bf16[2,3,4,1,4,5,128]{6,1,5,4,3,2,0:T(4,128)(2,1)} %copy.64) | copy-start | bytes 368644
  245.0 27.4 %copy-start.16 = (bf16[2,1,4,1,4,5,128]{6,1,5,4,3,2,0:T(2,128)(2,1)S(1)}, bf16[2,1,4,1,4,5,128]{6,1,5,4,3,2,0:T(2,128)(2,1)}, u32[]{:S(2)}) copy-start(bf16[2,1,4,1,4,5,128]{6,1,5,4,3,2,0:T(2,128)(2,1)} %copy.63) | copy-start | bytes 122884
  248.7 23.9 %copy-start.5 = (bf16[64,128,6]{1,2,0:T(8,128)(2,1)}, bf16[64,128,6]{1,2,0:T(8,128)(2,1)S(1)}, u32[]{:S(2)}) copy-start(bf16[64,128,6]{1,2,0:T(8,128)(2,1)S(1)} %convolution_convert_fusion.4) | copy-start | bytes 294916
  249.4 24.9 %collective-permute-start.22 = (bf16[64,768]{1,0:T(8,128)(2,1)}, bf16[64,768]{1,0:T(8,128)(2,1)}, u32[]{:S(2)}, u32[]{:S(2)}) collective-permute-start(bf16[64,768]{1,0:T(8,128)(2,1)} %bitcast.174), channel_id=1, source_target_pairs={{0,12},{1,13},{2,14},{3,15},{4,0},{5,1},{6,2},{7,3},{8,4},{9,5},{1... | collective-permute-start | bytes 294920 | tf_op jit(solution)/shard_map/ppermute | solution.py:23
  256.3 18.0 %collective-permute-start.21 = (bf16[64,768]{1,0:T(8,128)(2,1)}, bf16[64,768]{1,0:T(8,128)(2,1)}, u32[]{:S(2)}, u32[]{:S(2)}) collective-permute-start(bf16[64,768]{1,0:T(8,128)(2,1)} %bitcast.174), channel_id=1, source_target_pairs={{0,8},{1,9},{2,10},{3,11},{4,12},{5,13},{6,14},{7,15},{8,0},{9,1},... | collective-permute-start | bytes 294920 | tf_op jit(solution)/shard_map/ppermute | solution.py:23
  267.4 16.9 %collective-permute-start.20 = (bf16[64,768]{1,0:T(8,128)(2,1)}, bf16[64,768]{1,0:T(8,128)(2,1)}, u32[]{:S(2)}, u32[]{:S(2)}) collective-permute-start(bf16[64,768]{1,0:T(8,128)(2,1)} %bitcast.174), channel_id=1, source_target_pairs={{0,4},{1,5},{2,6},{3,7},{4,8},{5,9},{6,10},{7,11},{8,12},{9,13},{1... | collective-permute-start | bytes 294920 | tf_op jit(solution)/shard_map/ppermute | solution.py:23
  274.3 19.7 %copy-start.8 = (f32[64,6,128]{2,0,1:T(8,128)S(1)}, f32[64,6,128]{2,0,1:T(8,128)}, u32[]{:S(2)}) copy-start(f32[64,6,128]{2,0,1:T(8,128)} %get-tuple-element.156) | copy-start | bytes 589828
  285.4 13.2 %collective-permute-start.24 = (bf16[4,64,768]{2,1,0:T(8,128)(2,1)S(1)}, bf16[4,64,768]{2,1,0:T(8,128)(2,1)S(1)}, u32[]{:S(2)}, u32[]{:S(2)}) collective-permute-start(bf16[4,64,768]{2,1,0:T(8,128)(2,1)S(1)} %get-tuple-element.153), channel_id=1, source_target_pairs={{0,2},{1,3},{2,0},{3,1},{4,6},{5,7},{6,4},{7,5},{8,10},{9,11},{10,... | collective-permute-start | bytes 1179656 | tf_op jit(solution)/shard_map/ppermute | solution.py:23
  287.3 14.9 %collective-permute-start.23 = (bf16[4,64,768]{2,1,0:T(8,128)(2,1)S(1)}, bf16[4,64,768]{2,1,0:T(8,128)(2,1)S(1)}, u32[]{:S(2)}, u32[]{:S(2)}) collective-permute-start(bf16[4,64,768]{2,1,0:T(8,128)(2,1)S(1)} %get-tuple-element.153), channel_id=1, source_target_pairs={{0,1},{1,2},{2,3},{3,0},{4,5},{5,6},{6,7},{7,4},{8,9},{9,10},{10,1... | collective-permute-start | bytes 1179656 | tf_op jit(solution)/shard_map/ppermute | solution.py:23
  289.4 18.9 %collective-permute-start.25 = (bf16[4,64,768]{2,1,0:T(8,128)(2,1)S(1)}, bf16[4,64,768]{2,1,0:T(8,128)(2,1)S(1)}, u32[]{:S(2)}, u32[]{:S(2)}) collective-permute-start(bf16[4,64,768]{2,1,0:T(8,128)(2,1)S(1)} %get-tuple-element.153), channel_id=1, source_target_pairs={{0,3},{1,0},{2,1},{3,2},{4,7},{5,4},{6,5},{7,6},{8,11},{9,8},{10,9... | collective-permute-start | bytes 1179656 | tf_op jit(solution)/shard_map/ppermute | solution.py:23

commit v3 on v2

--- a/solution.py
+++ b/solution.py
@@ -66,21 +66,13 @@
     return (low_span, high_span, low_chord, high_chord)
 
 
-def gather_strip(shell):
-    cz = lax.axis_size("chord") // CY
-    first = jnp.stack([shell] + [chord_shift(shell, k, 0) for k in range(1, cz)])
-    return jnp.stack([first] + [chord_shift(first, 0, k) for k in range(1, CY)])
+def over_y(block):
+    return [block] + [chord_shift(block, 0, k) for k in range(1, CY)]
 
 
-def reduce_strip(partial):
-    cz = partial.shape[1]
-    part = partial[0]
-    for k in range(1, CY):
-        part = part + chord_shift(partial[k], 0, k)
-    total = part[0]
-    for k in range(1, cz):
-        total = total + chord_shift(part[k], k, 0)
-    return total
+def over_z(block):
+    cz = lax.axis_size("chord") // CY
+    return [block] + [chord_shift(block, k, 0) for k in range(1, cz)]
 
 
 def per_device(adj_rhs, diag_inv, face_jac, face_mask, wall_map, couple, shell_rhs, shell_inv):
@@ -95,12 +87,13 @@
     wall_local = wall_map.reshape(-1)
     wall_count = wall_local.shape[0]
     node = lax.iota(jnp.int32, shell_count)
-    ky = lax.iota(jnp.int32, CY)[:, None, None]
-    kz = lax.iota(jnp.int32, cz)[None, :, None]
-    got_ids = ((((zpos - kz) % cz) * CY + (ypos - ky) % CY) * shell_count + node).reshape(-1)
-    out_ids = ((((zpos + kz) % cz) * CY + (ypos + ky) % CY) * shell_count + node).reshape(-1)
-    pick_hit = (wall_local[:, None] == got_ids[None, :]).astype(jnp.bfloat16)
-    load_hit = (out_ids[:, None] == wall_local[None, :]).astype(jnp.bfloat16)
+    kz = lax.iota(jnp.int32, cz)[:, None]
+    got_ids = ((((zpos - kz) % cz) * CY + ypos) * shell_count + node).reshape(-1)
+    out_ids = ((((zpos + kz) % cz) * CY + ypos) * shell_count + node).reshape(-1)
+    maps_to = [wall_local] + [chord_shift(wall_local, 0, -k) for k in range(1, CY)]
+    maps_from = jnp.concatenate(over_y(wall_local))
+    pick_hits = [(m[:, None] == got_ids[None, :]).astype(jnp.bfloat16) for m in maps_to]
+    load_hit = (out_ids[:, None] == maps_from[None, :]).astype(jnp.bfloat16)
     fluid = jnp.einsum(
         "abmn,abnr->abmr", diag_inv, adj_rhs, preferred_element_type=jnp.float32
     ).astype(jnp.bfloat16)
@@ -113,17 +106,26 @@
         sent = jnp.einsum("abdmn,abnr->abdmr", face_jac, fluid, preferred_element_type=jnp.float32)
         sent = (sent * weights).astype(jnp.bfloat16)
         low_span, high_span, low_chord, high_chord = face_terms(sent)
-        strip = gather_strip(shell.reshape(shell_count, sdof * width))
-        strip = strip.reshape(size * shell_count, sdof * width)
-        picked = jnp.dot(pick_hit, strip, preferred_element_type=jnp.float32)
+        column = jnp.concatenate(over_z(shell.reshape(shell_count, sdof * width)))
+        served = [
+            jnp.dot(h, column, preferred_element_type=jnp.float32).astype(jnp.bfloat16)
+            for h in pick_hits
+        ]
+        picked = served[0].astype(jnp.float32)
+        for k in range(1, CY):
+            picked = picked + chord_shift(served[k], 0, k).astype(jnp.float32)
         wall_in = jnp.einsum(
             "sv,wsr->wvr", couple, picked.reshape(wall_count, sdof, width), precision=high
         )
         wall_rows = fluid.reshape(rows, cols, 4, 4, 4, NV, width)[:, :, :, :, 0].reshape(
             wall_count, NV * width
         )
-        partial = jnp.dot(load_hit, wall_rows, preferred_element_type=jnp.float32)
-        summed = reduce_strip(partial.reshape(CY, cz, shell_count, NV * width))
+        row_group = jnp.concatenate(over_y(wall_rows))
+        partial = jnp.dot(load_hit, row_group, preferred_element_type=jnp.float32)
+        partial = partial.reshape(cz, shell_count, NV * width)
+        summed = partial[0]
+        for k in range(1, cz):
+            summed = summed + chord_shift(partial[k], k, 0)
         shell_load = jnp.einsum(
             "sv,nvr->nsr", couple, summed.reshape(shell_count, NV, width), precision=high
         )

time: 319 us -> 284 us (0.89)
  the two profiles are of different devices: /device:TPU:45 before, /device:TPU:1 now
where the time goes in v3:
time: 284 us; the launch traced here: 282 us
  starting transfers between devices  157 us (55%)
  waiting for transfers between devices  47.5 us (17%)
  local copies, waits for them, and re-layouts  43.6 us (15%)
  matrix products  23.9 us (8%)
  other arithmetic  9.09 us (3%)
    ppermute x27, starting transfers between devices, chord_shift(): return lax.ppermute(block, 'chord', route)  134 us
    ppermute x27, waiting for transfers between devices, chord_shift(): return lax.ppermute(block, 'chord', route)  40.6 us
    ppermute x8, starting transfers between devices, passed_along(): return lax.ppermute(block, axis, route)  22.1 us
    unnamed x61, local copies, waits for them, and re-layouts  7.96 us
    dot_general x8, matrix products, per_device(): jnp.dot(h, column, preferred_element_type=jnp.float32).astype(jnp.bfloat16)  7.34 us
    ppermute x8, waiting for transfers between devices, passed_along(): return lax.ppermute(block, axis, route)  6.88 us
  transfers between devices with their start and end apart: 35, of which 8 were waited for; matrix products, arithmetic and copies ran while one was open for 19% of the time, Pallas kernels for 0%

profile of v3, /device:TPU:1, one launch (start us, length us, event | category | flops | bytes accessed | tf_op | source)
XLA Modules:
  0.0 282.3 jit_solution(3185536973651422575)
XLA Ops:
  0.6 1.0 copy.51
  1.7 1.3 convolution_convert_fusion.13
  3.6 9.6 %collective-permute-start.4 = (bf16[64,768]{1,0:T(8,128)(2,1)}, bf16[64,768]{1,0:T(8,128)(2,1)}, u32[]{:S(2)}, u32[]{:S(2)}) collective-permute-start(bf16[64,768]{1,0:T(8,128)(2,1)} %get-tuple-element.129), channel_id=1, source_target_pairs={{0,4},{1,5},{2,6},{3,7},{4,8},{5,9},{6,10},{7,11},{8,12},{9,13},{1... | collective-permute-start | bytes 294920 | tf_op jit(solution)/shard_map/ppermute | solution.py:23
  13.3 10.6 %collective-permute-start.5 = (bf16[64,768]{1,0:T(8,128)(2,1)}, bf16[64,768]{1,0:T(8,128)(2,1)}, u32[]{:S(2)}, u32[]{:S(2)}) collective-permute-start(bf16[64,768]{1,0:T(8,128)(2,1)} %get-tuple-element.129), channel_id=1, source_target_pairs={{0,8},{1,9},{2,10},{3,11},{4,12},{5,13},{6,14},{7,15},{8,0},{9,1},... | collective-permute-start | bytes 294920 | tf_op jit(solution)/shard_map/ppermute | solution.py:23
  24.7 3.2 %collective-permute-start.11 = (s32[128]{0:T(128)S(1)}, s32[128]{0:T(128)}, u32[]{:S(2)}, u32[]{:S(2)}) collective-permute-start(s32[128]{0:T(128)S(1)} %eq.31), channel_id=1, source_target_pairs={{0,1},{1,2},{2,3},{3,0},{4,5},{5,6},{6,7},{7,4},{8,9},{9,10},{10,1... | collective-permute-start | bytes 1544 | tf_op jit(solution)/shard_map/ppermute | solution.py:23
  27.9 4.5 %collective-permute-start.9 = (s32[128]{0:T(128)S(1)}, s32[128]{0:T(128)}, u32[]{:S(2)}, u32[]{:S(2)}) collective-permute-start(s32[128]{0:T(128)S(1)} %eq.31), channel_id=1, source_target_pairs={{0,2},{1,3},{2,0},{3,1},{4,6},{5,7},{6,4},{7,5},{8,10},{9,11},{10,... | collective-permute-start | bytes 1544 | tf_op jit(solution)/shard_map/ppermute | solution.py:23
  32.4 3.0 %collective-permute-start.7 = (s32[128]{0:T(128)S(1)}, s32[128]{0:T(128)}, u32[]{:S(2)}, u32[]{:S(2)}) collective-permute-start(s32[128]{0:T(128)S(1)} %eq.31), channel_id=1, source_target_pairs={{0,3},{1,0},{2,1},{3,2},{4,7},{5,4},{6,5},{7,6},{8,11},{9,8},{10,9... | collective-permute-start | bytes 1544 | tf_op jit(solution)/shard_map/ppermute | solution.py:23
  35.4 1.6 copy.38
  37.1 1.9 convolution_convert_fusion.2
  43.1 2.4 copy.70
  45.5 1.1 copy.126
  51.4 1.3 add.226
  53.8 4.7 %collective-permute-start = (bf16[1,4,80,128]{3,2,1,0:T(8,128)(2,1)}, bf16[1,4,80,128]{3,2,1,0:T(8,128)(2,1)S(1)}, u32[]{:S(2)}, u32[]{:S(2)}) collective-permute-start(bf16[1,4,80,128]{3,2,1,0:T(8,128)(2,1)} %get-tuple-element.147), channel_id=1, source_target_pairs={{0,16},{16,32},{32,48},{48,64},{64,80},{80,96},{96,112},{112,128},... | collective-permute-start | bytes 245768 | tf_op jit(solution)/shard_map/ppermute | solution.py:14
  58.6 2.3 collective-permute-start.2
  60.9 1.3 collective-permute-start.3
  62.9 13.4 %collective-permute-start.6 = (bf16[64,768]{1,0:T(8,128)(2,1)}, bf16[64,768]{1,0:T(8,128)(2,1)S(1)}, u32[]{:S(2)}, u32[]{:S(2)}) collective-permute-start(bf16[64,768]{1,0:T(8,128)(2,1)} %get-tuple-element.129), channel_id=1, source_target_pairs={{0,12},{1,13},{2,14},{3,15},{4,0},{5,1},{6,2},{7,3},{8,4},{9,5},{1... | collective-permute-start | bytes 294920 | tf_op jit(solution)/shard_map/ppermute | solution.py:23
  76.5 2.5 collective-permute-start.1
  79.0 1.9 collective-permute-start.19
  81.2 6.3 %collective-permute-done.1 = bf16[1,4,80,128]{3,2,1,0:T(8,128)(2,1)S(1)} collective-permute-done((bf16[1,4,80,128]{3,2,1,0:T(8,128)(2,1)S(1)}, bf16[1,4,80,128]{3,2,1,0:T(8,128)(2,1)S(1)}, u32[]{:S(2)}, u32[]{:S(2)}) %collective-permute-start.1) | collective-permute-done | bytes 81952 | tf_op jit(solution)/shard_map/ppermute | solution.py:14
  87.5 1.9 collective-permute-start.18
  90.3 1.9 collective-permute-start.17
  95.0 4.6 %collective-permute-start.12 = (bf16[128,768]{1,0:T(8,128)(2,1)S(1)}, bf16[128,768]{1,0:T(8,128)(2,1)S(1)}, u32[]{:S(2)}, u32[]{:S(2)}) collective-permute-start(bf16[128,768]{1,0:T(8,128)(2,1)S(1)} %convolution_convert_fusion.7), channel_id=1, source_target_pairs={{0,3},{1,0},{2,1},{3,2},{4,7},{5,4},{6,5},{7,6},{8,11},{9,8},{10,9... | collective-permute-start | bytes 589832 | tf_op jit(solution)/shard_map/ppermute | solution.py:23
  100.4 3.7 %collective-permute-start.10 = (bf16[128,768]{1,0:T(8,128)(2,1)S(1)}, bf16[128,768]{1,0:T(8,128)(2,1)S(1)}, u32[]{:S(2)}, u32[]{:S(2)}) collective-permute-start(bf16[128,768]{1,0:T(8,128)(2,1)S(1)} %convolution_convert_fusion.8), channel_id=1, source_target_pairs={{0,2},{1,3},{2,0},{3,1},{4,6},{5,7},{6,4},{7,5},{8,10},{9,11},{10,... | collective-permute-start | bytes 589832 | tf_op jit(solution)/shard_map/ppermute | solution.py:23
  105.0 1.9 collective-permute-start.8
  109.0 3.0 %collective-permute-start.22 = (f32[64,640]{1,0:T(8,128)}, f32[64,640]{1,0:T(8,128)}, u32[]{:S(2)}, u32[]{:S(2)}) collective-permute-start(f32[64,640]{1,0:T(8,128)} %get-tuple-element.134), channel_id=1, source_target_pairs={{0,12},{1,13},{2,14},{3,15},{4,0},{5,1},{6,2},{7,3},{8,4},{9,5},{1... | collective-permute-start | bytes 491528 | tf_op jit(solution)/shard_map/ppermute | solution.py:23
  112.1 2.7 collective-permute-start.21
  114.8 7.0 %collective-permute-start.20 = (f32[64,640]{1,0:T(8,128)}, f32[64,640]{1,0:T(8,128)}, u32[]{:S(2)}, u32[]{:S(2)}) collective-permute-start(f32[64,640]{1,0:T(8,128)} %get-tuple-element.133), channel_id=1, source_target_pairs={{0,4},{1,5},{2,6},{3,7},{4,8},{5,9},{6,10},{7,11},{8,12},{9,13},{1... | collective-permute-start | bytes 491528 | tf_op jit(solution)/shard_map/ppermute | solution.py:23
  122.9 1.9 copy.53
  124.8 2.0 copy.54
  126.8 1.7 convolution_negate_fusion.1
  133.9 4.6 %collective-permute-start.31 = (bf16[128,640]{1,0:T(8,128)(2,1)}, bf16[128,640]{1,0:T(8,128)(2,1)}, u32[]{:S(2)}, u32[]{:S(2)}) collective-permute-start(bf16[128,640]{1,0:T(8,128)(2,1)} %bitcast.119), channel_id=1, source_target_pairs={{0,3},{1,0},{2,1},{3,2},{4,7},{5,4},{6,5},{7,6},{8,11},{9,8},{10,9... | collective-permute-start | bytes 491528 | tf_op jit(solution)/shard_map/ppermute | solution.py:23
  138.5 1.9 collective-permute-start.30
  144.1 5.0 %collective-permute-start.13 = (bf16[1,4,80,128]{3,2,1,0:T(8,128)(2,1)}, bf16[1,4,80,128]{3,2,1,0:T(8,128)(2,1)}, u32[]{:S(2)}, u32[]{:S(2)}) collective-permute-start(bf16[1,4,80,128]{3,2,1,0:T(8,128)(2,1)} %get-tuple-element.141), channel_id=1, source_target_pairs={{0,16},{16,32},{32,48},{48,64},{64,80},{80,96},{96,112},{112,128},... | collective-permute-start | bytes 245768 | tf_op jit(solution)/shard_map/ppermute | solution.py:14
  149.2 3.1 %collective-permute-start.15 = (bf16[2,1,80,128]{3,2,1,0:T(8,128)(2,1)}, bf16[2,1,80,128]{3,2,1,0:T(8,128)(2,1)}, u32[]{:S(2)}, u32[]{:S(2)}) collective-permute-start(bf16[2,1,80,128]{3,2,1,0:T(8,128)(2,1)} %slice.608), channel_id=1, source_target_pairs={{0,1},{1,2},{2,3},{3,4},{4,5},{5,6},{6,7},{7,8},{8,9},{9,10},{10,1... | collective-permute-start | bytes 122888 | tf_op jit(solution)/shard_map/ppermute | solution.py:14
  152.3 1.3 collective-permute-start.16
  153.6 1.9 fusion.61
  155.4 1.6 reshape.875
  157.1 2.0 fusion.82
  159.1 4.3 %collective-permute-start.29 = (bf16[128,640]{1,0:T(8,128)(2,1)}, bf16[128,640]{1,0:T(8,128)(2,1)S(1)}, u32[]{:S(2)}, u32[]{:S(2)}) collective-permute-start(bf16[128,640]{1,0:T(8,128)(2,1)} %bitcast.119), channel_id=1, source_target_pairs={{0,1},{1,2},{2,3},{3,0},{4,5},{5,6},{6,7},{7,4},{8,9},{9,10},{10,1... | collective-permute-start | bytes 491528 | tf_op jit(solution)/shard_map/ppermute | solution.py:23
  164.3 1.9 collective-permute-start.14
  168.7 1.0 add_dynamic-update-slice_fusion
  170.6 1.5 fusion.14
  172.1 8.8 %collective-permute-start.34 = (f32[64,640]{1,0:T(8,128)S(1)}, f32[64,640]{1,0:T(8,128)S(1)}, u32[]{:S(2)}, u32[]{:S(2)}) collective-permute-start(f32[64,640]{1,0:T(8,128)S(1)} %get-tuple-element.131), channel_id=1, source_target_pairs={{0,12},{1,13},{2,14},{3,15},{4,0},{5,1},{6,2},{7,3},{8,4},{9,5},{1... | collective-permute-start | bytes 491528 | tf_op jit(solution)/shard_map/ppermute | solution.py:23
  181.0 8.7 %collective-permute-start.33 = (f32[64,640]{1,0:T(8,128)S(1)}, f32[64,640]{1,0:T(8,128)S(1)}, u32[]{:S(2)}, u32[]{:S(2)}) collective-permute-start(f32[64,640]{1,0:T(8,128)S(1)} %get-tuple-element.132), channel_id=1, source_target_pairs={{0,8},{1,9},{2,10},{3,11},{4,12},{5,13},{6,14},{7,15},{8,0},{9,1},... | collective-permute-start | bytes 491528 | tf_op jit(solution)/shard_map/ppermute | solution.py:23
  189.7 5.9 %collective-permute-start.32 = (f32[64,640]{1,0:T(8,128)S(1)}, f32[64,640]{1,0:T(8,128)S(1)}, u32[]{:S(2)}, u32[]{:S(2)}) collective-permute-start(f32[64,640]{1,0:T(8,128)S(1)} %get-tuple-element.130), channel_id=1, source_target_pairs={{0,4},{1,5},{2,6},{3,7},{4,8},{5,9},{6,10},{7,11},{8,12},{9,13},{1... | collective-permute-start | bytes 491528 | tf_op jit(solution)/shard_map/ppermute | solution.py:23
  195.9 11.5 %collective-permute-done.34 = f32[64,640]{1,0:T(8,128)S(1)} collective-permute-done((f32[64,640]{1,0:T(8,128)S(1)}, f32[64,640]{1,0:T(8,128)S(1)}, u32[]{:S(2)}, u32[]{:S(2)}) %collective-permute-start.34) | collective-permute-done | bytes 163872 | tf_op jit(solution)/shard_map/ppermute | solution.py:23
  207.5 7.5 %collective-permute-done.32 = f32[64,640]{1,0:T(8,128)S(1)} collective-permute-done((f32[64,640]{1,0:T(8,128)S(1)}, f32[64,640]{1,0:T(8,128)S(1)}, u32[]{:S(2)}, u32[]{:S(2)}) %collective-permute-start.32) | collective-permute-done | bytes 163872 | tf_op jit(solution)/shard_map/ppermute | solution.py:23
  215.7 1.6 reshape.879
  217.3 1.3 fusion.80
  218.7 1.1 convert_subtract_fusion
  220.5 5.7 %collective-permute-start.23 = (bf16[64,768]{1,0:T(8,128)(2,1)S(1)}, bf16[64,768]{1,0:T(8,128)(2,1)S(1)}, u32[]{:S(2)}, u32[]{:S(2)}) collective-permute-start(bf16[64,768]{1,0:T(8,128)(2,1)S(1)} %get-tuple-element.127), channel_id=1, source_target_pairs={{0,4},{1,5},{2,6},{3,7},{4,8},{5,9},{6,10},{7,11},{8,12},{9,13},{1... | collective-permute-start | bytes 294920 | tf_op jit(solution)/shard_map/ppermute | solution.py:23
  226.5 6.7 %collective-permute-start.24 = (bf16[64,768]{1,0:T(8,128)(2,1)S(1)}, bf16[64,768]{1,0:T(8,128)(2,1)S(1)}, u32[]{:S(2)}, u32[]{:S(2)}) collective-permute-start(bf16[64,768]{1,0:T(8,128)(2,1)S(1)} %get-tuple-element.127), channel_id=1, source_target_pairs={{0,8},{1,9},{2,10},{3,11},{4,12},{5,13},{6,14},{7,15},{8,0},{9,1},... | collective-permute-start | bytes 294920 | tf_op jit(solution)/shard_map/ppermute | solution.py:23
  233.2 7.3 %collective-permute-start.25 = (bf16[64,768]{1,0:T(8,128)(2,1)S(1)}, bf16[64,768]{1,0:T(8,128)(2,1)S(1)}, u32[]{:S(2)}, u32[]{:S(2)}) collective-permute-start(bf16[64,768]{1,0:T(8,128)(2,1)S(1)} %get-tuple-element.127), channel_id=1, source_target_pairs={{0,12},{1,13},{2,14},{3,15},{4,0},{5,1},{6,2},{7,3},{8,4},{9,5},{1... | collective-permute-start | bytes 294920 | tf_op jit(solution)/shard_map/ppermute | solution.py:23
  240.5 2.8 %collective-permute-done.24 = bf16[64,768]{1,0:T(8,128)(2,1)S(1)} collective-permute-done((bf16[64,768]{1,0:T(8,128)(2,1)S(1)}, bf16[64,768]{1,0:T(8,128)(2,1)S(1)}, u32[]{:S(2)}, u32[]{:S(2)}) %collective-permute-start.24) | collective-permute-done | bytes 98336 | tf_op jit(solution)/shard_map/ppermute | solution.py:23
  243.4 10.9 %collective-permute-done.25 = bf16[64,768]{1,0:T(8,128)(2,1)S(1)} collective-permute-done((bf16[64,768]{1,0:T(8,128)(2,1)S(1)}, bf16[64,768]{1,0:T(8,128)(2,1)S(1)}, u32[]{:S(2)}, u32[]{:S(2)}) %collective-permute-start.25) | collective-permute-done | bytes 98336 | tf_op jit(solution)/shard_map/ppermute | solution.py:23
  255.3 3.1 %collective-permute-start.28 = (bf16[128,768]{1,0:T(8,128)(2,1)S(1)}, bf16[128,768]{1,0:T(8,128)(2,1)S(1)}, u32[]{:S(2)}, u32[]{:S(2)}) collective-permute-start(bf16[128,768]{1,0:T(8,128)(2,1)S(1)} %convolution_convert_fusion.3), channel_id=1, source_target_pairs={{0,3},{1,0},{2,1},{3,2},{4,7},{5,4},{6,5},{7,6},{8,11},{9,8},{10,9... | collective-permute-start | bytes 589832 | tf_op jit(solution)/shard_map/ppermute | solution.py:23
  259.2 1.9 collective-permute-start.27
  262.1 2.5 collective-permute-start.26
  265.9 2.4 collective-permute-done.27
  268.3 5.3 %collective-permute-done.26 = bf16[128,768]{1,0:T(8,128)(2,1)S(1)} collective-permute-done((bf16[128,768]{1,0:T(8,128)(2,1)S(1)}, bf16[128,768]{1,0:T(8,128)(2,1)S(1)}, u32[]{:S(2)}, u32[]{:S(2)}) %collective-permute-start.26) | collective-permute-done | bytes 196640 | tf_op jit(solution)/shard_map/ppermute | solution.py:23
  274.6 1.9 copy.74
  276.5 2.0 copy.75
  278.5 1.7 convolution_negate_fusion
  280.8 1.5 fusion.2
  (165 shorter events, 41.8 us)
Async XLA Ops:
  0.6 36.4 %copy-start = (bf16[2,4,320,320]{3,2,1,0:T(8,128)(2,1)S(1)}, bf16[2,4,320,320]{3,2,1,0:T(8,128)(2,1)}, u32[]{:S(2)}) copy-start(bf16[2,4,320,320]{3,2,1,0:T(8,128)(2,1)} %param.29) | copy-start | bytes 4915204
  3.6 86.6 %collective-permute-start.4 = (bf16[64,768]{1,0:T(8,128)(2,1)}, bf16[64,768]{1,0:T(8,128)(2,1)}, u32[]{:S(2)}, u32[]{:S(2)}) collective-permute-start(bf16[64,768]{1,0:T(8,128)(2,1)} %get-tuple-element.129), channel_id=1, source_target_pairs={{0,4},{1,5},{2,6},{3,7},{4,8},{5,9},{6,10},{7,11},{8,12},{9,13},{1... | collective-permute-start | bytes 294920 | tf_op jit(solution)/shard_map/ppermute | solution.py:23
  13.3 79.9 %collective-permute-start.5 = (bf16[64,768]{1,0:T(8,128)(2,1)}, bf16[64,768]{1,0:T(8,128)(2,1)}, u32[]{:S(2)}, u32[]{:S(2)}) collective-permute-start(bf16[64,768]{1,0:T(8,128)(2,1)} %get-tuple-element.129), channel_id=1, source_target_pairs={{0,8},{1,9},{2,10},{3,11},{4,12},{5,13},{6,14},{7,15},{8,0},{9,1},... | collective-permute-start | bytes 294920 | tf_op jit(solution)/shard_map/ppermute | solution.py:23
  24.7 29.1 %collective-permute-start.11 = (s32[128]{0:T(128)S(1)}, s32[128]{0:T(128)}, u32[]{:S(2)}, u32[]{:S(2)}) collective-permute-start(s32[128]{0:T(128)S(1)} %eq.31), channel_id=1, source_target_pairs={{0,1},{1,2},{2,3},{3,0},{4,5},{5,6},{6,7},{7,4},{8,9},{9,10},{10,1... | collective-permute-start | bytes 1544 | tf_op jit(solution)/shard_map/ppermute | solution.py:23
  27.9 30.7 %collective-permute-start.9 = (s32[128]{0:T(128)S(1)}, s32[128]{0:T(128)}, u32[]{:S(2)}, u32[]{:S(2)}) collective-permute-start(s32[128]{0:T(128)S(1)} %eq.31), channel_id=1, source_target_pairs={{0,2},{1,3},{2,0},{3,1},{4,6},{5,7},{6,4},{7,5},{8,10},{9,11},{10,... | collective-permute-start | bytes 1544 | tf_op jit(solution)/shard_map/ppermute | solution.py:23
  32.4 28.5 %collective-permute-start.7 = (s32[128]{0:T(128)S(1)}, s32[128]{0:T(128)}, u32[]{:S(2)}, u32[]{:S(2)}) collective-permute-start(s32[128]{0:T(128)S(1)} %eq.31), channel_id=1, source_target_pairs={{0,3},{1,0},{2,1},{3,2},{4,7},{5,4},{6,5},{7,6},{8,11},{9,8},{10,9... | collective-permute-start | bytes 1544 | tf_op jit(solution)/shard_map/ppermute | solution.py:23
  37.0 1.9 copy-start.20
  37.0 1.9 copy-start.2
  39.0 0.8 copy-start.5
  45.5 1.1 copy-start.16
  45.5 1.7 copy-start.15
  45.5 2.4 copy-start.11
  52.7 23.7 %copy-start.18 = (bf16[1,4,80,128]{3,2,1,0:T(8,128)(2,1)S(1)}, bf16[1,4,80,128]{3,2,1,0:T(8,128)(2,1)}, u32[]{:S(2)}) copy-start(bf16[1,4,80,128]{3,2,1,0:T(8,128)(2,1)} %get-tuple-element.145) | copy-start | bytes 245764
  52.7 28.3 %copy-start.13 = (bf16[1,4,1,80,128]{4,1,3,2,0:T(4,128)(2,1)S(1)}, bf16[1,4,1,80,128]{4,1,3,2,0:T(4,128)(2,1)}, u32[]{:S(2)}) copy-start(bf16[1,4,1,80,128]{4,1,3,2,0:T(4,128)(2,1)} %copy.40) | copy-start | bytes 245764
  52.7 36.7 %copy-start.12 = (bf16[1,4,1,80,128]{4,1,3,2,0:T(4,128)(2,1)S(1)}, bf16[1,4,1,80,128]{4,1,3,2,0:T(4,128)(2,1)}, u32[]{:S(2)}) copy-start(bf16[1,4,1,80,128]{4,1,3,2,0:T(4,128)(2,1)} %copy.41) | copy-start | bytes 245764
  53.8 35.8 %copy-start.7 = (bf16[2,3,4,1,4,5,128]{6,1,5,4,3,2,0:T(4,128)(2,1)S(1)}, bf16[2,3,4,1,4,5,128]{6,1,5,4,3,2,0:T(4,128)(2,1)}, u32[]{:S(2)}) copy-start(bf16[2,3,4,1,4,5,128]{6,1,5,4,3,2,0:T(4,128)(2,1)} %copy.46) | copy-start | bytes 368644
  53.8 25.2 %collective-permute-start = (bf16[1,4,80,128]{3,2,1,0:T(8,128)(2,1)}, bf16[1,4,80,128]{3,2,1,0:T(8,128)(2,1)S(1)}, u32[]{:S(2)}, u32[]{:S(2)}) collective-permute-start(bf16[1,4,80,128]{3,2,1,0:T(8,128)(2,1)} %get-tuple-element.147), channel_id=1, source_target_pairs={{0,16},{16,32},{32,48},{48,64},{64,80},{80,96},{96,112},{112,128},... | collective-permute-start | bytes 245768 | tf_op jit(solution)/shard_map/ppermute | solution.py:14
  58.6 4.3 %collective-permute-start.2 = (bf16[2,1,80,128]{3,2,1,0:T(8,128)(2,1)}, bf16[2,1,80,128]{3,2,1,0:T(8,128)(2,1)S(1)}, u32[]{:S(2)}, u32[]{:S(2)}) collective-permute-start(bf16[2,1,80,128]{3,2,1,0:T(8,128)(2,1)} %slice.594), channel_id=1, source_target_pairs={{0,1},{1,2},{2,3},{3,4},{4,5},{5,6},{6,7},{7,8},{8,9},{9,10},{10,1... | collective-permute-start | bytes 122888 | tf_op jit(solution)/shard_map/ppermute | solution.py:14
  60.9 15.5 %collective-permute-start.3 = (bf16[2,1,80,128]{3,2,1,0:T(8,128)(2,1)}, bf16[2,1,80,128]{3,2,1,0:T(8,128)(2,1)S(1)}, u32[]{:S(2)}, u32[]{:S(2)}) collective-permute-start(bf16[2,1,80,128]{3,2,1,0:T(8,128)(2,1)} %slice.599), channel_id=1, source_target_pairs={{1,0},{2,1},{3,2},{4,3},{5,4},{6,5},{7,6},{8,7},{9,8},{10,9},{11,1... | collective-permute-start | bytes 122888 | tf_op jit(solution)/shard_map/ppermute | solution.py:14
  62.9 44.0 %copy-start.21 = (s32[512]{0:T(512)}, s32[512]{0:T(512)S(1)}, u32[]{:S(2)}) copy-start(s32[512]{0:T(512)S(1)} %pad_add_fusion) | copy-start | bytes 6148
  62.9 31.1 %collective-permute-start.6 = (bf16[64,768]{1,0:T(8,128)(2,1)}, bf16[64,768]{1,0:T(8,128)(2,1)S(1)}, u32[]{:S(2)}, u32[]{:S(2)}) collective-permute-start(bf16[64,768]{1,0:T(8,128)(2,1)} %get-tuple-element.129), channel_id=1, source_target_pairs={{0,12},{1,13},{2,14},{3,15},{4,0},{5,1},{6,2},{7,3},{8,4},{9,5},{1... | collective-permute-start | bytes 294920 | tf_op jit(solution)/shard_map/ppermute | solution.py:23
  76.5 11.0 %collective-permute-start.1 = (bf16[1,4,80,128]{3,2,1,0:T(8,128)(2,1)S(1)}, bf16[1,4,80,128]{3,2,1,0:T(8,128)(2,1)S(1)}, u32[]{:S(2)}, u32[]{:S(2)}) collective-permute-start(bf16[1,4,80,128]{3,2,1,0:T(8,128)(2,1)S(1)} %copy-done.18), channel_id=1, source_target_pairs={{16,0},{32,16},{48,32},{64,48},{80,64},{96,80},{112,96},{128,112},... | collective-permute-start | bytes 245768 | tf_op jit(solution)/shard_map/ppermute | solution.py:14
  79.0 25.9 %collective-permute-start.19 = (bf16[128,640]{1,0:T(8,128)(2,1)S(1)}, bf16[128,640]{1,0:T(8,128)(2,1)S(1)}, u32[]{:S(2)}, u32[]{:S(2)}) collective-permute-start(bf16[128,640]{1,0:T(8,128)(2,1)S(1)} %bitcast.148), channel_id=1, source_target_pairs={{0,3},{1,0},{2,1},{3,2},{4,7},{5,4},{6,5},{7,6},{8,11},{9,8},{10,9... | collective-permute-start | bytes 491528 | tf_op jit(solution)/shard_map/ppermute | solution.py:23
  81.0 8.9 %copy-start.9 = (bf16[2,3,4,1,4,5,128]{6,1,5,4,3,2,0:T(4,128)(2,1)S(1)}, bf16[2,3,4,1,4,5,128]{6,1,5,4,3,2,0:T(4,128)(2,1)}, u32[]{:S(2)}) copy-start(bf16[2,3,4,1,4,5,128]{6,1,5,4,3,2,0:T(4,128)(2,1)} %copy.49) | copy-start | bytes 368644
  87.5 19.4 %collective-permute-start.18 = (bf16[128,640]{1,0:T(8,128)(2,1)S(1)}, bf16[128,640]{1,0:T(8,128)(2,1)S(1)}, u32[]{:S(2)}, u32[]{:S(2)}) collective-permute-start(bf16[128,640]{1,0:T(8,128)(2,1)S(1)} %bitcast.149), channel_id=1, source_target_pairs={{0,2},{1,3},{2,0},{3,1},{4,6},{5,7},{6,4},{7,5},{8,10},{9,11},{10,... | collective-permute-start | bytes 491528 | tf_op jit(solution)/shard_map/ppermute | solution.py:23
  89.4 2.8 copy-start.4
  90.3 16.7 %copy-start.23 = (s32[256]{0:T(256)S(1)}, s32[256]{0:T(256)}, u32[]{:S(2)}) copy-start(s32[256]{0:T(256)} %add.226) | copy-start | bytes 3076
  90.3 16.6 %collective-permute-start.17 = (bf16[128,640]{1,0:T(8,128)(2,1)S(1)}, bf16[128,640]{1,0:T(8,128)(2,1)S(1)}, u32[]{:S(2)}, u32[]{:S(2)}) collective-permute-start(bf16[128,640]{1,0:T(8,128)(2,1)S(1)} %bitcast.150), channel_id=1, source_target_pairs={{0,1},{1,2},{2,3},{3,0},{4,5},{5,6},{6,7},{7,4},{8,9},{9,10},{10,1... | collective-permute-start | bytes 491528 | tf_op jit(solution)/shard_map/ppermute | solution.py:23
  95.0 19.8 %collective-permute-start.12 = (bf16[128,768]{1,0:T(8,128)(2,1)S(1)}, bf16[128,768]{1,0:T(8,128)(2,1)S(1)}, u32[]{:S(2)}, u32[]{:S(2)}) collective-permute-start(bf16[128,768]{1,0:T(8,128)(2,1)S(1)} %convolution_convert_fusion.7), channel_id=1, source_target_pairs={{0,3},{1,0},{2,1},{3,2},{4,7},{5,4},{6,5},{7,6},{8,11},{9,8},{10,9... | collective-permute-start | bytes 589832 | tf_op jit(solution)/shard_map/ppermute | solution.py:23
  100.4 21.5 %collective-permute-start.10 = (bf16[128,768]{1,0:T(8,128)(2,1)S(1)}, bf16[128,768]{1,0:T(8,128)(2,1)S(1)}, u32[]{:S(2)}, u32[]{:S(2)}) collective-permute-start(bf16[128,768]{1,0:T(8,128)(2,1)S(1)} %convolution_convert_fusion.8), channel_id=1, source_target_pairs={{0,2},{1,3},{2,0},{3,1},{4,6},{5,7},{6,4},{7,5},{8,10},{9,11},{10,... | collective-permute-start | bytes 589832 | tf_op jit(solution)/shard_map/ppermute | solution.py:23
  105.0 16.9 %collective-permute-start.8 = (bf16[128,768]{1,0:T(8,128)(2,1)S(1)}, bf16[128,768]{1,0:T(8,128)(2,1)S(1)}, u32[]{:S(2)}, u32[]{:S(2)}) collective-permute-start(bf16[128,768]{1,0:T(8,128)(2,1)S(1)} %convolution_convert_fusion.9), channel_id=1, source_target_pairs={{0,1},{1,2},{2,3},{3,0},{4,5},{5,6},{6,7},{7,4},{8,9},{9,10},{10,1... | collective-permute-start | bytes 589832 | tf_op jit(solution)/shard_map/ppermute | solution.py:23
  107.4 0.8 copy-start.10
  109.0 35.1 %collective-permute-start.22 = (f32[64,640]{1,0:T(8,128)}, f32[64,640]{1,0:T(8,128)}, u32[]{:S(2)}, u32[]{:S(2)}) collective-permute-start(f32[64,640]{1,0:T(8,128)} %get-tuple-element.134), channel_id=1, source_target_pairs={{0,12},{1,13},{2,14},{3,15},{4,0},{5,1},{6,2},{7,3},{8,4},{9,5},{1... | collective-permute-start | bytes 491528 | tf_op jit(solution)/shard_map/ppermute | solution.py:23
  112.1 37.1 %collective-permute-start.21 = (f32[64,640]{1,0:T(8,128)}, f32[64,640]{1,0:T(8,128)}, u32[]{:S(2)}, u32[]{:S(2)}) collective-permute-start(f32[64,640]{1,0:T(8,128)} %get-tuple-element.135), channel_id=1, source_target_pairs={{0,8},{1,9},{2,10},{3,11},{4,12},{5,13},{6,14},{7,15},{8,0},{9,1},... | collective-permute-start | bytes 491528 | tf_op jit(solution)/shard_map/ppermute | solution.py:23
  114.8 12.0 %copy-start.19 = (f32[6,5]{1,0:T(8,128)S(1)}, f32[6,5]{1,0:T(8,128)}, u32[]{:S(2)}) copy-start(f32[6,5]{1,0:T(8,128)} %param.33) | copy-start | bytes 364
  114.8 37.5 %collective-permute-start.20 = (f32[64,640]{1,0:T(8,128)}, f32[64,640]{1,0:T(8,128)}, u32[]{:S(2)}, u32[]{:S(2)}) collective-permute-start(f32[64,640]{1,0:T(8,128)} %get-tuple-element.133), channel_id=1, source_target_pairs={{0,4},{1,5},{2,6},{3,7},{4,8},{5,9},{6,10},{7,11},{8,12},{9,13},{1... | collective-permute-start | bytes 491528 | tf_op jit(solution)/shard_map/ppermute | solution.py:23
  129.1 1.5 copy-start.3
  133.9 36.6 %collective-permute-start.31 = (bf16[128,640]{1,0:T(8,128)(2,1)}, bf16[128,640]{1,0:T(8,128)(2,1)}, u32[]{:S(2)}, u32[]{:S(2)}) collective-permute-start(bf16[128,640]{1,0:T(8,128)(2,1)} %bitcast.119), channel_id=1, source_target_pairs={{0,3},{1,0},{2,1},{3,2},{4,7},{5,4},{6,5},{7,6},{8,11},{9,8},{10,9... | collective-permute-start | bytes 491528 | tf_op jit(solution)/shard_map/ppermute | solution.py:23
  138.5 32.0 %collective-permute-start.30 = (bf16[128,640]{1,0:T(8,128)(2,1)}, bf16[128,640]{1,0:T(8,128)(2,1)}, u32[]{:S(2)}, u32[]{:S(2)}) collective-permute-start(bf16[128,640]{1,0:T(8,128)(2,1)} %bitcast.119), channel_id=1, source_target_pairs={{0,2},{1,3},{2,0},{3,1},{4,6},{5,7},{6,4},{7,5},{8,10},{9,11},{10,... | collective-permute-start | bytes 491528 | tf_op jit(solution)/shard_map/ppermute | solution.py:23
  143.4 25.3 %copy-start.1 = (f32[2,4,4,4,4,5,128]{6,1,5,4,3,2,0:T(4,128)S(1)}, f32[2,4,4,4,4,5,128]{6,1,5,4,3,2,0:T(4,128)}, u32[]{:S(2)}) copy-start(f32[2,4,4,4,4,5,128]{6,1,5,4,3,2,0:T(4,128)} %copy.126) | copy-start | bytes 3932164
  144.1 23.6 %collective-permute-start.13 = (bf16[1,4,80,128]{3,2,1,0:T(8,128)(2,1)}, bf16[1,4,80,128]{3,2,1,0:T(8,128)(2,1)}, u32[]{:S(2)}, u32[]{:S(2)}) collective-permute-start(bf16[1,4,80,128]{3,2,1,0:T(8,128)(2,1)} %get-tuple-element.141), channel_id=1, source_target_pairs={{0,16},{16,32},{32,48},{48,64},{64,80},{80,96},{96,112},{112,128},... | collective-permute-start | bytes 245768 | tf_op jit(solution)/shard_map/ppermute | solution.py:14
  149.2 9.9 %collective-permute-start.15 = (bf16[2,1,80,128]{3,2,1,0:T(8,128)(2,1)}, bf16[2,1,80,128]{3,2,1,0:T(8,128)(2,1)}, u32[]{:S(2)}, u32[]{:S(2)}) collective-permute-start(bf16[2,1,80,128]{3,2,1,0:T(8,128)(2,1)} %slice.608), channel_id=1, source_target_pairs={{0,1},{1,2},{2,3},{3,4},{4,5},{5,6},{6,7},{7,8},{8,9},{9,10},{10,1... | collective-permute-start | bytes 122888 | tf_op jit(solution)/shard_map/ppermute | solution.py:14
  152.3 12.0 %collective-permute-start.16 = (bf16[2,1,80,128]{3,2,1,0:T(8,128)(2,1)}, bf16[2,1,80,128]{3,2,1,0:T(8,128)(2,1)}, u32[]{:S(2)}, u32[]{:S(2)}) collective-permute-start(bf16[2,1,80,128]{3,2,1,0:T(8,128)(2,1)} %slice.613), channel_id=1, source_target_pairs={{1,0},{2,1},{3,2},{4,3},{5,4},{6,5},{7,6},{8,7},{9,8},{10,9},{11,1... | collective-permute-start | bytes 122888 | tf_op jit(solution)/shard_map/ppermute | solution.py:14
  157.1 13.2 %copy-start.14 = (bf16[1,4,1,80,128]{4,1,3,2,0:T(4,128)(2,1)S(1)}, bf16[1,4,1,80,128]{4,1,3,2,0:T(4,128)(2,1)}, u32[]{:S(2)}) copy-start(bf16[1,4,1,80,128]{4,1,3,2,0:T(4,128)(2,1)} %copy.60) | copy-start | bytes 245764
  159.1 11.4 %copy-start.22 = (s32[512]{0:T(512)S(1)}, s32[512]{0:T(512)}, u32[]{:S(2)}) copy-start(s32[512]{0:T(512)} %copy-done.21) | copy-start | bytes 6148
  159.1 11.4 %copy-start.24 = (s32[256]{0:T(256)S(1)}, s32[256]{0:T(256)}, u32[]{:S(2)}) copy-start(s32[256]{0:T(256)} %add.226) | copy-start | bytes 3076
  159.1 11.4 %collective-permute-start.29 = (bf16[128,640]{1,0:T(8,128)(2,1)}, bf16[128,640]{1,0:T(8,128)(2,1)S(1)}, u32[]{:S(2)}, u32[]{:S(2)}) collective-permute-start(bf16[128,640]{1,0:T(8,128)(2,1)} %bitcast.119), channel_id=1, source_target_pairs={{0,1},{1,2},{2,3},{3,0},{4,5},{5,6},{6,7},{7,4},{8,9},{9,10},{10,1... | collective-permute-start | bytes 491528 | tf_op jit(solution)/shard_map/ppermute | solution.py:23
  164.3 6.0 %collective-permute-start.14 = (bf16[1,4,80,128]{3,2,1,0:T(8,128)(2,1)}, bf16[1,4,80,128]{3,2,1,0:T(8,128)(2,1)S(1)}, u32[]{:S(2)}, u32[]{:S(2)}) collective-permute-start(bf16[1,4,80,128]{3,2,1,0:T(8,128)(2,1)} %get-tuple-element.139), channel_id=1, source_target_pairs={{16,0},{32,16},{48,32},{64,48},{80,64},{96,80},{112,96},{128,112},... | collective-permute-start | bytes 245768 | tf_op jit(solution)/shard_map/ppermute | solution.py:14
  170.5 25.1 %copy-start.8 = (bf16[2,3,4,1,4,5,128]{6,1,5,4,3,2,0:T(4,128)(2,1)S(1)}, bf16[2,3,4,1,4,5,128]{6,1,5,4,3,2,0:T(4,128)(2,1)}, u32[]{:S(2)}) copy-start(bf16[2,3,4,1,4,5,128]{6,1,5,4,3,2,0:T(4,128)(2,1)} %copy.65) | copy-start | bytes 368644
  172.1 35.3 %collective-permute-start.34 = (f32[64,640]{1,0:T(8,128)S(1)}, f32[64,640]{1,0:T(8,128)S(1)}, u32[]{:S(2)}, u32[]{:S(2)}) collective-permute-start(f32[64,640]{1,0:T(8,128)S(1)} %get-tuple-element.131), channel_id=1, source_target_pairs={{0,12},{1,13},{2,14},{3,15},{4,0},{5,1},{6,2},{7,3},{8,4},{9,5},{1... | collective-permute-start | bytes 491528 | tf_op jit(solution)/shard_map/ppermute | solution.py:23
  181.0 26.5 %collective-permute-start.33 = (f32[64,640]{1,0:T(8,128)S(1)}, f32[64,640]{1,0:T(8,128)S(1)}, u32[]{:S(2)}, u32[]{:S(2)}) collective-permute-start(f32[64,640]{1,0:T(8,128)S(1)} %get-tuple-element.132), channel_id=1, source_target_pairs={{0,8},{1,9},{2,10},{3,11},{4,12},{5,13},{6,14},{7,15},{8,0},{9,1},... | collective-permute-start | bytes 491528 | tf_op jit(solution)/shard_map/ppermute | solution.py:23
  189.7 25.3 %collective-permute-start.32 = (f32[64,640]{1,0:T(8,128)S(1)}, f32[64,640]{1,0:T(8,128)S(1)}, u32[]{:S(2)}, u32[]{:S(2)}) collective-permute-start(f32[64,640]{1,0:T(8,128)S(1)} %get-tuple-element.130), channel_id=1, source_target_pairs={{0,4},{1,5},{2,6},{3,7},{4,8},{5,9},{6,10},{7,11},{8,12},{9,13},{1... | collective-permute-start | bytes 491528 | tf_op jit(solution)/shard_map/ppermute | solution.py:23
  217.3 8.9 %copy-start.6 = (bf16[2,3,4,1,4,5,128]{6,1,5,4,3,2,0:T(4,128)(2,1)S(1)}, bf16[2,3,4,1,4,5,128]{6,1,5,4,3,2,0:T(4,128)(2,1)}, u32[]{:S(2)}) copy-start(bf16[2,3,4,1,4,5,128]{6,1,5,4,3,2,0:T(4,128)(2,1)} %copy.68) | copy-start | bytes 368644
  217.3 8.9 %copy-start.17 = (bf16[2,1,4,1,4,5,128]{6,1,5,4,3,2,0:T(2,128)(2,1)S(1)}, bf16[2,1,4,1,4,5,128]{6,1,5,4,3,2,0:T(2,128)(2,1)}, u32[]{:S(2)}) copy-start(bf16[2,1,4,1,4,5,128]{6,1,5,4,3,2,0:T(2,128)(2,1)} %copy.69) | copy-start | bytes 122884
  220.5 20.1 %collective-permute-start.23 = (bf16[64,768]{1,0:T(8,128)(2,1)S(1)}, bf16[64,768]{1,0:T(8,128)(2,1)S(1)}, u32[]{:S(2)}, u32[]{:S(2)}) collective-permute-start(bf16[64,768]{1,0:T(8,128)(2,1)S(1)} %get-tuple-element.127), channel_id=1, source_target_pairs={{0,4},{1,5},{2,6},{3,7},{4,8},{5,9},{6,10},{7,11},{8,12},{9,13},{1... | collective-permute-start | bytes 294920 | tf_op jit(solution)/shard_map/ppermute | solution.py:23
  226.5 16.8 %collective-permute-start.24 = (bf16[64,768]{1,0:T(8,128)(2,1)S(1)}, bf16[64,768]{1,0:T(8,128)(2,1)S(1)}, u32[]{:S(2)}, u32[]{:S(2)}) collective-permute-start(bf16[64,768]{1,0:T(8,128)(2,1)S(1)} %get-tuple-element.127), channel_id=1, source_target_pairs={{0,8},{1,9},{2,10},{3,11},{4,12},{5,13},{6,14},{7,15},{8,0},{9,1},... | collective-permute-start | bytes 294920 | tf_op jit(solution)/shard_map/ppermute | solution.py:23
  233.2 21.1 %collective-permute-start.25 = (bf16[64,768]{1,0:T(8,128)(2,1)S(1)}, bf16[64,768]{1,0:T(8,128)(2,1)S(1)}, u32[]{:S(2)}, u32[]{:S(2)}) collective-permute-start(bf16[64,768]{1,0:T(8,128)(2,1)S(1)} %get-tuple-element.127), channel_id=1, source_target_pairs={{0,12},{1,13},{2,14},{3,15},{4,0},{5,1},{6,2},{7,3},{8,4},{9,5},{1... | collective-permute-start | bytes 294920 | tf_op jit(solution)/shard_map/ppermute | solution.py:23
  255.3 10.6 %collective-permute-start.28 = (bf16[128,768]{1,0:T(8,128)(2,1)S(1)}, bf16[128,768]{1,0:T(8,128)(2,1)S(1)}, u32[]{:S(2)}, u32[]{:S(2)}) collective-permute-start(bf16[128,768]{1,0:T(8,128)(2,1)S(1)} %convolution_convert_fusion.3), channel_id=1, source_target_pairs={{0,3},{1,0},{2,1},{3,2},{4,7},{5,4},{6,5},{7,6},{8,11},{9,8},{10,9... | collective-permute-start | bytes 589832 | tf_op jit(solution)/shard_map/ppermute | solution.py:23
  259.2 9.1 %collective-permute-start.27 = (bf16[128,768]{1,0:T(8,128)(2,1)S(1)}, bf16[128,768]{1,0:T(8,128)(2,1)S(1)}, u32[]{:S(2)}, u32[]{:S(2)}) collective-permute-start(bf16[128,768]{1,0:T(8,128)(2,1)S(1)} %convolution_convert_fusion.4), channel_id=1, source_target_pairs={{0,2},{1,3},{2,0},{3,1},{4,6},{5,7},{6,4},{7,5},{8,10},{9,11},{10,... | collective-permute-start | bytes 589832 | tf_op jit(solution)/shard_map/ppermute | solution.py:23
  262.1 11.5 %collective-permute-start.26 = (bf16[128,768]{1,0:T(8,128)(2,1)S(1)}, bf16[128,768]{1,0:T(8,128)(2,1)S(1)}, u32[]{:S(2)}, u32[]{:S(2)}) collective-permute-start(bf16[128,768]{1,0:T(8,128)(2,1)S(1)} %convolution_convert_fusion.5), channel_id=1, source_target_pairs={{0,1},{1,2},{2,3},{3,0},{4,5},{5,6},{6,7},{7,4},{8,9},{9,10},{10,1... | collective-permute-start | bytes 589832 | tf_op jit(solution)/shard_map/ppermute | solution.py:23

commit v4 on v3

--- a/solution.py
+++ b/solution.py
@@ -88,10 +88,11 @@
     wall_count = wall_local.shape[0]
     node = lax.iota(jnp.int32, shell_count)
     kz = lax.iota(jnp.int32, cz)[:, None]
+    ky = lax.iota(jnp.int32, CY)[:, None]
     got_ids = ((((zpos - kz) % cz) * CY + ypos) * shell_count + node).reshape(-1)
-    out_ids = ((((zpos + kz) % cz) * CY + ypos) * shell_count + node).reshape(-1)
+    out_ids = ((zpos * CY + (ypos + ky) % CY) * shell_count + node).reshape(-1)
     maps_to = [wall_local] + [chord_shift(wall_local, 0, -k) for k in range(1, CY)]
-    maps_from = jnp.concatenate(over_y(wall_local))
+    maps_from = jnp.concatenate(over_z(wall_local))
     pick_hits = [(m[:, None] == got_ids[None, :]).astype(jnp.bfloat16) for m in maps_to]
     load_hit = (out_ids[:, None] == maps_from[None, :]).astype(jnp.bfloat16)
     fluid = jnp.einsum(
@@ -106,29 +107,38 @@
         sent = jnp.einsum("abdmn,abnr->abdmr", face_jac, fluid, preferred_element_type=jnp.float32)
         sent = (sent * weights).astype(jnp.bfloat16)
         low_span, high_span, low_chord, high_chord = face_terms(sent)
-        column = jnp.concatenate(over_z(shell.reshape(shell_count, sdof * width)))
-        served = [
-            jnp.dot(h, column, preferred_element_type=jnp.float32).astype(jnp.bfloat16)
-            for h in pick_hits
+        wall_rows = fluid.reshape(rows, cols, 4, 4, 4, NV, width)[:, :, :, :, 0].reshape(
+            wall_count * NV, width
+        )
+        shell_rows = shell.reshape(shell_count * sdof, width)
+        cut = shell_count * sdof
+        arrived = over_z(jnp.concatenate([shell_rows, wall_rows]))
+        column = jnp.concatenate(
+            [a[:cut].reshape(shell_count, sdof * width) for a in arrived]
+        )
+        row_group = jnp.concatenate(
+            [a[cut:].reshape(wall_count, NV * width) for a in arrived]
+        )
+        partial = jnp.dot(load_hit, row_group, preferred_element_type=jnp.float32)
+        partial = partial.reshape(CY, shell_count * NV, width)
+        packs = [
+            jnp.concatenate(
+                [
+                    jnp.dot(h, column, preferred_element_type=jnp.float32).reshape(
+                        wall_count * sdof, width
+                    ),
+                    partial[k],
+                ]
+            )
+            for k, h in enumerate(pick_hits)
         ]
-        picked = served[0].astype(jnp.float32)
+        total = packs[0]
         for k in range(1, CY):
-            picked = picked + chord_shift(served[k], 0, k).astype(jnp.float32)
-        wall_in = jnp.einsum(
-            "sv,wsr->wvr", couple, picked.reshape(wall_count, sdof, width), precision=high
-        )
-        wall_rows = fluid.reshape(rows, cols, 4, 4, 4, NV, width)[:, :, :, :, 0].reshape(
-            wall_count, NV * width
-        )
-        row_group = jnp.concatenate(over_y(wall_rows))
-        partial = jnp.dot(load_hit, row_group, preferred_element_type=jnp.float32)
-        partial = partial.reshape(cz, shell_count, NV * width)
-        summed = partial[0]
-        for k in range(1, cz):
-            summed = summed + chord_shift(partial[k], k, 0)
-        shell_load = jnp.einsum(
-            "sv,nvr->nsr", couple, summed.reshape(shell_count, NV, width), precision=high
-        )
+            total = total + chord_shift(packs[k], 0, k)
+        picked = total[: wall_count * sdof].reshape(wall_count, sdof, width)
+        summed = total[wall_count * sdof :].reshape(shell_count, NV, width)
+        wall_in = jnp.einsum("sv,wsr->wvr", couple, picked, precision=high)
+        shell_load = jnp.einsum("sv,nvr->nsr", couple, summed, precision=high)
         resid = assemble(adj_rhs, low_span, high_span, low_chord, high_chord, wall_in)
         fluid = jnp.einsum(
             "abmn,abnr->abmr", diag_inv, resid, preferred_element_type=jnp.float32

time: 284 us -> 343 us (1.21)
  the two profiles are of different devices: /device:TPU:1 before, /device:TPU:39 now
where the time goes in v4:
time: 343 us; the launch traced here: 339 us
  starting transfers between devices  140 us (41%)
  local copies, waits for them, and re-layouts  117 us (34%)
  matrix products  30.9 us (9%)
  waiting for transfers between devices  27.6 us (8%)
  other arithmetic  21.9 us (6%)
    ppermute x18, starting transfers between devices, chord_shift(): return lax.ppermute(block, 'chord', route)  119 us
    ppermute x18, waiting for transfers between devices, chord_shift(): return lax.ppermute(block, 'chord', route)  23.8 us
    ppermute x8, starting transfers between devices, passed_along(): return lax.ppermute(block, axis, route)  20.6 us
    unnamed x71, local copies, waits for them, and re-layouts  17.3 us
    dot_general x8, matrix products, per_device(): jnp.dot(h, column, preferred_element_type=jnp.float32)  16 us
    reshape x8, local copies, waits for them, and re-layouts, per_device(): jnp.dot(h, column, preferred_element_type=jnp.float32)  14.1 us
    squeeze x8, local copies, waits for them, and re-layouts, per_device(): partial[k]  12.7 us
    concatenate x6, other arithmetic, per_device(): jnp.concatenate([jnp.dot(h, column, preferred_element_type=jnp.float32).r...  11.6 us
  transfers between devices with their start and end apart: 26, of which 6 were waited for; matrix products, arithmetic and copies ran while one was open for 33% of the time, Pallas kernels for 0%

profile of v4, /device:TPU:39, one launch (start us, length us, event | category | flops | bytes accessed | tf_op | source)
XLA Modules:
  0.0 339.4 jit_solution(2324948454447725416)
XLA Ops:
  6.6 11.5 %collective-permute-start.6 = (bf16[1024,128]{1,0:T(8,128)(2,1)}, bf16[1024,128]{1,0:T(8,128)(2,1)}, u32[]{:S(2)}, u32[]{:S(2)}) collective-permute-start(bf16[1024,128]{1,0:T(8,128)(2,1)} %constant_dynamic-update-slice_fusion), channel_id=1, source_target_pairs={{0,12},{1,13},{2,14},{3,15},{4,0},{5,1},{6,2},{7,3},{8,4},{9,5},{1... | collective-permute-start | bytes 786440 | tf_op jit(solution)/shard_map/ppermute | solution.py:23
  18.2 4.9 %collective-permute-start.5 = (bf16[1024,128]{1,0:T(8,128)(2,1)}, bf16[1024,128]{1,0:T(8,128)(2,1)}, u32[]{:S(2)}, u32[]{:S(2)}) collective-permute-start(bf16[1024,128]{1,0:T(8,128)(2,1)} %constant_dynamic-update-slice_fusion), channel_id=1, source_target_pairs={{0,8},{1,9},{2,10},{3,11},{4,12},{5,13},{6,14},{7,15},{8,0},{9,1},... | collective-permute-start | bytes 786440 | tf_op jit(solution)/shard_map/ppermute | solution.py:23
  23.2 2.3 collective-permute-start.9
  25.5 12.1 %collective-permute-start.8 = (s32[128]{0:T(128)S(1)}, s32[128]{0:T(128)}, u32[]{:S(2)}, u32[]{:S(2)}) collective-permute-start(s32[128]{0:T(128)S(1)} %eq.31), channel_id=1, source_target_pairs={{0,8},{1,9},{2,10},{3,11},{4,12},{5,13},{6,14},{7,15},{8,0},{9,1},... | collective-permute-start | bytes 1544 | tf_op jit(solution)/shard_map/ppermute | solution.py:23
  37.6 4.0 %collective-permute-start.7 = (s32[128]{0:T(128)S(1)}, s32[128]{0:T(128)}, u32[]{:S(2)}, u32[]{:S(2)}) collective-permute-start(s32[128]{0:T(128)S(1)} %eq.31), channel_id=1, source_target_pairs={{0,4},{1,5},{2,6},{3,7},{4,8},{5,9},{6,10},{7,11},{8,12},{9,13},{1... | collective-permute-start | bytes 1544 | tf_op jit(solution)/shard_map/ppermute | solution.py:23
  43.3 1.7 fusion.4
  57.4 4.6 %collective-permute-done.9 = s32[128]{0:T(128)} collective-permute-done((s32[128]{0:T(128)S(1)}, s32[128]{0:T(128)}, u32[]{:S(2)}, u32[]{:S(2)}) %collective-permute-start.9) | collective-permute-done | bytes 544 | tf_op jit(solution)/shard_map/ppermute | solution.py:23
  62.0 1.9 collective-permute-start
  63.9 3.0 collective-permute-done.8
  66.9 3.2 collective-permute-start.2
  72.1 10.5 %collective-permute-start.4 = (bf16[1024,128]{1,0:T(8,128)(2,1)}, bf16[1024,128]{1,0:T(8,128)(2,1)}, u32[]{:S(2)}, u32[]{:S(2)}) collective-permute-start(bf16[1024,128]{1,0:T(8,128)(2,1)} %constant_dynamic-update-slice_fusion), channel_id=1, source_target_pairs={{0,4},{1,5},{2,6},{3,7},{4,8},{5,9},{6,10},{7,11},{8,12},{9,13},{1... | collective-permute-start | bytes 786440 | tf_op jit(solution)/shard_map/ppermute | solution.py:23
  83.4 1.9 collective-permute-start.14
  86.0 4.4 %collective-permute-start.1 = (bf16[1,4,80,128]{3,2,1,0:T(8,128)(2,1)}, bf16[1,4,80,128]{3,2,1,0:T(8,128)(2,1)S(1)}, u32[]{:S(2)}, u32[]{:S(2)}) collective-permute-start(bf16[1,4,80,128]{3,2,1,0:T(8,128)(2,1)} %get-tuple-element.143), channel_id=1, source_target_pairs={{16,0},{32,16},{48,32},{64,48},{80,64},{96,80},{112,96},{128,112},... | collective-permute-start | bytes 245768 | tf_op jit(solution)/shard_map/ppermute | solution.py:14
  92.4 4.5 %collective-permute-start.12 = (s32[128]{0:T(128)S(1)}, s32[128]{0:T(128)}, u32[]{:S(2)}, u32[]{:S(2)}) collective-permute-start(s32[128]{0:T(128)S(1)} %eq.31), channel_id=1, source_target_pairs={{0,2},{1,3},{2,0},{3,1},{4,6},{5,7},{6,4},{7,5},{8,10},{9,11},{10,... | collective-permute-start | bytes 1544 | tf_op jit(solution)/shard_map/ppermute | solution.py:23
  97.2 1.9 collective-permute-start.10
  100.7 1.7 reshape.938
  104.0 1.7 reshape.937
  107.3 1.7 reshape.936
  127.1 2.0 fusion.48
  129.1 1.8 reshape.941
  130.9 1.9 pad_maximum_fusion.2
  132.8 2.5 collective-permute-start.15
  136.9 2.0 fusion.52
  138.9 1.8 reshape.940
  140.7 1.9 pad_maximum_fusion.1
  142.6 4.5 %collective-permute-start.13 = (f32[1088,128]{1,0:T(8,128)}, f32[1088,128]{1,0:T(8,128)}, u32[]{:S(2)}, u32[]{:S(2)}) collective-permute-start(f32[1088,128]{1,0:T(8,128)} %pad_maximum_fusion.1), channel_id=1, source_target_pairs={{0,2},{1,3},{2,0},{3,1},{4,6},{5,7},{6,4},{7,5},{8,10},{9,11},{10,... | collective-permute-start | bytes 1671176 | tf_op jit(solution)/shard_map/ppermute | solution.py:23
  148.8 2.0 fusion.56
  150.7 1.8 reshape.939
  152.5 1.9 pad_maximum_fusion
  154.5 2.1 collective-permute-start.11
  159.9 2.0 fusion.60
  161.9 1.8 reshape.935
  163.7 8.1 %collective-permute-done.11 = f32[1088,128]{1,0:T(8,128)} collective-permute-done((f32[1088,128]{1,0:T(8,128)}, f32[1088,128]{1,0:T(8,128)}, u32[]{:S(2)}, u32[]{:S(2)}) %collective-permute-start.11) | collective-permute-done | bytes 557088 | tf_op jit(solution)/shard_map/ppermute | solution.py:23
  171.8 1.6 fusion.29
  175.0 1.9 reshape.942
  176.9 1.7 convolution_negate_fusion.1
  187.3 3.1 collective-permute-start.22
  190.5 7.7 %collective-permute-start.21 = (bf16[1024,128]{1,0:T(8,128)(2,1)}, bf16[1024,128]{1,0:T(8,128)(2,1)}, u32[]{:S(2)}, u32[]{:S(2)}) collective-permute-start(bf16[1024,128]{1,0:T(8,128)(2,1)} %constant_dynamic-update-slice_fusion.5), channel_id=1, source_target_pairs={{0,8},{1,9},{2,10},{3,11},{4,12},{5,13},{6,14},{7,15},{8,0},{9,1},... | collective-permute-start | bytes 786440 | tf_op jit(solution)/shard_map/ppermute | solution.py:23
  198.2 4.0 %collective-permute-start.16 = (bf16[1,4,80,128]{3,2,1,0:T(8,128)(2,1)}, bf16[1,4,80,128]{3,2,1,0:T(8,128)(2,1)S(1)}, u32[]{:S(2)}, u32[]{:S(2)}) collective-permute-start(bf16[1,4,80,128]{3,2,1,0:T(8,128)(2,1)} %get-tuple-element.135), channel_id=1, source_target_pairs={{0,16},{16,32},{32,48},{48,64},{64,80},{80,96},{96,112},{112,128},... | collective-permute-start | bytes 245768 | tf_op jit(solution)/shard_map/ppermute | solution.py:14
  203.0 2.7 collective-permute-start.18
  213.8 38.3 %collective-permute-start.20 = (bf16[1024,128]{1,0:T(8,128)(2,1)}, bf16[1024,128]{1,0:T(8,128)(2,1)}, u32[]{:S(2)}, u32[]{:S(2)}) collective-permute-start(bf16[1024,128]{1,0:T(8,128)(2,1)} %constant_dynamic-update-slice_fusion.5), channel_id=1, source_target_pairs={{0,4},{1,5},{2,6},{3,7},{4,8},{5,9},{6,10},{7,11},{8,12},{9,13},{1... | collective-permute-start | bytes 786440 | tf_op jit(solution)/shard_map/ppermute | solution.py:23
  252.8 1.9 collective-permute-start.17
  255.7 2.9 collective-permute-done.17
  260.2 1.7 reshape.952
  263.5 1.7 reshape.951
  266.8 1.7 reshape.950
  286.6 2.0 fusion.46
  288.6 1.8 reshape.955
  290.4 1.9 pad_maximum_fusion.5
  292.3 1.9 collective-permute-start.25
  295.8 2.0 fusion.50
  297.8 1.8 reshape.954
  299.6 1.9 pad_maximum_fusion.4
  301.5 1.9 collective-permute-start.24
  305.0 2.0 fusion.54
  307.0 1.8 reshape.953
  308.8 2.0 pad_maximum_fusion.3
  310.7 3.6 %collective-permute-start.23 = (f32[1088,128]{1,0:T(8,128)}, f32[1088,128]{1,0:T(8,128)}, u32[]{:S(2)}, u32[]{:S(2)}) collective-permute-start(f32[1088,128]{1,0:T(8,128)} %pad_maximum_fusion.3), channel_id=1, source_target_pairs={{0,1},{1,2},{2,3},{3,0},{4,5},{5,6},{6,7},{7,4},{8,9},{9,10},{10,1... | collective-permute-start | bytes 1671176 | tf_op jit(solution)/shard_map/ppermute | solution.py:23
  317.6 2.0 fusion.58
  319.6 1.8 reshape.949
  321.4 8.0 %collective-permute-done.23 = f32[1088,128]{1,0:T(8,128)} collective-permute-done((f32[1088,128]{1,0:T(8,128)}, f32[1088,128]{1,0:T(8,128)}, u32[]{:S(2)}, u32[]{:S(2)}) %collective-permute-start.23) | collective-permute-done | bytes 557088 | tf_op jit(solution)/shard_map/ppermute | solution.py:23
  329.4 1.6 fusion.31
  332.0 1.8 reshape.956
  333.8 1.7 convolution_negate_fusion
  (214 shorter events, 109.8 us)
Async XLA Ops:
  0.6 3.0 copy-start
  0.6 3.0 copy-start.5
  3.0 1.4 copy-start.12
  4.4 0.8 copy-start.4
  5.2 17.9 %copy-start.25 = (s32[2,4,16]{2,1,0:T(4,128)S(1)}, s32[2,4,16]{2,1,0:T(4,128)}, u32[]{:S(2)}) copy-start(s32[2,4,16]{2,1,0:T(4,128)} %param.32) | copy-start | bytes 1540
  5.8 31.8 %copy-start.6 = (bf16[2,4,4,4,1,5,128]{6,5,3,2,1,0,4:T(8,128)(2,1)}, bf16[2,4,4,4,1,5,128]{6,5,3,2,1,0,4:T(8,128)(2,1)S(1)}, u32[]{:S(2)}) copy-start(bf16[2,4,4,4,1,5,128]{6,5,3,2,1,0,4:T(8,128)(2,1)S(1)} %copy.54) | copy-start | bytes 491524
  5.8 37.4 %copy-start.26 = (s32[2,4,4]{2,1,0:T(4,128)S(1)}, s32[2,4,4]{2,1,0:T(4,128)}, u32[]{:S(2)}) copy-start(s32[2,4,4]{2,1,0:T(4,128)} %param.31) | copy-start | bytes 388
  6.6 90.5 %collective-permute-start.6 = (bf16[1024,128]{1,0:T(8,128)(2,1)}, bf16[1024,128]{1,0:T(8,128)(2,1)}, u32[]{:S(2)}, u32[]{:S(2)}) collective-permute-start(bf16[1024,128]{1,0:T(8,128)(2,1)} %constant_dynamic-update-slice_fusion), channel_id=1, source_target_pairs={{0,12},{1,13},{2,14},{3,15},{4,0},{5,1},{6,2},{7,3},{8,4},{9,5},{1... | collective-permute-start | bytes 786440 | tf_op jit(solution)/shard_map/ppermute | solution.py:23
  18.2 84.2 %collective-permute-start.5 = (bf16[1024,128]{1,0:T(8,128)(2,1)}, bf16[1024,128]{1,0:T(8,128)(2,1)}, u32[]{:S(2)}, u32[]{:S(2)}) collective-permute-start(bf16[1024,128]{1,0:T(8,128)(2,1)} %constant_dynamic-update-slice_fusion), channel_id=1, source_target_pairs={{0,8},{1,9},{2,10},{3,11},{4,12},{5,13},{6,14},{7,15},{8,0},{9,1},... | collective-permute-start | bytes 786440 | tf_op jit(solution)/shard_map/ppermute | solution.py:23
  23.2 20.1 %copy-start.2 = (bf16[2,4,4,80,320]{4,3,2,1,0:T(8,128)(2,1)S(1)}, bf16[2,4,4,80,320]{4,3,2,1,0:T(8,128)(2,1)}, u32[]{:S(2)}) copy-start(bf16[2,4,4,80,320]{4,3,2,1,0:T(8,128)(2,1)} %param.30) | copy-start | bytes 4915204
  23.2 38.8 %collective-permute-start.9 = (s32[128]{0:T(128)S(1)}, s32[128]{0:T(128)}, u32[]{:S(2)}, u32[]{:S(2)}) collective-permute-start(s32[128]{0:T(128)S(1)} %eq.31), channel_id=1, source_target_pairs={{0,12},{1,13},{2,14},{3,15},{4,0},{5,1},{6,2},{7,3},{8,4},{9,5},{1... | collective-permute-start | bytes 1544 | tf_op jit(solution)/shard_map/ppermute | solution.py:23
  25.5 41.4 %collective-permute-start.8 = (s32[128]{0:T(128)S(1)}, s32[128]{0:T(128)}, u32[]{:S(2)}, u32[]{:S(2)}) collective-permute-start(s32[128]{0:T(128)S(1)} %eq.31), channel_id=1, source_target_pairs={{0,8},{1,9},{2,10},{3,11},{4,12},{5,13},{6,14},{7,15},{8,0},{9,1},... | collective-permute-start | bytes 1544 | tf_op jit(solution)/shard_map/ppermute | solution.py:23
  37.6 32.5 %collective-permute-start.7 = (s32[128]{0:T(128)S(1)}, s32[128]{0:T(128)}, u32[]{:S(2)}, u32[]{:S(2)}) collective-permute-start(s32[128]{0:T(128)S(1)} %eq.31), channel_id=1, source_target_pairs={{0,4},{1,5},{2,6},{3,7},{4,8},{5,9},{6,10},{7,11},{8,12},{9,13},{1... | collective-permute-start | bytes 1544 | tf_op jit(solution)/shard_map/ppermute | solution.py:23
  48.3 1.1 copy-start.19
  48.3 1.8 copy-start.18
  50.7 5.2 %copy-start.7 = (bf16[2,4,4,4,1,5,128]{6,5,3,2,1,0,4:T(8,128)(2,1)S(1)}, bf16[2,4,4,4,1,5,128]{6,5,3,2,1,0,4:T(8,128)(2,1)}, u32[]{:S(2)}) copy-start(bf16[2,4,4,4,1,5,128]{6,5,3,2,1,0,4:T(8,128)(2,1)} %copy-done.6) | copy-start | bytes 491524
  57.4 39.6 %copy-start.17 = (bf16[1,4,1,80,128]{4,1,3,2,0:T(4,128)(2,1)S(1)}, bf16[1,4,1,80,128]{4,1,3,2,0:T(4,128)(2,1)}, u32[]{:S(2)}) copy-start(bf16[1,4,1,80,128]{4,1,3,2,0:T(4,128)(2,1)} %copy.41) | copy-start | bytes 245764
  62.0 24.0 %collective-permute-start = (bf16[1,4,80,128]{3,2,1,0:T(8,128)(2,1)}, bf16[1,4,80,128]{3,2,1,0:T(8,128)(2,1)S(1)}, u32[]{:S(2)}, u32[]{:S(2)}) collective-permute-start(bf16[1,4,80,128]{3,2,1,0:T(8,128)(2,1)} %get-tuple-element.145), channel_id=1, source_target_pairs={{0,16},{16,32},{32,48},{48,64},{64,80},{80,96},{96,112},{112,128},... | collective-permute-start | bytes 245768 | tf_op jit(solution)/shard_map/ppermute | solution.py:14
  66.9 5.2 %collective-permute-start.2 = (bf16[2,1,80,128]{3,2,1,0:T(8,128)(2,1)}, bf16[2,1,80,128]{3,2,1,0:T(8,128)(2,1)S(1)}, u32[]{:S(2)}, u32[]{:S(2)}) collective-permute-start(bf16[2,1,80,128]{3,2,1,0:T(8,128)(2,1)} %slice.658), channel_id=1, source_target_pairs={{0,1},{1,2},{2,3},{3,4},{4,5},{5,6},{6,7},{7,8},{8,9},{9,10},{10,1... | collective-permute-start | bytes 122888 | tf_op jit(solution)/shard_map/ppermute | solution.py:14
  70.1 13.2 %collective-permute-start.3 = (bf16[2,1,80,128]{3,2,1,0:T(8,128)(2,1)}, bf16[2,1,80,128]{3,2,1,0:T(8,128)(2,1)S(1)}, u32[]{:S(2)}, u32[]{:S(2)}) collective-permute-start(bf16[2,1,80,128]{3,2,1,0:T(8,128)(2,1)} %slice.663), channel_id=1, source_target_pairs={{1,0},{2,1},{3,2},{4,3},{5,4},{6,5},{7,6},{8,7},{9,8},{10,9},{11,1... | collective-permute-start | bytes 122888 | tf_op jit(solution)/shard_map/ppermute | solution.py:14
  72.1 36.9 %copy-start.27 = (s32[512]{0:T(512)}, s32[512]{0:T(512)S(1)}, u32[]{:S(2)}) copy-start(s32[512]{0:T(512)S(1)} %pad_add_fusion) | copy-start | bytes 6148
  72.1 33.6 %collective-permute-start.4 = (bf16[1024,128]{1,0:T(8,128)(2,1)}, bf16[1024,128]{1,0:T(8,128)(2,1)}, u32[]{:S(2)}, u32[]{:S(2)}) collective-permute-start(bf16[1024,128]{1,0:T(8,128)(2,1)} %constant_dynamic-update-slice_fusion), channel_id=1, source_target_pairs={{0,4},{1,5},{2,6},{3,7},{4,8},{5,9},{6,10},{7,11},{8,12},{9,13},{1... | collective-permute-start | bytes 786440 | tf_op jit(solution)/shard_map/ppermute | solution.py:23
  83.4 43.7 %collective-permute-start.14 = (s32[128]{0:T(128)S(1)}, s32[128]{0:T(128)}, u32[]{:S(2)}, u32[]{:S(2)}) collective-permute-start(s32[128]{0:T(128)S(1)} %eq.31), channel_id=1, source_target_pairs={{0,1},{1,2},{2,3},{3,0},{4,5},{5,6},{6,7},{7,4},{8,9},{9,10},{10,1... | collective-permute-start | bytes 1544 | tf_op jit(solution)/shard_map/ppermute | solution.py:23
  86.0 6.4 %collective-permute-start.1 = (bf16[1,4,80,128]{3,2,1,0:T(8,128)(2,1)}, bf16[1,4,80,128]{3,2,1,0:T(8,128)(2,1)S(1)}, u32[]{:S(2)}, u32[]{:S(2)}) collective-permute-start(bf16[1,4,80,128]{3,2,1,0:T(8,128)(2,1)} %get-tuple-element.143), channel_id=1, source_target_pairs={{16,0},{32,16},{48,32},{64,48},{80,64},{96,80},{112,96},{128,112},... | collective-permute-start | bytes 245768 | tf_op jit(solution)/shard_map/ppermute | solution.py:14
  92.4 44.5 %collective-permute-start.12 = (s32[128]{0:T(128)S(1)}, s32[128]{0:T(128)}, u32[]{:S(2)}, u32[]{:S(2)}) collective-permute-start(s32[128]{0:T(128)S(1)} %eq.31), channel_id=1, source_target_pairs={{0,2},{1,3},{2,0},{3,1},{4,6},{5,7},{6,4},{7,5},{8,10},{9,11},{10,... | collective-permute-start | bytes 1544 | tf_op jit(solution)/shard_map/ppermute | solution.py:23
  97.2 51.6 %collective-permute-start.10 = (s32[128]{0:T(128)S(1)}, s32[128]{0:T(128)}, u32[]{:S(2)}, u32[]{:S(2)}) collective-permute-start(s32[128]{0:T(128)S(1)} %eq.31), channel_id=1, source_target_pairs={{0,3},{1,0},{2,1},{3,2},{4,7},{5,4},{6,5},{7,6},{8,11},{9,8},{10,9... | collective-permute-start | bytes 1544 | tf_op jit(solution)/shard_map/ppermute | solution.py:23
  132.8 30.8 %collective-permute-start.15 = (f32[1088,128]{1,0:T(8,128)}, f32[1088,128]{1,0:T(8,128)}, u32[]{:S(2)}, u32[]{:S(2)}) collective-permute-start(f32[1088,128]{1,0:T(8,128)} %pad_maximum_fusion.2), channel_id=1, source_target_pairs={{0,3},{1,0},{2,1},{3,2},{4,7},{5,4},{6,5},{7,6},{8,11},{9,8},{10,9... | collective-permute-start | bytes 1671176 | tf_op jit(solution)/shard_map/ppermute | solution.py:23
  142.6 21.0 %collective-permute-start.13 = (f32[1088,128]{1,0:T(8,128)}, f32[1088,128]{1,0:T(8,128)}, u32[]{:S(2)}, u32[]{:S(2)}) collective-permute-start(f32[1088,128]{1,0:T(8,128)} %pad_maximum_fusion.1), channel_id=1, source_target_pairs={{0,2},{1,3},{2,0},{3,1},{4,6},{5,7},{6,4},{7,5},{8,10},{9,11},{10,... | collective-permute-start | bytes 1671176 | tf_op jit(solution)/shard_map/ppermute | solution.py:23
  152.5 5.4 %copy-start.15 = (bf16[2,3,4,1,4,5,128]{6,1,5,4,3,2,0:T(4,128)(2,1)S(1)}, bf16[2,3,4,1,4,5,128]{6,1,5,4,3,2,0:T(4,128)(2,1)}, u32[]{:S(2)}) copy-start(bf16[2,3,4,1,4,5,128]{6,1,5,4,3,2,0:T(4,128)(2,1)} %copy.49) | copy-start | bytes 368644
  152.5 5.4 %copy-start.20 = (bf16[2,1,4,1,4,5,128]{6,1,5,4,3,2,0:T(2,128)(2,1)S(1)}, bf16[2,1,4,1,4,5,128]{6,1,5,4,3,2,0:T(2,128)(2,1)}, u32[]{:S(2)}) copy-start(bf16[2,1,4,1,4,5,128]{6,1,5,4,3,2,0:T(2,128)(2,1)} %copy.50) | copy-start | bytes 122884
  154.5 17.3 %collective-permute-start.11 = (f32[1088,128]{1,0:T(8,128)}, f32[1088,128]{1,0:T(8,128)}, u32[]{:S(2)}, u32[]{:S(2)}) collective-permute-start(f32[1088,128]{1,0:T(8,128)} %pad_maximum_fusion), channel_id=1, source_target_pairs={{0,1},{1,2},{2,3},{3,0},{4,5},{5,6},{6,7},{7,4},{8,9},{9,10},{10,1... | collective-permute-start | bytes 1671176 | tf_op jit(solution)/shard_map/ppermute | solution.py:23
  173.4 0.8 copy-start.10
  174.3 2.7 copy-start.24
  179.2 1.5 copy-start.3
  181.4 2.7 slice-start
  181.4 3.1 copy-start.13
  186.5 20.4 %copy-start.8 = (bf16[2,4,4,4,1,5,128]{6,5,3,2,1,0,4:T(8,128)(2,1)}, bf16[2,4,4,4,1,5,128]{6,5,3,2,1,0,4:T(8,128)(2,1)S(1)}, u32[]{:S(2)}) copy-start(bf16[2,4,4,4,1,5,128]{6,5,3,2,1,0,4:T(8,128)(2,1)S(1)} %copy.74) | copy-start | bytes 491524
  187.3 65.5 %copy-start.23 = (bf16[1,4,80,128]{3,2,1,0:T(8,128)(2,1)S(1)}, bf16[1,4,80,128]{3,2,1,0:T(8,128)(2,1)}, u32[]{:S(2)}) copy-start(bf16[1,4,80,128]{3,2,1,0:T(8,128)(2,1)} %get-tuple-element.133) | copy-start | bytes 245764
  187.3 71.5 %collective-permute-start.22 = (bf16[1024,128]{1,0:T(8,128)(2,1)}, bf16[1024,128]{1,0:T(8,128)(2,1)S(1)}, u32[]{:S(2)}, u32[]{:S(2)}) collective-permute-start(bf16[1024,128]{1,0:T(8,128)(2,1)} %constant_dynamic-update-slice_fusion.5), channel_id=1, source_target_pairs={{0,12},{1,13},{2,14},{3,15},{4,0},{5,1},{6,2},{7,3},{8,4},{9,5},{1... | collective-permute-start | bytes 786440 | tf_op jit(solution)/shard_map/ppermute | solution.py:23
  190.5 71.4 %collective-permute-start.21 = (bf16[1024,128]{1,0:T(8,128)(2,1)}, bf16[1024,128]{1,0:T(8,128)(2,1)}, u32[]{:S(2)}, u32[]{:S(2)}) collective-permute-start(bf16[1024,128]{1,0:T(8,128)(2,1)} %constant_dynamic-update-slice_fusion.5), channel_id=1, source_target_pairs={{0,8},{1,9},{2,10},{3,11},{4,12},{5,13},{6,14},{7,15},{8,0},{9,1},... | collective-permute-start | bytes 786440 | tf_op jit(solution)/shard_map/ppermute | solution.py:23
  198.2 57.3 %collective-permute-start.16 = (bf16[1,4,80,128]{3,2,1,0:T(8,128)(2,1)}, bf16[1,4,80,128]{3,2,1,0:T(8,128)(2,1)S(1)}, u32[]{:S(2)}, u32[]{:S(2)}) collective-permute-start(bf16[1,4,80,128]{3,2,1,0:T(8,128)(2,1)} %get-tuple-element.135), channel_id=1, source_target_pairs={{0,16},{16,32},{32,48},{48,64},{64,80},{80,96},{96,112},{112,128},... | collective-permute-start | bytes 245768 | tf_op jit(solution)/shard_map/ppermute | solution.py:14
  203.0 10.8 %collective-permute-start.18 = (bf16[2,1,80,128]{3,2,1,0:T(8,128)(2,1)S(1)}, bf16[2,1,80,128]{3,2,1,0:T(8,128)(2,1)S(1)}, u32[]{:S(2)}, u32[]{:S(2)}) collective-permute-start(bf16[2,1,80,128]{3,2,1,0:T(8,128)(2,1)S(1)} %slice.684), channel_id=1, source_target_pairs={{0,1},{1,2},{2,3},{3,4},{4,5},{5,6},{6,7},{7,8},{8,9},{9,10},{10,1... | collective-permute-start | bytes 122888 | tf_op jit(solution)/shard_map/ppermute | solution.py:14
  205.6 47.2 %collective-permute-start.19 = (bf16[2,1,80,128]{3,2,1,0:T(8,128)(2,1)}, bf16[2,1,80,128]{3,2,1,0:T(8,128)(2,1)S(1)}, u32[]{:S(2)}, u32[]{:S(2)}) collective-permute-start(bf16[2,1,80,128]{3,2,1,0:T(8,128)(2,1)} %slice.689), channel_id=1, source_target_pairs={{1,0},{2,1},{3,2},{4,3},{5,4},{6,5},{7,6},{8,7},{9,8},{10,9},{11,1... | collective-permute-start | bytes 122888 | tf_op jit(solution)/shard_map/ppermute | solution.py:14
  207.6 5.5 %copy-start.9 = (bf16[2,4,4,4,1,5,128]{6,5,3,2,1,0,4:T(8,128)(2,1)S(1)}, bf16[2,4,4,4,1,5,128]{6,5,3,2,1,0,4:T(8,128)(2,1)}, u32[]{:S(2)}) copy-start(bf16[2,4,4,4,1,5,128]{6,5,3,2,1,0,4:T(8,128)(2,1)} %copy-done.8) | copy-start | bytes 491524
  207.6 47.9 %copy-start.1 = (f32[2,4,4,4,4,5,128]{6,1,5,4,3,2,0:T(4,128)S(1)}, f32[2,4,4,4,4,5,128]{6,1,5,4,3,2,0:T(4,128)}, u32[]{:S(2)}) copy-start(f32[2,4,4,4,4,5,128]{6,1,5,4,3,2,0:T(4,128)} %copy.123) | copy-start | bytes 3932164
  213.8 51.4 %collective-permute-start.20 = (bf16[1024,128]{1,0:T(8,128)(2,1)}, bf16[1024,128]{1,0:T(8,128)(2,1)}, u32[]{:S(2)}, u32[]{:S(2)}) collective-permute-start(bf16[1024,128]{1,0:T(8,128)(2,1)} %constant_dynamic-update-slice_fusion.5), channel_id=1, source_target_pairs={{0,4},{1,5},{2,6},{3,7},{4,8},{5,9},{6,10},{7,11},{8,12},{9,13},{1... | collective-permute-start | bytes 786440 | tf_op jit(solution)/shard_map/ppermute | solution.py:23
  252.8 5.7 %collective-permute-start.17 = (bf16[1,4,80,128]{3,2,1,0:T(8,128)(2,1)S(1)}, bf16[1,4,80,128]{3,2,1,0:T(8,128)(2,1)S(1)}, u32[]{:S(2)}, u32[]{:S(2)}) collective-permute-start(bf16[1,4,80,128]{3,2,1,0:T(8,128)(2,1)S(1)} %copy-done.23), channel_id=1, source_target_pairs={{16,0},{32,16},{48,32},{64,48},{80,64},{96,80},{112,96},{128,112},... | collective-permute-start | bytes 245768 | tf_op jit(solution)/shard_map/ppermute | solution.py:14
  258.6 9.8 %copy-start.28 = (s32[512]{0:T(512)S(1)}, s32[512]{0:T(512)}, u32[]{:S(2)}) copy-start(s32[512]{0:T(512)} %copy-done.27) | copy-start | bytes 6148
  258.8 0.7 copy-start.22
  292.3 29.1 %collective-permute-start.25 = (f32[1088,128]{1,0:T(8,128)}, f32[1088,128]{1,0:T(8,128)}, u32[]{:S(2)}, u32[]{:S(2)}) collective-permute-start(f32[1088,128]{1,0:T(8,128)} %pad_maximum_fusion.5), channel_id=1, source_target_pairs={{0,3},{1,0},{2,1},{3,2},{4,7},{5,4},{6,5},{7,6},{8,11},{9,8},{10,9... | collective-permute-start | bytes 1671176 | tf_op jit(solution)/shard_map/ppermute | solution.py:23
  301.5 19.9 %collective-permute-start.24 = (f32[1088,128]{1,0:T(8,128)}, f32[1088,128]{1,0:T(8,128)}, u32[]{:S(2)}, u32[]{:S(2)}) collective-permute-start(f32[1088,128]{1,0:T(8,128)} %pad_maximum_fusion.4), channel_id=1, source_target_pairs={{0,2},{1,3},{2,0},{3,1},{4,6},{5,7},{6,4},{7,5},{8,10},{9,11},{10,... | collective-permute-start | bytes 1671176 | tf_op jit(solution)/shard_map/ppermute | solution.py:23
  308.8 6.9 %copy-start.16 = (bf16[2,3,4,1,4,5,128]{6,1,5,4,3,2,0:T(4,128)(2,1)S(1)}, bf16[2,3,4,1,4,5,128]{6,1,5,4,3,2,0:T(4,128)(2,1)}, u32[]{:S(2)}) copy-start(bf16[2,3,4,1,4,5,128]{6,1,5,4,3,2,0:T(4,128)(2,1)} %copy.69) | copy-start | bytes 368644
  308.8 6.9 %copy-start.21 = (bf16[2,1,4,1,4,5,128]{6,1,5,4,3,2,0:T(2,128)(2,1)S(1)}, bf16[2,1,4,1,4,5,128]{6,1,5,4,3,2,0:T(2,128)(2,1)}, u32[]{:S(2)}) copy-start(bf16[2,1,4,1,4,5,128]{6,1,5,4,3,2,0:T(2,128)(2,1)} %copy.70) | copy-start | bytes 122884
  310.7 18.6 %collective-permute-start.23 = (f32[1088,128]{1,0:T(8,128)}, f32[1088,128]{1,0:T(8,128)}, u32[]{:S(2)}, u32[]{:S(2)}) collective-permute-start(f32[1088,128]{1,0:T(8,128)} %pad_maximum_fusion.3), channel_id=1, source_target_pairs={{0,1},{1,2},{2,3},{3,0},{4,5},{5,6},{6,7},{7,4},{8,9},{9,10},{10,1... | collective-permute-start | bytes 1671176 | tf_op jit(solution)/shard_map/ppermute | solution.py:23
  331.0 1.0 copy-start.11
  336.1 1.5 slice-start.1
  336.1 1.9 copy-start.14

commit v5 on v3

--- a/solution.py
+++ b/solution.py
@@ -87,13 +87,24 @@
     wall_local = wall_map.reshape(-1)
     wall_count = wall_local.shape[0]
     node = lax.iota(jnp.int32, shell_count)
-    kz = lax.iota(jnp.int32, cz)[:, None]
-    got_ids = ((((zpos - kz) % cz) * CY + ypos) * shell_count + node).reshape(-1)
-    out_ids = ((((zpos + kz) % cz) * CY + ypos) * shell_count + node).reshape(-1)
+    none_s = jnp.full((shell_count,), -1, jnp.int32)
+    none_w = jnp.full((wall_count,), -1, jnp.int32)
+    held = over_z(wall_local)
+    col_s = jnp.concatenate(
+        [
+            jnp.concatenate([(((zpos - k) % cz) * CY + ypos) * shell_count + node, none_w])
+            for k in range(cz)
+        ]
+    )
+    col_w = jnp.concatenate([jnp.concatenate([none_s, held[k]]) for k in range(cz)])
     maps_to = [wall_local] + [chord_shift(wall_local, 0, -k) for k in range(1, CY)]
-    maps_from = jnp.concatenate(over_y(wall_local))
-    pick_hits = [(m[:, None] == got_ids[None, :]).astype(jnp.bfloat16) for m in maps_to]
-    load_hit = (out_ids[:, None] == maps_from[None, :]).astype(jnp.bfloat16)
+    hits = []
+    for k in range(CY):
+        want_s = jnp.concatenate([maps_to[k], none_s - 1])
+        owner = (zpos * CY + (ypos + k) % CY) * shell_count + node
+        want_w = jnp.concatenate([none_w - 1, owner])
+        hit = (want_s[:, None] == col_s[None, :]) | (want_w[:, None] == col_w[None, :])
+        hits.append(hit.astype(jnp.bfloat16))
     fluid = jnp.einsum(
         "abmn,abnr->abmr", diag_inv, adj_rhs, preferred_element_type=jnp.float32
     ).astype(jnp.bfloat16)
@@ -106,29 +117,20 @@
         sent = jnp.einsum("abdmn,abnr->abdmr", face_jac, fluid, preferred_element_type=jnp.float32)
         sent = (sent * weights).astype(jnp.bfloat16)
         low_span, high_span, low_chord, high_chord = face_terms(sent)
-        column = jnp.concatenate(over_z(shell.reshape(shell_count, sdof * width)))
-        served = [
-            jnp.dot(h, column, preferred_element_type=jnp.float32).astype(jnp.bfloat16)
-            for h in pick_hits
-        ]
-        picked = served[0].astype(jnp.float32)
-        for k in range(1, CY):
-            picked = picked + chord_shift(served[k], 0, k).astype(jnp.float32)
-        wall_in = jnp.einsum(
-            "sv,wsr->wvr", couple, picked.reshape(wall_count, sdof, width), precision=high
-        )
         wall_rows = fluid.reshape(rows, cols, 4, 4, 4, NV, width)[:, :, :, :, 0].reshape(
             wall_count, NV * width
         )
-        row_group = jnp.concatenate(over_y(wall_rows))
-        partial = jnp.dot(load_hit, row_group, preferred_element_type=jnp.float32)
-        partial = partial.reshape(cz, shell_count, NV * width)
-        summed = partial[0]
-        for k in range(1, cz):
-            summed = summed + chord_shift(partial[k], k, 0)
-        shell_load = jnp.einsum(
-            "sv,nvr->nsr", couple, summed.reshape(shell_count, NV, width), precision=high
-        )
+        wall_rows = jnp.pad(wall_rows, ((0, 0), (0, (sdof - NV) * width)))
+        block = jnp.concatenate([shell.reshape(shell_count, sdof * width), wall_rows])
+        column = jnp.concatenate(over_z(block))
+        served = [jnp.dot(h, column, preferred_element_type=jnp.float32) for h in hits]
+        total = served[0]
+        for k in range(1, CY):
+            total = total + chord_shift(served[k], 0, k)
+        picked = total[:wall_count].reshape(wall_count, sdof, width)
+        summed = total[wall_count:, : NV * width].reshape(shell_count, NV, width)
+        wall_in = jnp.einsum("sv,wsr->wvr", couple, picked, precision=high)
+        shell_load = jnp.einsum("sv,nvr->nsr", couple, summed, precision=high)
         resid = assemble(adj_rhs, low_span, high_span, low_chord, high_chord, wall_in)
         fluid = jnp.einsum(
             "abmn,abnr->abmr", diag_inv, resid, preferred_element_type=jnp.float32

time: 284 us -> 323 us (1.14)
  the two profiles are of different devices: /device:TPU:1 before, /device:TPU:100 now
where the time goes in v5:
time: 323 us; the launch traced here: 321 us
  starting transfers between devices  151 us (47%)
  waiting for transfers between devices  95.7 us (30%)
  local copies, waits for them, and re-layouts  42.6 us (13%)
  matrix products  21.9 us (7%)
  other arithmetic  7.11 us (2%)
    ppermute x18, starting transfers between devices, chord_shift(): return lax.ppermute(block, 'chord', route)  135 us
    ppermute x8, waiting for transfers between devices, passed_along(): return lax.ppermute(block, axis, route)  51.2 us
    ppermute x18, waiting for transfers between devices, chord_shift(): return lax.ppermute(block, 'chord', route)  44.5 us
    ppermute x8, starting transfers between devices, passed_along(): return lax.ppermute(block, axis, route)  16.3 us
    unnamed x95, local copies, waits for them, and re-layouts  8.88 us
    dot_general x8, matrix products, per_device(): jnp.dot(h, column, preferred_element_type=jnp.float32)  8.63 us
  transfers between devices with their start and end apart: 26, of which 8 were waited for; matrix products, arithmetic and copies ran while one was open for 13% of the time, Pallas kernels for 0%

profile of v5, /device:TPU:100, one launch (start us, length us, event | category | flops | bytes accessed | tf_op | source)
XLA Modules:
  0.0 320.7 jit_solution(6146463438321810014)
XLA Ops:
  0.6 1.4 reshape.777
  2.1 9.1 %collective-permute-start.4 = (s32[128]{0:T(128)}, s32[128]{0:T(128)S(1)}, u32[]{:S(2)}, u32[]{:S(2)}) collective-permute-start(s32[128]{0:T(128)} %reshape.777), channel_id=1, source_target_pairs={{0,4},{1,5},{2,6},{3,7},{4,8},{5,9},{6,10},{7,11},{8,12},{9,13},{1... | collective-permute-start | bytes 1544 | tf_op jit(solution)/shard_map/ppermute | solution.py:23
  11.2 8.2 %collective-permute-start.5 = (s32[128]{0:T(128)}, s32[128]{0:T(128)S(1)}, u32[]{:S(2)}, u32[]{:S(2)}) collective-permute-start(s32[128]{0:T(128)} %reshape.777), channel_id=1, source_target_pairs={{0,8},{1,9},{2,10},{3,11},{4,12},{5,13},{6,14},{7,15},{8,0},{9,1},... | collective-permute-start | bytes 1544 | tf_op jit(solution)/shard_map/ppermute | solution.py:23
  19.4 4.9 %collective-permute-start.10 = (s32[128]{0:T(128)}, s32[128]{0:T(128)S(1)}, u32[]{:S(2)}, u32[]{:S(2)}) collective-permute-start(s32[128]{0:T(128)} %reshape.777), channel_id=1, source_target_pairs={{0,3},{1,0},{2,1},{3,2},{4,7},{5,4},{6,5},{7,6},{8,11},{9,8},{10,9... | collective-permute-start | bytes 1544 | tf_op jit(solution)/shard_map/ppermute | solution.py:23
  24.3 2.5 collective-permute-start.12
  26.9 0.9 copy.51
  27.8 1.3 convolution_convert_fusion.5
  29.7 1.7 convolution_convert_fusion.2
  33.6 1.9 collective-permute-start.7
  35.6 2.2 fusion.4
  42.2 1.9 collective-permute-start
  44.1 3.5 %collective-permute-start.2 = (bf16[2,1,80,128]{3,2,1,0:T(8,128)(2,1)}, bf16[2,1,80,128]{3,2,1,0:T(8,128)(2,1)}, u32[]{:S(2)}, u32[]{:S(2)}) collective-permute-start(bf16[2,1,80,128]{3,2,1,0:T(8,128)(2,1)} %slice.570), channel_id=1, source_target_pairs={{0,1},{1,2},{2,3},{3,4},{4,5},{5,6},{6,7},{7,8},{8,9},{9,10},{10,1... | collective-permute-start | bytes 122888 | tf_op jit(solution)/shard_map/ppermute | solution.py:14
  47.6 1.3 collective-permute-start.3
  49.6 1.6 copy.38
  53.7 4.5 %collective-permute-start.14 = (s32[128]{0:T(128)}, s32[128]{0:T(128)S(1)}, u32[]{:S(2)}, u32[]{:S(2)}) collective-permute-start(s32[128]{0:T(128)} %reshape.777), channel_id=1, source_target_pairs={{0,1},{1,2},{2,3},{3,0},{4,5},{5,6},{6,7},{7,4},{8,9},{9,10},{10,1... | collective-permute-start | bytes 1544 | tf_op jit(solution)/shard_map/ppermute | solution.py:23
  58.9 1.1 copy.127
  61.6 2.5 collective-permute-done.14
  64.0 11.4 %collective-permute-start.6 = (s32[128]{0:T(128)}, s32[128]{0:T(128)}, u32[]{:S(2)}, u32[]{:S(2)}) collective-permute-start(s32[128]{0:T(128)} %reshape.777), channel_id=1, source_target_pairs={{0,12},{1,13},{2,14},{3,15},{4,0},{5,1},{6,2},{7,3},{8,4},{9,5},{1... | collective-permute-start | bytes 1544 | tf_op jit(solution)/shard_map/ppermute | solution.py:23
  77.0 1.2 concatenate.186
  78.2 1.1 concatenate.188
  79.3 1.3 concatenate.190
  80.6 7.4 %collective-permute-start.8 = (bf16[192,768]{1,0:T(8,128)(2,1)}, bf16[192,768]{1,0:T(8,128)(2,1)}, u32[]{:S(2)}, u32[]{:S(2)}) collective-permute-start(bf16[192,768]{1,0:T(8,128)(2,1)} %pad_maximum_fusion), channel_id=1, source_target_pairs={{0,8},{1,9},{2,10},{3,11},{4,12},{5,13},{6,14},{7,15},{8,0},{9,1},... | collective-permute-start | bytes 884744 | tf_op jit(solution)/shard_map/ppermute | solution.py:23
  88.5 0.8 concatenate.183
  89.3 3.3 %collective-permute-start.9 = (bf16[192,768]{1,0:T(8,128)(2,1)}, bf16[192,768]{1,0:T(8,128)(2,1)S(1)}, u32[]{:S(2)}, u32[]{:S(2)}) collective-permute-start(bf16[192,768]{1,0:T(8,128)(2,1)} %pad_maximum_fusion), channel_id=1, source_target_pairs={{0,12},{1,13},{2,14},{3,15},{4,0},{5,1},{6,2},{7,3},{8,4},{9,5},{1... | collective-permute-start | bytes 884744 | tf_op jit(solution)/shard_map/ppermute | solution.py:23
  92.7 0.8 copy.43
  93.6 1.9 collective-permute-start.1
  95.5 0.8 copy.48
  96.4 0.9 copy.39
  97.3 1.0 add_dynamic-update-slice_fusion.1
  98.4 35.1 %collective-permute-done.1 = bf16[1,4,80,128]{3,2,1,0:T(8,128)(2,1)S(1)} collective-permute-done((bf16[1,4,80,128]{3,2,1,0:T(8,128)(2,1)}, bf16[1,4,80,128]{3,2,1,0:T(8,128)(2,1)S(1)}, u32[]{:S(2)}, u32[]{:S(2)}) %collective-permute-start.1) | collective-permute-done | bytes 81952 | tf_op jit(solution)/shard_map/ppermute | solution.py:14
  133.5 1.7 constant_dynamic-update-slice_fusion.2
  135.3 1.7 constant_dynamic-update-slice_fusion.1
  137.7 1.7 fusion.15
  139.4 1.9 collective-permute-start.11
  141.4 1.7 fusion.17
  143.1 6.2 %collective-permute-start.13 = (f32[192,768]{1,0:T(8,128)S(1)}, f32[192,768]{1,0:T(8,128)S(1)}, u32[]{:S(2)}, u32[]{:S(2)}) collective-permute-start(f32[192,768]{1,0:T(8,128)S(1)} %fusion.17), channel_id=1, source_target_pairs={{0,2},{1,3},{2,0},{3,1},{4,6},{5,7},{6,4},{7,5},{8,10},{9,11},{10,... | collective-permute-start | bytes 1769480 | tf_op jit(solution)/shard_map/ppermute | solution.py:23
  149.3 1.7 fusion.19
  151.0 2.1 collective-permute-start.15
  154.0 3.8 %collective-permute-done.11 = f32[192,768]{1,0:T(8,128)S(1)} collective-permute-done((f32[192,768]{1,0:T(8,128)S(1)}, f32[192,768]{1,0:T(8,128)S(1)}, u32[]{:S(2)}, u32[]{:S(2)}) %collective-permute-start.11) | collective-permute-done | bytes 589856 | tf_op jit(solution)/shard_map/ppermute | solution.py:23
  157.7 12.4 %collective-permute-done.13 = f32[192,768]{1,0:T(8,128)S(1)} collective-permute-done((f32[192,768]{1,0:T(8,128)S(1)}, f32[192,768]{1,0:T(8,128)S(1)}, u32[]{:S(2)}, u32[]{:S(2)}) %collective-permute-start.13) | collective-permute-done | bytes 589856 | tf_op jit(solution)/shard_map/ppermute | solution.py:23
  170.1 3.5 %collective-permute-done.15 = f32[192,768]{1,0:T(8,128)S(1)} collective-permute-done((f32[192,768]{1,0:T(8,128)S(1)}, f32[192,768]{1,0:T(8,128)S(1)}, u32[]{:S(2)}, u32[]{:S(2)}) %collective-permute-start.15) | collective-permute-done | bytes 589856 | tf_op jit(solution)/shard_map/ppermute | solution.py:23
  173.6 1.7 fusion.6
  176.8 1.9 copy.55
  178.7 2.0 copy.56
  180.7 1.7 convolution_negate_fusion.1
  183.7 0.9 copy-done.2
  187.8 2.8 collective-permute-start.20
  190.6 1.9 collective-permute-start.16
  192.6 2.5 collective-permute-start.18
  195.1 1.3 collective-permute-start.19
  196.4 17.3 %collective-permute-start.21 = (bf16[192,768]{1,0:T(8,128)(2,1)S(1)}, bf16[192,768]{1,0:T(8,128)(2,1)S(1)}, u32[]{:S(2)}, u32[]{:S(2)}) collective-permute-start(bf16[192,768]{1,0:T(8,128)(2,1)S(1)} %pad_maximum_fusion.1), channel_id=1, source_target_pairs={{0,8},{1,9},{2,10},{3,11},{4,12},{5,13},{6,14},{7,15},{8,0},{9,1},... | collective-permute-start | bytes 884744 | tf_op jit(solution)/shard_map/ppermute | solution.py:23
  214.2 42.4 %collective-permute-start.22 = (bf16[192,768]{1,0:T(8,128)(2,1)S(1)}, bf16[192,768]{1,0:T(8,128)(2,1)S(1)}, u32[]{:S(2)}, u32[]{:S(2)}) collective-permute-start(bf16[192,768]{1,0:T(8,128)(2,1)S(1)} %pad_maximum_fusion.1), channel_id=1, source_target_pairs={{0,12},{1,13},{2,14},{3,15},{4,0},{5,1},{6,2},{7,3},{8,4},{9,5},{1... | collective-permute-start | bytes 884744 | tf_op jit(solution)/shard_map/ppermute | solution.py:23
  256.7 1.9 collective-permute-start.17
  259.0 16.1 %collective-permute-done.17 = bf16[1,4,80,128]{3,2,1,0:T(8,128)(2,1)S(1)} collective-permute-done((bf16[1,4,80,128]{3,2,1,0:T(8,128)(2,1)S(1)}, bf16[1,4,80,128]{3,2,1,0:T(8,128)(2,1)S(1)}, u32[]{:S(2)}, u32[]{:S(2)}) %collective-permute-start.17) | collective-permute-done | bytes 81952 | tf_op jit(solution)/shard_map/ppermute | solution.py:14
  277.0 1.9 collective-permute-start.23
  278.9 1.9 collective-permute-start.24
  280.8 5.4 %collective-permute-start.25 = (f32[192,768]{1,0:T(8,128)S(1)}, f32[192,768]{1,0:T(8,128)S(1)}, u32[]{:S(2)}, u32[]{:S(2)}) collective-permute-start(f32[192,768]{1,0:T(8,128)S(1)} %fusion.18), channel_id=1, source_target_pairs={{0,3},{1,0},{2,1},{3,2},{4,7},{5,4},{6,5},{7,6},{8,11},{9,8},{10,9... | collective-permute-start | bytes 1769480 | tf_op jit(solution)/shard_map/ppermute | solution.py:23
  287.0 19.8 %collective-permute-done.23 = f32[192,768]{1,0:T(8,128)S(1)} collective-permute-done((f32[192,768]{1,0:T(8,128)S(1)}, f32[192,768]{1,0:T(8,128)S(1)}, u32[]{:S(2)}, u32[]{:S(2)}) %collective-permute-start.23) | collective-permute-done | bytes 589856 | tf_op jit(solution)/shard_map/ppermute | solution.py:23
  306.8 2.5 collective-permute-done.25
  309.8 0.8 slice.595
  311.3 1.9 copy.76
  313.2 2.0 copy.77
  315.2 1.7 convolution_negate_fusion
  317.5 1.5 fusion.2
  (196 shorter events, 28.9 us)
Async XLA Ops:
  0.6 29.1 %copy-start = (bf16[2,4,320,320]{3,2,1,0:T(8,128)(2,1)S(1)}, bf16[2,4,320,320]{3,2,1,0:T(8,128)(2,1)}, u32[]{:S(2)}) copy-start(bf16[2,4,320,320]{3,2,1,0:T(8,128)(2,1)} %param.29) | copy-start | bytes 4915204
  2.1 40.1 %collective-permute-start.4 = (s32[128]{0:T(128)}, s32[128]{0:T(128)S(1)}, u32[]{:S(2)}, u32[]{:S(2)}) collective-permute-start(s32[128]{0:T(128)} %reshape.777), channel_id=1, source_target_pairs={{0,4},{1,5},{2,6},{3,7},{4,8},{5,9},{6,10},{7,11},{8,12},{9,13},{1... | collective-permute-start | bytes 1544 | tf_op jit(solution)/shard_map/ppermute | solution.py:23
  11.2 33.0 %collective-permute-start.5 = (s32[128]{0:T(128)}, s32[128]{0:T(128)S(1)}, u32[]{:S(2)}, u32[]{:S(2)}) collective-permute-start(s32[128]{0:T(128)} %reshape.777), channel_id=1, source_target_pairs={{0,8},{1,9},{2,10},{3,11},{4,12},{5,13},{6,14},{7,15},{8,0},{9,1},... | collective-permute-start | bytes 1544 | tf_op jit(solution)/shard_map/ppermute | solution.py:23
  19.4 28.2 %collective-permute-start.10 = (s32[128]{0:T(128)}, s32[128]{0:T(128)S(1)}, u32[]{:S(2)}, u32[]{:S(2)}) collective-permute-start(s32[128]{0:T(128)} %reshape.777), channel_id=1, source_target_pairs={{0,3},{1,0},{2,1},{3,2},{4,7},{5,4},{6,5},{7,6},{8,11},{9,8},{10,9... | collective-permute-start | bytes 1544 | tf_op jit(solution)/shard_map/ppermute | solution.py:23
  24.3 29.3 %collective-permute-start.12 = (s32[128]{0:T(128)}, s32[128]{0:T(128)S(1)}, u32[]{:S(2)}, u32[]{:S(2)}) collective-permute-start(s32[128]{0:T(128)} %reshape.777), channel_id=1, source_target_pairs={{0,2},{1,3},{2,0},{3,1},{4,6},{5,7},{6,4},{7,5},{8,10},{9,11},{10,... | collective-permute-start | bytes 1544 | tf_op jit(solution)/shard_map/ppermute | solution.py:23
  32.0 3.7 %copy-start.34 = (s32[2,4,4]{2,1,0:T(4,128)S(1)}, s32[2,4,4]{2,1,0:T(4,128)}, u32[]{:S(2)}) copy-start(s32[2,4,4]{2,1,0:T(4,128)} %param.31) | copy-start | bytes 388
  33.6 100.0 %collective-permute-start.7 = (bf16[192,768]{1,0:T(8,128)(2,1)}, bf16[192,768]{1,0:T(8,128)(2,1)}, u32[]{:S(2)}, u32[]{:S(2)}) collective-permute-start(bf16[192,768]{1,0:T(8,128)(2,1)} %pad_maximum_fusion), channel_id=1, source_target_pairs={{0,4},{1,5},{2,6},{3,7},{4,8},{5,9},{6,10},{7,11},{8,12},{9,13},{1... | collective-permute-start | bytes 884744 | tf_op jit(solution)/shard_map/ppermute | solution.py:23
  38.6 10.4 %copy-start.5 = (bf16[2,4,80,128]{3,2,1,0:T(8,128)(2,1)}, bf16[2,4,80,128]{3,2,1,0:T(8,128)(2,1)S(1)}, u32[]{:S(2)}) copy-start(bf16[2,4,80,128]{3,2,1,0:T(8,128)(2,1)S(1)} %get-tuple-element.136) | copy-start | bytes 491524
  38.6 10.4 %copy-start.7 = (bf16[2,4,80,128]{3,2,1,0:T(8,128)(2,1)}, bf16[2,4,80,128]{3,2,1,0:T(8,128)(2,1)S(1)}, u32[]{:S(2)}) copy-start(bf16[2,4,80,128]{3,2,1,0:T(8,128)(2,1)S(1)} %get-tuple-element.137) | copy-start | bytes 491524
  40.9 11.0 %copy-start.39 = (s32[64]{0:T(128)S(1)}, s32[64]{0:T(128)}, u32[]{:S(2)}) copy-start(s32[64]{0:T(128)} %iota_add_fusion.1) | copy-start | bytes 772
  41.0 11.5 %copy-start.40 = (s32[64]{0:T(128)S(1)}, s32[64]{0:T(128)}, u32[]{:S(2)}) copy-start(s32[64]{0:T(128)} %iota_add_fusion) | copy-start | bytes 772
  41.0 17.2 %copy-start.15 = (bf16[1,4,1,80,128]{4,3,2,1,0:T(8,128)(2,1)S(1)}, bf16[1,4,1,80,128]{4,3,2,1,0:T(8,128)(2,1)}, u32[]{:S(2)}) copy-start(bf16[1,4,1,80,128]{4,3,2,1,0:T(8,128)(2,1)} %get-tuple-element.140) | copy-start | bytes 245764
  42.2 6.8 %copy-start.35 = (s32[128]{0:T(128)}, s32[128]{0:T(128)S(1)}, u32[]{:S(2)}) copy-start(s32[128]{0:T(128)S(1)} %collective-permute-done.4) | copy-start | bytes 1540
  42.2 54.2 %collective-permute-start = (bf16[1,4,80,128]{3,2,1,0:T(8,128)(2,1)}, bf16[1,4,80,128]{3,2,1,0:T(8,128)(2,1)}, u32[]{:S(2)}, u32[]{:S(2)}) collective-permute-start(bf16[1,4,80,128]{3,2,1,0:T(8,128)(2,1)} %get-tuple-element.141), channel_id=1, source_target_pairs={{0,16},{16,32},{32,48},{48,64},{64,80},{80,96},{96,112},{112,128},... | collective-permute-start | bytes 245768 | tf_op jit(solution)/shard_map/ppermute | solution.py:14
  44.1 4.8 %copy-start.36 = (s32[128]{0:T(128)}, s32[128]{0:T(128)S(1)}, u32[]{:S(2)}) copy-start(s32[128]{0:T(128)S(1)} %collective-permute-done.5) | copy-start | bytes 1540
  44.1 45.2 %collective-permute-start.2 = (bf16[2,1,80,128]{3,2,1,0:T(8,128)(2,1)}, bf16[2,1,80,128]{3,2,1,0:T(8,128)(2,1)}, u32[]{:S(2)}, u32[]{:S(2)}) collective-permute-start(bf16[2,1,80,128]{3,2,1,0:T(8,128)(2,1)} %slice.570), channel_id=1, source_target_pairs={{0,1},{1,2},{2,3},{3,4},{4,5},{5,6},{6,7},{7,8},{8,9},{9,10},{10,1... | collective-permute-start | bytes 122888 | tf_op jit(solution)/shard_map/ppermute | solution.py:14
  47.6 1.3 copy-start.37
  47.6 45.9 %collective-permute-start.3 = (bf16[2,1,80,128]{3,2,1,0:T(8,128)(2,1)}, bf16[2,1,80,128]{3,2,1,0:T(8,128)(2,1)}, u32[]{:S(2)}, u32[]{:S(2)}) collective-permute-start(bf16[2,1,80,128]{3,2,1,0:T(8,128)(2,1)} %slice.575), channel_id=1, source_target_pairs={{1,0},{2,1},{3,2},{4,3},{5,4},{6,5},{7,6},{8,7},{9,8},{10,9},{11,1... | collective-permute-start | bytes 122888 | tf_op jit(solution)/shard_map/ppermute | solution.py:14
  49.6 124.0 %copy-start.18 = (s32[192]{0:T(256)}, s32[192]{0:T(256)S(1)}, u32[]{:S(2)}) copy-start(s32[192]{0:T(256)S(1)} %concatenate.180) | copy-start | bytes 2308
  49.6 1.7 copy-start.8
  49.6 1.7 copy-start.6
  53.6 6.3 %copy-start.38 = (s32[128]{0:T(128)}, s32[128]{0:T(128)S(1)}, u32[]{:S(2)}) copy-start(s32[128]{0:T(128)S(1)} %collective-permute-done.12) | copy-start | bytes 1540
  53.7 10.4 %collective-permute-start.14 = (s32[128]{0:T(128)}, s32[128]{0:T(128)S(1)}, u32[]{:S(2)}, u32[]{:S(2)}) collective-permute-start(s32[128]{0:T(128)} %reshape.777), channel_id=1, source_target_pairs={{0,1},{1,2},{2,3},{3,0},{4,5},{5,6},{6,7},{7,4},{8,9},{9,10},{10,1... | collective-permute-start | bytes 1544 | tf_op jit(solution)/shard_map/ppermute | solution.py:23
  58.9 1.1 copy-start.14
  64.0 12.2 %copy-start.41 = (s32[128]{0:T(128)}, s32[128]{0:T(128)S(1)}, u32[]{:S(2)}) copy-start(s32[128]{0:T(128)S(1)} %collective-permute-done.14) | copy-start | bytes 1540
  64.0 16.5 %collective-permute-start.6 = (s32[128]{0:T(128)}, s32[128]{0:T(128)}, u32[]{:S(2)}, u32[]{:S(2)}) collective-permute-start(s32[128]{0:T(128)} %reshape.777), channel_id=1, source_target_pairs={{0,12},{1,13},{2,14},{3,15},{4,0},{5,1},{6,2},{7,3},{8,4},{9,5},{1... | collective-permute-start | bytes 1544 | tf_op jit(solution)/shard_map/ppermute | solution.py:23
  80.6 54.7 %collective-permute-start.8 = (bf16[192,768]{1,0:T(8,128)(2,1)}, bf16[192,768]{1,0:T(8,128)(2,1)}, u32[]{:S(2)}, u32[]{:S(2)}) collective-permute-start(bf16[192,768]{1,0:T(8,128)(2,1)} %pad_maximum_fusion), channel_id=1, source_target_pairs={{0,8},{1,9},{2,10},{3,11},{4,12},{5,13},{6,14},{7,15},{8,0},{9,1},... | collective-permute-start | bytes 884744 | tf_op jit(solution)/shard_map/ppermute | solution.py:23
  89.3 47.6 %collective-permute-start.9 = (bf16[192,768]{1,0:T(8,128)(2,1)}, bf16[192,768]{1,0:T(8,128)(2,1)S(1)}, u32[]{:S(2)}, u32[]{:S(2)}) collective-permute-start(bf16[192,768]{1,0:T(8,128)(2,1)} %pad_maximum_fusion), channel_id=1, source_target_pairs={{0,12},{1,13},{2,14},{3,15},{4,0},{5,1},{6,2},{7,3},{8,4},{9,5},{1... | collective-permute-start | bytes 884744 | tf_op jit(solution)/shard_map/ppermute | solution.py:23
  93.6 39.9 %collective-permute-start.1 = (bf16[1,4,80,128]{3,2,1,0:T(8,128)(2,1)}, bf16[1,4,80,128]{3,2,1,0:T(8,128)(2,1)S(1)}, u32[]{:S(2)}, u32[]{:S(2)}) collective-permute-start(bf16[1,4,80,128]{3,2,1,0:T(8,128)(2,1)} %get-tuple-element.139), channel_id=1, source_target_pairs={{16,0},{32,16},{48,32},{64,48},{80,64},{96,80},{112,96},{128,112},... | collective-permute-start | bytes 245768 | tf_op jit(solution)/shard_map/ppermute | solution.py:14
  97.3 40.4 %copy-start.26 = (s32[192]{0:T(256)S(1)}, s32[192]{0:T(256)}, u32[]{:S(2)}) copy-start(s32[192]{0:T(256)} %concatenate.187) | copy-start | bytes 2308
  97.3 40.4 %copy-start.32 = (s32[192]{0:T(256)S(1)}, s32[192]{0:T(256)}, u32[]{:S(2)}) copy-start(s32[192]{0:T(256)} %concatenate.186) | copy-start | bytes 2308
  136.9 4.4 %copy-start.24 = (s32[192]{0:T(256)S(1)}, s32[192]{0:T(256)}, u32[]{:S(2)}) copy-start(s32[192]{0:T(256)} %concatenate.189) | copy-start | bytes 2308
  137.0 4.4 %copy-start.30 = (s32[192]{0:T(256)S(1)}, s32[192]{0:T(256)}, u32[]{:S(2)}) copy-start(s32[192]{0:T(256)} %concatenate.188) | copy-start | bytes 2308
  139.4 9.9 %copy-start.22 = (s32[192]{0:T(256)S(1)}, s32[192]{0:T(256)}, u32[]{:S(2)}) copy-start(s32[192]{0:T(256)} %concatenate.191) | copy-start | bytes 2308
  139.4 9.9 %copy-start.28 = (s32[192]{0:T(256)S(1)}, s32[192]{0:T(256)}, u32[]{:S(2)}) copy-start(s32[192]{0:T(256)} %concatenate.190) | copy-start | bytes 2308
  139.4 18.3 %collective-permute-start.11 = (f32[192,768]{1,0:T(8,128)S(1)}, f32[192,768]{1,0:T(8,128)S(1)}, u32[]{:S(2)}, u32[]{:S(2)}) collective-permute-start(f32[192,768]{1,0:T(8,128)S(1)} %fusion.15), channel_id=1, source_target_pairs={{0,1},{1,2},{2,3},{3,0},{4,5},{5,6},{6,7},{7,4},{8,9},{9,10},{10,1... | collective-permute-start | bytes 1769480 | tf_op jit(solution)/shard_map/ppermute | solution.py:23
  143.1 10.1 %copy-start.16 = (bf16[1,4,1,80,128]{4,1,3,2,0:T(4,128)(2,1)S(1)}, bf16[1,4,1,80,128]{4,1,3,2,0:T(4,128)(2,1)}, u32[]{:S(2)}) copy-start(bf16[1,4,1,80,128]{4,1,3,2,0:T(4,128)(2,1)} %copy.41) | copy-start | bytes 245764
  143.1 10.2 %copy-start.9 = (bf16[2,3,4,1,4,5,128]{6,1,5,4,3,2,0:T(4,128)(2,1)S(1)}, bf16[2,3,4,1,4,5,128]{6,1,5,4,3,2,0:T(4,128)(2,1)}, u32[]{:S(2)}) copy-start(bf16[2,3,4,1,4,5,128]{6,1,5,4,3,2,0:T(4,128)(2,1)} %copy.46) | copy-start | bytes 368644
  143.1 10.5 %copy-start.10 = (bf16[2,3,4,1,4,5,128]{6,1,5,4,3,2,0:T(4,128)(2,1)S(1)}, bf16[2,3,4,1,4,5,128]{6,1,5,4,3,2,0:T(4,128)(2,1)}, u32[]{:S(2)}) copy-start(bf16[2,3,4,1,4,5,128]{6,1,5,4,3,2,0:T(4,128)(2,1)} %copy.49) | copy-start | bytes 368644
  143.1 27.0 %collective-permute-start.13 = (f32[192,768]{1,0:T(8,128)S(1)}, f32[192,768]{1,0:T(8,128)S(1)}, u32[]{:S(2)}, u32[]{:S(2)}) collective-permute-start(f32[192,768]{1,0:T(8,128)S(1)} %fusion.17), channel_id=1, source_target_pairs={{0,2},{1,3},{2,0},{3,1},{4,6},{5,7},{6,4},{7,5},{8,10},{9,11},{10,... | collective-permute-start | bytes 1769480 | tf_op jit(solution)/shard_map/ppermute | solution.py:23
  151.0 22.6 %collective-permute-start.15 = (f32[192,768]{1,0:T(8,128)S(1)}, f32[192,768]{1,0:T(8,128)S(1)}, u32[]{:S(2)}, u32[]{:S(2)}) collective-permute-start(f32[192,768]{1,0:T(8,128)S(1)} %fusion.19), channel_id=1, source_target_pairs={{0,3},{1,0},{2,1},{3,2},{4,7},{5,4},{6,5},{7,6},{8,11},{9,8},{10,9... | collective-permute-start | bytes 1769480 | tf_op jit(solution)/shard_map/ppermute | solution.py:23
  153.2 20.5 %copy-start.20 = (s32[192]{0:T(256)S(1)}, s32[192]{0:T(256)}, u32[]{:S(2)}) copy-start(s32[192]{0:T(256)} %concatenate.182) | copy-start | bytes 2308
  175.3 5.4 %copy-start.17 = (f32[6,5]{1,0:T(8,128)S(1)}, f32[6,5]{1,0:T(8,128)}, u32[]{:S(2)}) copy-start(f32[6,5]{1,0:T(8,128)} %param.33) | copy-start | bytes 364
  183.0 1.5 copy-start.2
  185.2 1.4 copy-start.11
  185.7 1.2 copy-start.3
  186.6 1.1 copy-start.13
  187.8 87.3 %collective-permute-start.20 = (bf16[192,768]{1,0:T(8,128)(2,1)S(1)}, bf16[192,768]{1,0:T(8,128)(2,1)S(1)}, u32[]{:S(2)}, u32[]{:S(2)}) collective-permute-start(bf16[192,768]{1,0:T(8,128)(2,1)S(1)} %pad_maximum_fusion.1), channel_id=1, source_target_pairs={{0,4},{1,5},{2,6},{3,7},{4,8},{5,9},{6,10},{7,11},{8,12},{9,13},{1... | collective-permute-start | bytes 884744 | tf_op jit(solution)/shard_map/ppermute | solution.py:23
  190.6 68.2 %collective-permute-start.16 = (bf16[1,4,80,128]{3,2,1,0:T(8,128)(2,1)S(1)}, bf16[1,4,80,128]{3,2,1,0:T(8,128)(2,1)S(1)}, u32[]{:S(2)}, u32[]{:S(2)}) collective-permute-start(bf16[1,4,80,128]{3,2,1,0:T(8,128)(2,1)S(1)} %get-tuple-element.135), channel_id=1, source_target_pairs={{0,16},{16,32},{32,48},{48,64},{64,80},{80,96},{96,112},{112,128},... | collective-permute-start | bytes 245768 | tf_op jit(solution)/shard_map/ppermute | solution.py:14
  192.5 66.3 %copy-start.1 = (f32[2,4,4,4,4,5,128]{6,1,5,4,3,2,0:T(4,128)S(1)}, f32[2,4,4,4,4,5,128]{6,1,5,4,3,2,0:T(4,128)}, u32[]{:S(2)}) copy-start(f32[2,4,4,4,4,5,128]{6,1,5,4,3,2,0:T(4,128)} %copy.127) | copy-start | bytes 3932164
  192.6 21.6 %collective-permute-start.18 = (bf16[2,1,80,128]{3,2,1,0:T(8,128)(2,1)S(1)}, bf16[2,1,80,128]{3,2,1,0:T(8,128)(2,1)S(1)}, u32[]{:S(2)}, u32[]{:S(2)}) collective-permute-start(bf16[2,1,80,128]{3,2,1,0:T(8,128)(2,1)S(1)} %slice.586), channel_id=1, source_target_pairs={{0,1},{1,2},{2,3},{3,4},{4,5},{5,6},{6,7},{7,8},{8,9},{9,10},{10,1... | collective-permute-start | bytes 122888 | tf_op jit(solution)/shard_map/ppermute | solution.py:14
  195.1 61.6 %collective-permute-start.19 = (bf16[2,1,80,128]{3,2,1,0:T(8,128)(2,1)S(1)}, bf16[2,1,80,128]{3,2,1,0:T(8,128)(2,1)S(1)}, u32[]{:S(2)}, u32[]{:S(2)}) collective-permute-start(bf16[2,1,80,128]{3,2,1,0:T(8,128)(2,1)S(1)} %slice.591), channel_id=1, source_target_pairs={{1,0},{2,1},{3,2},{4,3},{5,4},{6,5},{7,6},{8,7},{9,8},{10,9},{11,1... | collective-permute-start | bytes 122888 | tf_op jit(solution)/shard_map/ppermute | solution.py:14
  196.4 78.7 %collective-permute-start.21 = (bf16[192,768]{1,0:T(8,128)(2,1)S(1)}, bf16[192,768]{1,0:T(8,128)(2,1)S(1)}, u32[]{:S(2)}, u32[]{:S(2)}) collective-permute-start(bf16[192,768]{1,0:T(8,128)(2,1)S(1)} %pad_maximum_fusion.1), channel_id=1, source_target_pairs={{0,8},{1,9},{2,10},{3,11},{4,12},{5,13},{6,14},{7,15},{8,0},{9,1},... | collective-permute-start | bytes 884744 | tf_op jit(solution)/shard_map/ppermute | solution.py:23
  214.2 61.0 %collective-permute-start.22 = (bf16[192,768]{1,0:T(8,128)(2,1)S(1)}, bf16[192,768]{1,0:T(8,128)(2,1)S(1)}, u32[]{:S(2)}, u32[]{:S(2)}) collective-permute-start(bf16[192,768]{1,0:T(8,128)(2,1)S(1)} %pad_maximum_fusion.1), channel_id=1, source_target_pairs={{0,12},{1,13},{2,14},{3,15},{4,0},{5,1},{6,2},{7,3},{8,4},{9,5},{1... | collective-permute-start | bytes 884744 | tf_op jit(solution)/shard_map/ppermute | solution.py:23
  256.7 18.3 %collective-permute-start.17 = (bf16[1,4,80,128]{3,2,1,0:T(8,128)(2,1)S(1)}, bf16[1,4,80,128]{3,2,1,0:T(8,128)(2,1)S(1)}, u32[]{:S(2)}, u32[]{:S(2)}) collective-permute-start(bf16[1,4,80,128]{3,2,1,0:T(8,128)(2,1)S(1)} %get-tuple-element.133), channel_id=1, source_target_pairs={{16,0},{32,16},{48,32},{64,48},{80,64},{96,80},{112,96},{128,112},... | collective-permute-start | bytes 245768 | tf_op jit(solution)/shard_map/ppermute | solution.py:14
  258.8 16.4 %copy-start.27 = (s32[192]{0:T(256)S(1)}, s32[192]{0:T(256)}, u32[]{:S(2)}) copy-start(s32[192]{0:T(256)} %concatenate.187) | copy-start | bytes 2308
  258.8 16.4 %copy-start.33 = (s32[192]{0:T(256)S(1)}, s32[192]{0:T(256)}, u32[]{:S(2)}) copy-start(s32[192]{0:T(256)} %concatenate.186) | copy-start | bytes 2308
  277.0 29.9 %collective-permute-start.23 = (f32[192,768]{1,0:T(8,128)S(1)}, f32[192,768]{1,0:T(8,128)S(1)}, u32[]{:S(2)}, u32[]{:S(2)}) collective-permute-start(f32[192,768]{1,0:T(8,128)S(1)} %fusion.14), channel_id=1, source_target_pairs={{0,1},{1,2},{2,3},{3,0},{4,5},{5,6},{6,7},{7,4},{8,9},{9,10},{10,1... | collective-permute-start | bytes 1769480 | tf_op jit(solution)/shard_map/ppermute | solution.py:23
  278.9 27.9 %collective-permute-start.24 = (f32[192,768]{1,0:T(8,128)S(1)}, f32[192,768]{1,0:T(8,128)S(1)}, u32[]{:S(2)}, u32[]{:S(2)}) collective-permute-start(f32[192,768]{1,0:T(8,128)S(1)} %fusion.16), channel_id=1, source_target_pairs={{0,2},{1,3},{2,0},{3,1},{4,6},{5,7},{6,4},{7,5},{8,10},{9,11},{10,... | collective-permute-start | bytes 1769480 | tf_op jit(solution)/shard_map/ppermute | solution.py:23
  280.8 28.5 %collective-permute-start.25 = (f32[192,768]{1,0:T(8,128)S(1)}, f32[192,768]{1,0:T(8,128)S(1)}, u32[]{:S(2)}, u32[]{:S(2)}) collective-permute-start(f32[192,768]{1,0:T(8,128)S(1)} %fusion.18), channel_id=1, source_target_pairs={{0,3},{1,0},{2,1},{3,2},{4,7},{5,4},{6,5},{7,6},{8,11},{9,8},{10,9... | collective-permute-start | bytes 1769480 | tf_op jit(solution)/shard_map/ppermute | solution.py:23
  286.2 23.2 %copy-start.19 = (s32[192]{0:T(256)S(1)}, s32[192]{0:T(256)}, u32[]{:S(2)}) copy-start(s32[192]{0:T(256)} %copy-done.18) | copy-start | bytes 2308
  286.2 23.2 %copy-start.21 = (s32[192]{0:T(256)S(1)}, s32[192]{0:T(256)}, u32[]{:S(2)}) copy-start(s32[192]{0:T(256)} %concatenate.182) | copy-start | bytes 2308
  317.4 1.5 copy-start.12
  317.5 1.9 copy-start.4
  (4 other events, 2.7 us)

commit v6 on v3

--- a/solution.py
+++ b/solution.py
@@ -111,16 +111,22 @@
             jnp.dot(h, column, preferred_element_type=jnp.float32).astype(jnp.bfloat16)
             for h in pick_hits
         ]
+        wall_rows = fluid.reshape(rows, cols, 4, 4, 4, NV, width)[:, :, :, :, 0].reshape(
+            wall_count, NV * width
+        )
+        padded = jnp.pad(wall_rows, ((0, 0), (0, (sdof - NV) * width)))
+        arrived = [
+            chord_shift(jnp.concatenate([served[k], padded]), 0, k) for k in range(1, CY)
+        ]
         picked = served[0].astype(jnp.float32)
-        for k in range(1, CY):
-            picked = picked + chord_shift(served[k], 0, k).astype(jnp.float32)
+        for a in arrived:
+            picked = picked + a[:wall_count].astype(jnp.float32)
         wall_in = jnp.einsum(
             "sv,wsr->wvr", couple, picked.reshape(wall_count, sdof, width), precision=high
         )
-        wall_rows = fluid.reshape(rows, cols, 4, 4, 4, NV, width)[:, :, :, :, 0].reshape(
-            wall_count, NV * width
+        row_group = jnp.concatenate(
+            [wall_rows] + [a[wall_count:, : NV * width] for a in arrived]
         )
-        row_group = jnp.concatenate(over_y(wall_rows))
         partial = jnp.dot(load_hit, row_group, preferred_element_type=jnp.float32)
         partial = partial.reshape(cz, shell_count, NV * width)
         summed = partial[0]

time: 284 us -> 299 us (1.053)
  the two profiles are of different devices: /device:TPU:1 before, /device:TPU:37 now
where the time goes in v6:
time: 299 us; the launch traced here: 297 us
  starting transfers between devices  131 us (44%)
  waiting for transfers between devices  91 us (30%)
  local copies, waits for them, and re-layouts  44.5 us (15%)
  matrix products  21 us (7%)
  other arithmetic  7.84 us (3%)
    ppermute x21, starting transfers between devices, chord_shift(): return lax.ppermute(block, 'chord', route)  113 us
    ppermute x21, waiting for transfers between devices, chord_shift(): return lax.ppermute(block, 'chord', route)  84.5 us
    ppermute x8, starting transfers between devices, passed_along(): return lax.ppermute(block, axis, route)  18.4 us
    unnamed x79, local copies, waits for them, and re-layouts  9.37 us
    dot_general x8, matrix products, per_device(): jnp.dot(h, column, preferred_element_type=jnp.float32).astype(jnp.bfloat16)  7.29 us
    ppermute x8, waiting for transfers between devices, passed_along(): return lax.ppermute(block, axis, route)  6.47 us
  transfers between devices with their start and end apart: 29, of which 13 were waited for; matrix products, arithmetic and copies ran while one was open for 12% of the time, Pallas kernels for 0%

profile of v6, /device:TPU:37, one launch (start us, length us, event | category | flops | bytes accessed | tf_op | source)
XLA Modules:
  0.0 297.4 jit_solution(14005234611574942874)
XLA Ops:
  0.6 1.0 copy.51
  1.7 1.3 convolution_convert_fusion.13
  3.6 8.8 %collective-permute-start.4 = (bf16[64,768]{1,0:T(8,128)(2,1)}, bf16[64,768]{1,0:T(8,128)(2,1)}, u32[]{:S(2)}, u32[]{:S(2)}) collective-permute-start(bf16[64,768]{1,0:T(8,128)(2,1)} %get-tuple-element.129), channel_id=1, source_target_pairs={{0,4},{1,5},{2,6},{3,7},{4,8},{5,9},{6,10},{7,11},{8,12},{9,13},{1... | collective-permute-start | bytes 294920 | tf_op jit(solution)/shard_map/ppermute | solution.py:23
  12.4 9.7 %collective-permute-start.5 = (bf16[64,768]{1,0:T(8,128)(2,1)}, bf16[64,768]{1,0:T(8,128)(2,1)}, u32[]{:S(2)}, u32[]{:S(2)}) collective-permute-start(bf16[64,768]{1,0:T(8,128)(2,1)} %get-tuple-element.129), channel_id=1, source_target_pairs={{0,8},{1,9},{2,10},{3,11},{4,12},{5,13},{6,14},{7,15},{8,0},{9,1},... | collective-permute-start | bytes 294920 | tf_op jit(solution)/shard_map/ppermute | solution.py:23
  23.0 4.6 %collective-permute-start.7 = (s32[128]{0:T(128)S(1)}, s32[128]{0:T(128)}, u32[]{:S(2)}, u32[]{:S(2)}) collective-permute-start(s32[128]{0:T(128)S(1)} %eq.31), channel_id=1, source_target_pairs={{0,3},{1,0},{2,1},{3,2},{4,7},{5,4},{6,5},{7,6},{8,11},{9,8},{10,9... | collective-permute-start | bytes 1544 | tf_op jit(solution)/shard_map/ppermute | solution.py:23
  27.6 2.3 collective-permute-start.9
  29.9 2.6 collective-permute-start.11
  32.5 1.6 copy.38
  34.1 1.9 convolution_convert_fusion.2
  40.2 2.4 copy.53
  42.6 1.1 copy.126
  46.6 1.0 copy.47
  49.1 1.0 slice.649
  51.5 4.7 %collective-permute-start = (bf16[1,4,80,128]{3,2,1,0:T(8,128)(2,1)}, bf16[1,4,80,128]{3,2,1,0:T(8,128)(2,1)S(1)}, u32[]{:S(2)}, u32[]{:S(2)}) collective-permute-start(bf16[1,4,80,128]{3,2,1,0:T(8,128)(2,1)} %get-tuple-element.147), channel_id=1, source_target_pairs={{0,16},{16,32},{32,48},{48,64},{64,80},{80,96},{96,112},{112,128},... | collective-permute-start | bytes 245768 | tf_op jit(solution)/shard_map/ppermute | solution.py:14
  56.2 3.5 %collective-permute-start.2 = (bf16[2,1,80,128]{3,2,1,0:T(8,128)(2,1)}, bf16[2,1,80,128]{3,2,1,0:T(8,128)(2,1)S(1)}, u32[]{:S(2)}, u32[]{:S(2)}) collective-permute-start(bf16[2,1,80,128]{3,2,1,0:T(8,128)(2,1)} %slice.642), channel_id=1, source_target_pairs={{0,1},{1,2},{2,3},{3,4},{4,5},{5,6},{6,7},{7,8},{8,9},{9,10},{10,1... | collective-permute-start | bytes 122888 | tf_op jit(solution)/shard_map/ppermute | solution.py:14
  59.8 1.3 collective-permute-start.3
  61.1 1.2 pad_add_fusion
  62.3 12.7 %collective-permute-start.6 = (bf16[64,768]{1,0:T(8,128)(2,1)}, bf16[64,768]{1,0:T(8,128)(2,1)S(1)}, u32[]{:S(2)}, u32[]{:S(2)}) collective-permute-start(bf16[64,768]{1,0:T(8,128)(2,1)} %get-tuple-element.129), channel_id=1, source_target_pairs={{0,12},{1,13},{2,14},{3,15},{4,0},{5,1},{6,2},{7,3},{8,4},{9,5},{1... | collective-permute-start | bytes 294920 | tf_op jit(solution)/shard_map/ppermute | solution.py:23
  75.1 1.9 collective-permute-start.1
  77.2 1.0 add_dynamic-update-slice_fusion.1
  78.2 6.5 %collective-permute-done.1 = bf16[1,4,80,128]{3,2,1,0:T(8,128)(2,1)S(1)} collective-permute-done((bf16[1,4,80,128]{3,2,1,0:T(8,128)(2,1)}, bf16[1,4,80,128]{3,2,1,0:T(8,128)(2,1)S(1)}, u32[]{:S(2)}, u32[]{:S(2)}) %collective-permute-start.1) | collective-permute-done | bytes 81952 | tf_op jit(solution)/shard_map/ppermute | solution.py:14
  84.9 0.9 constant_dynamic-update-slice_fusion.2
  89.5 1.9 collective-permute-start.12
  91.5 1.9 collective-permute-start.10
  93.4 3.4 %collective-permute-start.8 = (bf16[256,768]{1,0:T(8,128)(2,1)S(1)}, bf16[256,768]{1,0:T(8,128)(2,1)S(1)}, u32[]{:S(2)}, u32[]{:S(2)}) collective-permute-start(bf16[256,768]{1,0:T(8,128)(2,1)S(1)} %get-tuple-element.151), channel_id=1, source_target_pairs={{0,1},{1,2},{2,3},{3,0},{4,5},{5,6},{6,7},{7,4},{8,9},{9,10},{10,1... | collective-permute-start | bytes 1179656 | tf_op jit(solution)/shard_map/ppermute | solution.py:23
  97.4 4.5 %collective-permute-done.12 = bf16[256,768]{1,0:T(8,128)(2,1)S(1)} collective-permute-done((bf16[256,768]{1,0:T(8,128)(2,1)S(1)}, bf16[256,768]{1,0:T(8,128)(2,1)S(1)}, u32[]{:S(2)}, u32[]{:S(2)}) %collective-permute-start.12) | collective-permute-done | bytes 393248 | tf_op jit(solution)/shard_map/ppermute | solution.py:23
  101.9 3.5 %collective-permute-done.10 = bf16[256,768]{1,0:T(8,128)(2,1)S(1)} collective-permute-done((bf16[256,768]{1,0:T(8,128)(2,1)S(1)}, bf16[256,768]{1,0:T(8,128)(2,1)S(1)}, u32[]{:S(2)}, u32[]{:S(2)}) %collective-permute-start.10) | collective-permute-done | bytes 393248 | tf_op jit(solution)/shard_map/ppermute | solution.py:23
  105.4 8.9 %collective-permute-done.8 = bf16[256,768]{1,0:T(8,128)(2,1)S(1)} collective-permute-done((bf16[256,768]{1,0:T(8,128)(2,1)S(1)}, bf16[256,768]{1,0:T(8,128)(2,1)S(1)}, u32[]{:S(2)}, u32[]{:S(2)}) %collective-permute-start.8) | collective-permute-done | bytes 393248 | tf_op jit(solution)/shard_map/ppermute | solution.py:23
  115.1 1.0 fusion.12
  116.1 1.9 copy.55
  118.0 2.0 copy.56
  120.0 1.7 convolution_negate_fusion.1
  124.6 1.9 collective-permute-start.13
  126.5 2.4 collective-permute-start.14
  129.0 1.3 collective-permute-start.15
  130.3 1.3 collective-permute-start.16
  137.3 13.4 %collective-permute-start.19 = (f32[64,640]{1,0:T(8,128)S(1)}, f32[64,640]{1,0:T(8,128)S(1)}, u32[]{:S(2)}, u32[]{:S(2)}) collective-permute-start(f32[64,640]{1,0:T(8,128)S(1)} %get-tuple-element.134), channel_id=1, source_target_pairs={{0,12},{1,13},{2,14},{3,15},{4,0},{5,1},{6,2},{7,3},{8,4},{9,5},{1... | collective-permute-start | bytes 491528 | tf_op jit(solution)/shard_map/ppermute | solution.py:23
  152.0 4.2 %collective-permute-start.18 = (f32[64,640]{1,0:T(8,128)S(1)}, f32[64,640]{1,0:T(8,128)S(1)}, u32[]{:S(2)}, u32[]{:S(2)}) collective-permute-start(f32[64,640]{1,0:T(8,128)S(1)} %get-tuple-element.135), channel_id=1, source_target_pairs={{0,8},{1,9},{2,10},{3,11},{4,12},{5,13},{6,14},{7,15},{8,0},{9,1},... | collective-permute-start | bytes 491528 | tf_op jit(solution)/shard_map/ppermute | solution.py:23
  157.0 5.5 %collective-permute-start.17 = (f32[64,640]{1,0:T(8,128)S(1)}, f32[64,640]{1,0:T(8,128)S(1)}, u32[]{:S(2)}, u32[]{:S(2)}) collective-permute-start(f32[64,640]{1,0:T(8,128)S(1)} %get-tuple-element.133), channel_id=1, source_target_pairs={{0,4},{1,5},{2,6},{3,7},{4,8},{5,9},{6,10},{7,11},{8,12},{9,13},{1... | collective-permute-start | bytes 491528 | tf_op jit(solution)/shard_map/ppermute | solution.py:23
  164.1 11.6 %collective-permute-done.18 = f32[64,640]{1,0:T(8,128)S(1)} collective-permute-done((f32[64,640]{1,0:T(8,128)S(1)}, f32[64,640]{1,0:T(8,128)S(1)}, u32[]{:S(2)}, u32[]{:S(2)}) %collective-permute-start.18) | collective-permute-done | bytes 163872 | tf_op jit(solution)/shard_map/ppermute | solution.py:23
  175.8 13.1 %collective-permute-done.17 = f32[64,640]{1,0:T(8,128)S(1)} collective-permute-done((f32[64,640]{1,0:T(8,128)S(1)}, f32[64,640]{1,0:T(8,128)S(1)}, u32[]{:S(2)}, u32[]{:S(2)}) %collective-permute-start.17) | collective-permute-done | bytes 163872 | tf_op jit(solution)/shard_map/ppermute | solution.py:23
  189.6 1.6 reshape.875
  191.2 1.3 fusion.84
  194.2 2.7 collective-permute-start.20
  197.0 11.4 %collective-permute-start.21 = (bf16[64,768]{1,0:T(8,128)(2,1)S(1)}, bf16[64,768]{1,0:T(8,128)(2,1)S(1)}, u32[]{:S(2)}, u32[]{:S(2)}) collective-permute-start(bf16[64,768]{1,0:T(8,128)(2,1)S(1)} %get-tuple-element.127), channel_id=1, source_target_pairs={{0,8},{1,9},{2,10},{3,11},{4,12},{5,13},{6,14},{7,15},{8,0},{9,1},... | collective-permute-start | bytes 294920 | tf_op jit(solution)/shard_map/ppermute | solution.py:23
  208.5 2.8 collective-permute-start.22
  211.4 3.7 %collective-permute-done.21 = bf16[64,768]{1,0:T(8,128)(2,1)S(1)} collective-permute-done((bf16[64,768]{1,0:T(8,128)(2,1)S(1)}, bf16[64,768]{1,0:T(8,128)(2,1)S(1)}, u32[]{:S(2)}, u32[]{:S(2)}) %collective-permute-start.21) | collective-permute-done | bytes 98336 | tf_op jit(solution)/shard_map/ppermute | solution.py:23
  215.1 3.1 %collective-permute-done.22 = bf16[64,768]{1,0:T(8,128)(2,1)S(1)} collective-permute-done((bf16[64,768]{1,0:T(8,128)(2,1)S(1)}, bf16[64,768]{1,0:T(8,128)(2,1)S(1)}, u32[]{:S(2)}, u32[]{:S(2)}) %collective-permute-start.22) | collective-permute-done | bytes 98336 | tf_op jit(solution)/shard_map/ppermute | solution.py:23
  221.0 2.4 collective-permute-start.25
  223.4 1.9 collective-permute-start.24
  225.3 2.9 collective-permute-start.23
  228.9 2.6 collective-permute-done.25
  231.5 3.3 %collective-permute-done.24 = bf16[256,768]{1,0:T(8,128)(2,1)S(1)} collective-permute-done((bf16[256,768]{1,0:T(8,128)(2,1)S(1)}, bf16[256,768]{1,0:T(8,128)(2,1)S(1)}, u32[]{:S(2)}, u32[]{:S(2)}) %collective-permute-start.24) | collective-permute-done | bytes 393248 | tf_op jit(solution)/shard_map/ppermute | solution.py:23
  234.8 11.4 %collective-permute-done.23 = bf16[256,768]{1,0:T(8,128)(2,1)S(1)} collective-permute-done((bf16[256,768]{1,0:T(8,128)(2,1)S(1)}, bf16[256,768]{1,0:T(8,128)(2,1)S(1)}, u32[]{:S(2)}, u32[]{:S(2)}) %collective-permute-start.23) | collective-permute-done | bytes 393248 | tf_op jit(solution)/shard_map/ppermute | solution.py:23
  247.0 1.0 fusion.8
  248.0 1.9 copy.76
  250.0 2.0 copy.77
  251.9 1.7 convolution_negate_fusion
  257.5 7.6 %collective-permute-start.28 = (f32[64,640]{1,0:T(8,128)S(1)}, f32[64,640]{1,0:T(8,128)S(1)}, u32[]{:S(2)}, u32[]{:S(2)}) collective-permute-start(f32[64,640]{1,0:T(8,128)S(1)} %get-tuple-element.131), channel_id=1, source_target_pairs={{0,12},{1,13},{2,14},{3,15},{4,0},{5,1},{6,2},{7,3},{8,4},{9,5},{1... | collective-permute-start | bytes 491528 | tf_op jit(solution)/shard_map/ppermute | solution.py:23
  265.2 4.5 %collective-permute-start.27 = (f32[64,640]{1,0:T(8,128)S(1)}, f32[64,640]{1,0:T(8,128)S(1)}, u32[]{:S(2)}, u32[]{:S(2)}) collective-permute-start(f32[64,640]{1,0:T(8,128)S(1)} %get-tuple-element.132), channel_id=1, source_target_pairs={{0,8},{1,9},{2,10},{3,11},{4,12},{5,13},{6,14},{7,15},{8,0},{9,1},... | collective-permute-start | bytes 491528 | tf_op jit(solution)/shard_map/ppermute | solution.py:23
  269.7 5.7 %collective-permute-start.26 = (f32[64,640]{1,0:T(8,128)S(1)}, f32[64,640]{1,0:T(8,128)S(1)}, u32[]{:S(2)}, u32[]{:S(2)}) collective-permute-start(f32[64,640]{1,0:T(8,128)S(1)} %get-tuple-element.130), channel_id=1, source_target_pairs={{0,4},{1,5},{2,6},{3,7},{4,8},{5,9},{6,10},{7,11},{8,12},{9,13},{1... | collective-permute-start | bytes 491528 | tf_op jit(solution)/shard_map/ppermute | solution.py:23
  275.3 1.5 fusion.2
  276.9 4.9 %collective-permute-done.27 = f32[64,640]{1,0:T(8,128)S(1)} collective-permute-done((f32[64,640]{1,0:T(8,128)S(1)}, f32[64,640]{1,0:T(8,128)S(1)}, u32[]{:S(2)}, u32[]{:S(2)}) %collective-permute-start.27) | collective-permute-done | bytes 163872 | tf_op jit(solution)/shard_map/ppermute | solution.py:23
  281.7 13.8 %collective-permute-done.26 = f32[64,640]{1,0:T(8,128)S(1)} collective-permute-done((f32[64,640]{1,0:T(8,128)S(1)}, f32[64,640]{1,0:T(8,128)S(1)}, u32[]{:S(2)}, u32[]{:S(2)}) %collective-permute-start.26) | collective-permute-done | bytes 163872 | tf_op jit(solution)/shard_map/ppermute | solution.py:23
  (180 shorter events, 41.3 us)
Async XLA Ops:
  0.6 33.5 %copy-start = (bf16[2,4,320,320]{3,2,1,0:T(8,128)(2,1)S(1)}, bf16[2,4,320,320]{3,2,1,0:T(8,128)(2,1)}, u32[]{:S(2)}) copy-start(bf16[2,4,320,320]{3,2,1,0:T(8,128)(2,1)} %param.29) | copy-start | bytes 4915204
  3.6 81.3 %collective-permute-start.4 = (bf16[64,768]{1,0:T(8,128)(2,1)}, bf16[64,768]{1,0:T(8,128)(2,1)}, u32[]{:S(2)}, u32[]{:S(2)}) collective-permute-start(bf16[64,768]{1,0:T(8,128)(2,1)} %get-tuple-element.129), channel_id=1, source_target_pairs={{0,4},{1,5},{2,6},{3,7},{4,8},{5,9},{6,10},{7,11},{8,12},{9,13},{1... | collective-permute-start | bytes 294920 | tf_op jit(solution)/shard_map/ppermute | solution.py:23
  12.4 73.4 %collective-permute-start.5 = (bf16[64,768]{1,0:T(8,128)(2,1)}, bf16[64,768]{1,0:T(8,128)(2,1)}, u32[]{:S(2)}, u32[]{:S(2)}) collective-permute-start(bf16[64,768]{1,0:T(8,128)(2,1)} %get-tuple-element.129), channel_id=1, source_target_pairs={{0,8},{1,9},{2,10},{3,11},{4,12},{5,13},{6,14},{7,15},{8,0},{9,1},... | collective-permute-start | bytes 294920 | tf_op jit(solution)/shard_map/ppermute | solution.py:23
  23.0 28.5 %collective-permute-start.7 = (s32[128]{0:T(128)S(1)}, s32[128]{0:T(128)}, u32[]{:S(2)}, u32[]{:S(2)}) collective-permute-start(s32[128]{0:T(128)S(1)} %eq.31), channel_id=1, source_target_pairs={{0,3},{1,0},{2,1},{3,2},{4,7},{5,4},{6,5},{7,6},{8,11},{9,8},{10,9... | collective-permute-start | bytes 1544 | tf_op jit(solution)/shard_map/ppermute | solution.py:23
  27.6 28.6 %collective-permute-start.9 = (s32[128]{0:T(128)S(1)}, s32[128]{0:T(128)}, u32[]{:S(2)}, u32[]{:S(2)}) collective-permute-start(s32[128]{0:T(128)S(1)} %eq.31), channel_id=1, source_target_pairs={{0,2},{1,3},{2,0},{3,1},{4,6},{5,7},{6,4},{7,5},{8,10},{9,11},{10,... | collective-permute-start | bytes 1544 | tf_op jit(solution)/shard_map/ppermute | solution.py:23
  29.9 29.9 %collective-permute-start.11 = (s32[128]{0:T(128)S(1)}, s32[128]{0:T(128)}, u32[]{:S(2)}, u32[]{:S(2)}) collective-permute-start(s32[128]{0:T(128)S(1)} %eq.31), channel_id=1, source_target_pairs={{0,1},{1,2},{2,3},{3,0},{4,5},{5,6},{6,7},{7,4},{8,9},{9,10},{10,1... | collective-permute-start | bytes 1544 | tf_op jit(solution)/shard_map/ppermute | solution.py:23
  34.1 1.9 copy-start.30
  34.1 1.9 copy-start.2
  36.0 0.8 copy-start.5
  42.6 1.1 copy-start.25
  42.6 1.8 copy-start.24
  42.6 2.4 copy-start.15
  51.5 33.2 %copy-start.22 = (bf16[1,4,1,80,128]{4,1,3,2,0:T(4,128)(2,1)S(1)}, bf16[1,4,1,80,128]{4,1,3,2,0:T(4,128)(2,1)}, u32[]{:S(2)}) copy-start(bf16[1,4,1,80,128]{4,1,3,2,0:T(4,128)(2,1)} %copy.41) | copy-start | bytes 245764
  51.5 33.4 %copy-start.4 = (bf16[256,768]{1,0:T(8,128)(2,1)S(1)}, bf16[256,768]{1,0:T(8,128)(2,1)}, u32[]{:S(2)}) copy-start(bf16[256,768]{1,0:T(8,128)(2,1)} %get-tuple-element.128) | copy-start | bytes 1179652
  51.5 25.6 %collective-permute-start = (bf16[1,4,80,128]{3,2,1,0:T(8,128)(2,1)}, bf16[1,4,80,128]{3,2,1,0:T(8,128)(2,1)S(1)}, u32[]{:S(2)}, u32[]{:S(2)}) collective-permute-start(bf16[1,4,80,128]{3,2,1,0:T(8,128)(2,1)} %get-tuple-element.147), channel_id=1, source_target_pairs={{0,16},{16,32},{32,48},{48,64},{64,80},{80,96},{96,112},{112,128},... | collective-permute-start | bytes 245768 | tf_op jit(solution)/shard_map/ppermute | solution.py:14
  56.2 6.1 %collective-permute-start.2 = (bf16[2,1,80,128]{3,2,1,0:T(8,128)(2,1)}, bf16[2,1,80,128]{3,2,1,0:T(8,128)(2,1)S(1)}, u32[]{:S(2)}, u32[]{:S(2)}) collective-permute-start(bf16[2,1,80,128]{3,2,1,0:T(8,128)(2,1)} %slice.642), channel_id=1, source_target_pairs={{0,1},{1,2},{2,3},{3,4},{4,5},{5,6},{6,7},{7,8},{8,9},{9,10},{10,1... | collective-permute-start | bytes 122888 | tf_op jit(solution)/shard_map/ppermute | solution.py:14
  59.8 15.3 %collective-permute-start.3 = (bf16[2,1,80,128]{3,2,1,0:T(8,128)(2,1)}, bf16[2,1,80,128]{3,2,1,0:T(8,128)(2,1)S(1)}, u32[]{:S(2)}, u32[]{:S(2)}) collective-permute-start(bf16[2,1,80,128]{3,2,1,0:T(8,128)(2,1)} %slice.647), channel_id=1, source_target_pairs={{1,0},{2,1},{3,2},{4,3},{5,4},{6,5},{7,6},{8,7},{9,8},{10,9},{11,1... | collective-permute-start | bytes 122888 | tf_op jit(solution)/shard_map/ppermute | solution.py:14
  62.3 24.5 %collective-permute-start.6 = (bf16[64,768]{1,0:T(8,128)(2,1)}, bf16[64,768]{1,0:T(8,128)(2,1)S(1)}, u32[]{:S(2)}, u32[]{:S(2)}) collective-permute-start(bf16[64,768]{1,0:T(8,128)(2,1)} %get-tuple-element.129), channel_id=1, source_target_pairs={{0,12},{1,13},{2,14},{3,15},{4,0},{5,1},{6,2},{7,3},{8,4},{9,5},{1... | collective-permute-start | bytes 294920 | tf_op jit(solution)/shard_map/ppermute | solution.py:23
  75.1 9.6 %collective-permute-start.1 = (bf16[1,4,80,128]{3,2,1,0:T(8,128)(2,1)}, bf16[1,4,80,128]{3,2,1,0:T(8,128)(2,1)S(1)}, u32[]{:S(2)}, u32[]{:S(2)}) collective-permute-start(bf16[1,4,80,128]{3,2,1,0:T(8,128)(2,1)} %get-tuple-element.145), channel_id=1, source_target_pairs={{16,0},{32,16},{48,32},{64,48},{80,64},{96,80},{112,96},{128,112},... | collective-permute-start | bytes 245768 | tf_op jit(solution)/shard_map/ppermute | solution.py:14
  84.9 4.6 %copy-start.11 = (bf16[16,8,5,128]{3,1,2,0:T(8,128)(2,1)S(1)}, bf16[16,8,5,128]{3,1,2,0:T(8,128)(2,1)}, u32[]{:S(2)}) copy-start(bf16[16,8,5,128]{3,1,2,0:T(8,128)(2,1)} %copy.117) | copy-start | bytes 491524
  88.5 8.2 %copy-start.7 = (bf16[2,3,4,1,4,5,128]{6,1,5,4,3,2,0:T(4,128)(2,1)S(1)}, bf16[2,3,4,1,4,5,128]{6,1,5,4,3,2,0:T(4,128)(2,1)}, u32[]{:S(2)}) copy-start(bf16[2,3,4,1,4,5,128]{6,1,5,4,3,2,0:T(4,128)(2,1)} %copy.46) | copy-start | bytes 368644
  89.5 7.7 %copy-start.10 = (bf16[2,3,4,1,4,5,128]{6,1,5,4,3,2,0:T(4,128)(2,1)S(1)}, bf16[2,3,4,1,4,5,128]{6,1,5,4,3,2,0:T(4,128)(2,1)}, u32[]{:S(2)}) copy-start(bf16[2,3,4,1,4,5,128]{6,1,5,4,3,2,0:T(4,128)(2,1)} %copy.49) | copy-start | bytes 368644
  89.5 12.4 %collective-permute-start.12 = (bf16[256,768]{1,0:T(8,128)(2,1)S(1)}, bf16[256,768]{1,0:T(8,128)(2,1)S(1)}, u32[]{:S(2)}, u32[]{:S(2)}) collective-permute-start(bf16[256,768]{1,0:T(8,128)(2,1)S(1)} %get-tuple-element.153), channel_id=1, source_target_pairs={{0,3},{1,0},{2,1},{3,2},{4,7},{5,4},{6,5},{7,6},{8,11},{9,8},{10,9... | collective-permute-start | bytes 1179656 | tf_op jit(solution)/shard_map/ppermute | solution.py:23
  91.5 13.9 %collective-permute-start.10 = (bf16[256,768]{1,0:T(8,128)(2,1)S(1)}, bf16[256,768]{1,0:T(8,128)(2,1)S(1)}, u32[]{:S(2)}, u32[]{:S(2)}) collective-permute-start(bf16[256,768]{1,0:T(8,128)(2,1)S(1)} %get-tuple-element.152), channel_id=1, source_target_pairs={{0,2},{1,3},{2,0},{3,1},{4,6},{5,7},{6,4},{7,5},{8,10},{9,11},{10,... | collective-permute-start | bytes 1179656 | tf_op jit(solution)/shard_map/ppermute | solution.py:23
  93.4 20.9 %collective-permute-start.8 = (bf16[256,768]{1,0:T(8,128)(2,1)S(1)}, bf16[256,768]{1,0:T(8,128)(2,1)S(1)}, u32[]{:S(2)}, u32[]{:S(2)}) collective-permute-start(bf16[256,768]{1,0:T(8,128)(2,1)S(1)} %get-tuple-element.151), channel_id=1, source_target_pairs={{0,1},{1,2},{2,3},{3,0},{4,5},{5,6},{6,7},{7,4},{8,9},{9,10},{10,1... | collective-permute-start | bytes 1179656 | tf_op jit(solution)/shard_map/ppermute | solution.py:23
  97.4 22.6 %copy-start.29 = (f32[6,5]{1,0:T(8,128)S(1)}, f32[6,5]{1,0:T(8,128)}, u32[]{:S(2)}) copy-start(f32[6,5]{1,0:T(8,128)} %param.33) | copy-start | bytes 364
  101.9 12.4 %copy-start.16 = (bf16[256,768]{1,0:T(8,128)(2,1)}, bf16[256,768]{1,0:T(8,128)(2,1)S(1)}, u32[]{:S(2)}) copy-start(bf16[256,768]{1,0:T(8,128)(2,1)S(1)} %collective-permute-done.12) | copy-start | bytes 1179652
  105.4 8.9 %copy-start.17 = (bf16[256,768]{1,0:T(8,128)(2,1)}, bf16[256,768]{1,0:T(8,128)(2,1)S(1)}, u32[]{:S(2)}) copy-start(bf16[256,768]{1,0:T(8,128)(2,1)S(1)} %collective-permute-done.10) | copy-start | bytes 1179652
  114.4 0.8 copy-start.18
  122.3 1.5 copy-start.3
  124.5 9.9 %copy-start.12 = (bf16[16,8,5,128]{3,1,2,0:T(8,128)(2,1)S(1)}, bf16[16,8,5,128]{3,1,2,0:T(8,128)(2,1)}, u32[]{:S(2)}) copy-start(bf16[16,8,5,128]{3,1,2,0:T(8,128)(2,1)} %copy.117) | copy-start | bytes 491524
  124.5 9.9 %copy-start.31 = (s32[512]{0:T(512)S(1)}, s32[512]{0:T(512)}, u32[]{:S(2)}) copy-start(s32[512]{0:T(512)} %pad_add_fusion) | copy-start | bytes 6148
  124.5 9.9 %copy-start.32 = (s32[256]{0:T(256)S(1)}, s32[256]{0:T(256)}, u32[]{:S(2)}) copy-start(s32[256]{0:T(256)} %add.230) | copy-start | bytes 3076
  124.6 38.6 %collective-permute-start.13 = (bf16[1,4,80,128]{3,2,1,0:T(8,128)(2,1)S(1)}, bf16[1,4,80,128]{3,2,1,0:T(8,128)(2,1)S(1)}, u32[]{:S(2)}, u32[]{:S(2)}) collective-permute-start(bf16[1,4,80,128]{3,2,1,0:T(8,128)(2,1)S(1)} %get-tuple-element.141), channel_id=1, source_target_pairs={{0,16},{16,32},{32,48},{48,64},{64,80},{80,96},{96,112},{112,128},... | collective-permute-start | bytes 245768 | tf_op jit(solution)/shard_map/ppermute | solution.py:14
  126.5 36.7 %collective-permute-start.14 = (bf16[1,4,80,128]{3,2,1,0:T(8,128)(2,1)S(1)}, bf16[1,4,80,128]{3,2,1,0:T(8,128)(2,1)S(1)}, u32[]{:S(2)}, u32[]{:S(2)}) collective-permute-start(bf16[1,4,80,128]{3,2,1,0:T(8,128)(2,1)S(1)} %get-tuple-element.139), channel_id=1, source_target_pairs={{16,0},{32,16},{48,32},{64,48},{80,64},{96,80},{112,96},{128,112},... | collective-permute-start | bytes 245768 | tf_op jit(solution)/shard_map/ppermute | solution.py:14
  129.0 23.1 %collective-permute-start.15 = (bf16[2,1,80,128]{3,2,1,0:T(8,128)(2,1)S(1)}, bf16[2,1,80,128]{3,2,1,0:T(8,128)(2,1)S(1)}, u32[]{:S(2)}, u32[]{:S(2)}) collective-permute-start(bf16[2,1,80,128]{3,2,1,0:T(8,128)(2,1)S(1)} %slice.660), channel_id=1, source_target_pairs={{0,1},{1,2},{2,3},{3,4},{4,5},{5,6},{6,7},{7,8},{8,9},{9,10},{10,1... | collective-permute-start | bytes 122888 | tf_op jit(solution)/shard_map/ppermute | solution.py:14
  130.3 26.7 %collective-permute-start.16 = (bf16[2,1,80,128]{3,2,1,0:T(8,128)(2,1)S(1)}, bf16[2,1,80,128]{3,2,1,0:T(8,128)(2,1)S(1)}, u32[]{:S(2)}, u32[]{:S(2)}) collective-permute-start(bf16[2,1,80,128]{3,2,1,0:T(8,128)(2,1)S(1)} %slice.665), channel_id=1, source_target_pairs={{1,0},{2,1},{3,2},{4,3},{5,4},{6,5},{7,6},{8,7},{9,8},{10,9},{11,1... | collective-permute-start | bytes 122888 | tf_op jit(solution)/shard_map/ppermute | solution.py:14
  137.3 26.8 %collective-permute-start.19 = (f32[64,640]{1,0:T(8,128)S(1)}, f32[64,640]{1,0:T(8,128)S(1)}, u32[]{:S(2)}, u32[]{:S(2)}) collective-permute-start(f32[64,640]{1,0:T(8,128)S(1)} %get-tuple-element.134), channel_id=1, source_target_pairs={{0,12},{1,13},{2,14},{3,15},{4,0},{5,1},{6,2},{7,3},{8,4},{9,5},{1... | collective-permute-start | bytes 491528 | tf_op jit(solution)/shard_map/ppermute | solution.py:23
  150.7 13.3 %copy-start.1 = (f32[2,4,4,4,4,5,128]{6,1,5,4,3,2,0:T(4,128)S(1)}, f32[2,4,4,4,4,5,128]{6,1,5,4,3,2,0:T(4,128)}, u32[]{:S(2)}) copy-start(f32[2,4,4,4,4,5,128]{6,1,5,4,3,2,0:T(4,128)} %copy.126) | copy-start | bytes 3932164
  152.0 23.7 %collective-permute-start.18 = (f32[64,640]{1,0:T(8,128)S(1)}, f32[64,640]{1,0:T(8,128)S(1)}, u32[]{:S(2)}, u32[]{:S(2)}) collective-permute-start(f32[64,640]{1,0:T(8,128)S(1)} %get-tuple-element.135), channel_id=1, source_target_pairs={{0,8},{1,9},{2,10},{3,11},{4,12},{5,13},{6,14},{7,15},{8,0},{9,1},... | collective-permute-start | bytes 491528 | tf_op jit(solution)/shard_map/ppermute | solution.py:23
  157.0 31.9 %collective-permute-start.17 = (f32[64,640]{1,0:T(8,128)S(1)}, f32[64,640]{1,0:T(8,128)S(1)}, u32[]{:S(2)}, u32[]{:S(2)}) collective-permute-start(f32[64,640]{1,0:T(8,128)S(1)} %get-tuple-element.133), channel_id=1, source_target_pairs={{0,4},{1,5},{2,6},{3,7},{4,8},{5,9},{6,10},{7,11},{8,12},{9,13},{1... | collective-permute-start | bytes 491528 | tf_op jit(solution)/shard_map/ppermute | solution.py:23
  191.2 5.7 %copy-start.23 = (bf16[1,4,1,80,128]{4,1,3,2,0:T(4,128)(2,1)S(1)}, bf16[1,4,1,80,128]{4,1,3,2,0:T(4,128)(2,1)}, u32[]{:S(2)}) copy-start(bf16[1,4,1,80,128]{4,1,3,2,0:T(4,128)(2,1)} %copy.62) | copy-start | bytes 245764
  191.2 5.7 %copy-start.26 = (bf16[1,4,80,128]{3,1,2,0:T(4,128)(2,1)S(1)}, bf16[1,4,80,128]{3,1,2,0:T(4,128)(2,1)}, u32[]{:S(2)}) copy-start(bf16[1,4,80,128]{3,1,2,0:T(4,128)(2,1)} %copy.63) | copy-start | bytes 245764
  194.2 17.2 %collective-permute-start.20 = (bf16[64,768]{1,0:T(8,128)(2,1)S(1)}, bf16[64,768]{1,0:T(8,128)(2,1)S(1)}, u32[]{:S(2)}, u32[]{:S(2)}) collective-permute-start(bf16[64,768]{1,0:T(8,128)(2,1)S(1)} %get-tuple-element.127), channel_id=1, source_target_pairs={{0,4},{1,5},{2,6},{3,7},{4,8},{5,9},{6,10},{7,11},{8,12},{9,13},{1... | collective-permute-start | bytes 294920 | tf_op jit(solution)/shard_map/ppermute | solution.py:23
  197.0 23.8 %copy-start.13 = (bf16[16,8,5,128]{3,1,2,0:T(8,128)(2,1)S(1)}, bf16[16,8,5,128]{3,1,2,0:T(8,128)(2,1)}, u32[]{:S(2)}) copy-start(bf16[16,8,5,128]{3,1,2,0:T(8,128)(2,1)} %copy.116) | copy-start | bytes 491524
  197.0 18.0 %collective-permute-start.21 = (bf16[64,768]{1,0:T(8,128)(2,1)S(1)}, bf16[64,768]{1,0:T(8,128)(2,1)S(1)}, u32[]{:S(2)}, u32[]{:S(2)}) collective-permute-start(bf16[64,768]{1,0:T(8,128)(2,1)S(1)} %get-tuple-element.127), channel_id=1, source_target_pairs={{0,8},{1,9},{2,10},{3,11},{4,12},{5,13},{6,14},{7,15},{8,0},{9,1},... | collective-permute-start | bytes 294920 | tf_op jit(solution)/shard_map/ppermute | solution.py:23
  208.5 9.7 %collective-permute-start.22 = (bf16[64,768]{1,0:T(8,128)(2,1)S(1)}, bf16[64,768]{1,0:T(8,128)(2,1)S(1)}, u32[]{:S(2)}, u32[]{:S(2)}) collective-permute-start(bf16[64,768]{1,0:T(8,128)(2,1)S(1)} %get-tuple-element.127), channel_id=1, source_target_pairs={{0,12},{1,13},{2,14},{3,15},{4,0},{5,1},{6,2},{7,3},{8,4},{9,5},{1... | collective-permute-start | bytes 294920 | tf_op jit(solution)/shard_map/ppermute | solution.py:23
  219.9 8.3 %copy-start.8 = (bf16[2,3,4,1,4,5,128]{6,1,5,4,3,2,0:T(4,128)(2,1)S(1)}, bf16[2,3,4,1,4,5,128]{6,1,5,4,3,2,0:T(4,128)(2,1)}, u32[]{:S(2)}) copy-start(bf16[2,3,4,1,4,5,128]{6,1,5,4,3,2,0:T(4,128)(2,1)} %copy.67) | copy-start | bytes 368644
  220.0 8.3 %copy-start.27 = (bf16[2,1,4,1,4,5,128]{6,1,5,4,3,2,0:T(2,128)(2,1)S(1)}, bf16[2,1,4,1,4,5,128]{6,1,5,4,3,2,0:T(2,128)(2,1)}, u32[]{:S(2)}) copy-start(bf16[2,1,4,1,4,5,128]{6,1,5,4,3,2,0:T(2,128)(2,1)} %copy.66) | copy-start | bytes 122884
  220.9 7.7 %copy-start.9 = (bf16[2,3,4,1,4,5,128]{6,1,5,4,3,2,0:T(4,128)(2,1)S(1)}, bf16[2,3,4,1,4,5,128]{6,1,5,4,3,2,0:T(4,128)(2,1)}, u32[]{:S(2)}) copy-start(bf16[2,3,4,1,4,5,128]{6,1,5,4,3,2,0:T(4,128)(2,1)} %copy.70) | copy-start | bytes 368644
  220.9 7.7 %copy-start.28 = (bf16[2,1,4,1,4,5,128]{6,1,5,4,3,2,0:T(2,128)(2,1)S(1)}, bf16[2,1,4,1,4,5,128]{6,1,5,4,3,2,0:T(2,128)(2,1)}, u32[]{:S(2)}) copy-start(bf16[2,1,4,1,4,5,128]{6,1,5,4,3,2,0:T(2,128)(2,1)} %copy.71) | copy-start | bytes 122884
  221.0 10.5 %collective-permute-start.25 = (bf16[256,768]{1,0:T(8,128)(2,1)S(1)}, bf16[256,768]{1,0:T(8,128)(2,1)S(1)}, u32[]{:S(2)}, u32[]{:S(2)}) collective-permute-start(bf16[256,768]{1,0:T(8,128)(2,1)S(1)} %get-tuple-element.150), channel_id=1, source_target_pairs={{0,3},{1,0},{2,1},{3,2},{4,7},{5,4},{6,5},{7,6},{8,11},{9,8},{10,9... | collective-permute-start | bytes 1179656 | tf_op jit(solution)/shard_map/ppermute | solution.py:23
  223.4 11.5 %collective-permute-start.24 = (bf16[256,768]{1,0:T(8,128)(2,1)S(1)}, bf16[256,768]{1,0:T(8,128)(2,1)S(1)}, u32[]{:S(2)}, u32[]{:S(2)}) collective-permute-start(bf16[256,768]{1,0:T(8,128)(2,1)S(1)} %get-tuple-element.149), channel_id=1, source_target_pairs={{0,2},{1,3},{2,0},{3,1},{4,6},{5,7},{6,4},{7,5},{8,10},{9,11},{10,... | collective-permute-start | bytes 1179656 | tf_op jit(solution)/shard_map/ppermute | solution.py:23
  225.3 20.9 %collective-permute-start.23 = (bf16[256,768]{1,0:T(8,128)(2,1)S(1)}, bf16[256,768]{1,0:T(8,128)(2,1)S(1)}, u32[]{:S(2)}, u32[]{:S(2)}) collective-permute-start(bf16[256,768]{1,0:T(8,128)(2,1)S(1)} %get-tuple-element.148), channel_id=1, source_target_pairs={{0,1},{1,2},{2,3},{3,0},{4,5},{5,6},{6,7},{7,4},{8,9},{9,10},{10,1... | collective-permute-start | bytes 1179656 | tf_op jit(solution)/shard_map/ppermute | solution.py:23
  231.5 14.7 %copy-start.19 = (bf16[256,768]{1,0:T(8,128)(2,1)}, bf16[256,768]{1,0:T(8,128)(2,1)S(1)}, u32[]{:S(2)}) copy-start(bf16[256,768]{1,0:T(8,128)(2,1)S(1)} %collective-permute-done.25) | copy-start | bytes 1179652
  234.8 11.4 %copy-start.20 = (bf16[256,768]{1,0:T(8,128)(2,1)}, bf16[256,768]{1,0:T(8,128)(2,1)S(1)}, u32[]{:S(2)}) copy-start(bf16[256,768]{1,0:T(8,128)(2,1)S(1)} %collective-permute-done.24) | copy-start | bytes 1179652
  246.2 0.8 copy-start.21
  254.0 3.1 %copy-start.14 = (bf16[16,8,5,128]{3,1,2,0:T(8,128)(2,1)S(1)}, bf16[16,8,5,128]{3,1,2,0:T(8,128)(2,1)}, u32[]{:S(2)}) copy-start(bf16[16,8,5,128]{3,1,2,0:T(8,128)(2,1)} %copy.116) | copy-start | bytes 491524
  254.0 3.1 %copy-start.33 = (s32[256]{0:T(256)S(1)}, s32[256]{0:T(256)}, u32[]{:S(2)}) copy-start(s32[256]{0:T(256)} %add.230) | copy-start | bytes 3076
  257.5 19.3 %collective-permute-start.28 = (f32[64,640]{1,0:T(8,128)S(1)}, f32[64,640]{1,0:T(8,128)S(1)}, u32[]{:S(2)}, u32[]{:S(2)}) collective-permute-start(f32[64,640]{1,0:T(8,128)S(1)} %get-tuple-element.131), channel_id=1, source_target_pairs={{0,12},{1,13},{2,14},{3,15},{4,0},{5,1},{6,2},{7,3},{8,4},{9,5},{1... | collective-permute-start | bytes 491528 | tf_op jit(solution)/shard_map/ppermute | solution.py:23
  265.2 16.6 %collective-permute-start.27 = (f32[64,640]{1,0:T(8,128)S(1)}, f32[64,640]{1,0:T(8,128)S(1)}, u32[]{:S(2)}, u32[]{:S(2)}) collective-permute-start(f32[64,640]{1,0:T(8,128)S(1)} %get-tuple-element.132), channel_id=1, source_target_pairs={{0,8},{1,9},{2,10},{3,11},{4,12},{5,13},{6,14},{7,15},{8,0},{9,1},... | collective-permute-start | bytes 491528 | tf_op jit(solution)/shard_map/ppermute | solution.py:23
  269.7 25.9 %collective-permute-start.26 = (f32[64,640]{1,0:T(8,128)S(1)}, f32[64,640]{1,0:T(8,128)S(1)}, u32[]{:S(2)}, u32[]{:S(2)}) collective-permute-start(f32[64,640]{1,0:T(8,128)S(1)} %get-tuple-element.130), channel_id=1, source_target_pairs={{0,4},{1,5},{2,6},{3,7},{4,8},{5,9},{6,10},{7,11},{8,12},{9,13},{1... | collective-permute-start | bytes 491528 | tf_op jit(solution)/shard_map/ppermute | solution.py:23
  276.9 19.2 %copy-start.6 = (bf16[64,6,128]{2,0,1:T(8,128)(2,1)S(1)}, bf16[64,6,128]{2,0,1:T(8,128)(2,1)}, u32[]{:S(2)}) copy-start(bf16[64,6,128]{2,0,1:T(8,128)(2,1)} %param.34) | copy-start | bytes 294916

commit v7 on v3

--- a/solution.py
+++ b/solution.py
@@ -90,10 +90,8 @@
     kz = lax.iota(jnp.int32, cz)[:, None]
     got_ids = ((((zpos - kz) % cz) * CY + ypos) * shell_count + node).reshape(-1)
     out_ids = ((((zpos + kz) % cz) * CY + ypos) * shell_count + node).reshape(-1)
-    maps_to = [wall_local] + [chord_shift(wall_local, 0, -k) for k in range(1, CY)]
-    maps_from = jnp.concatenate(over_y(wall_local))
-    pick_hits = [(m[:, None] == got_ids[None, :]).astype(jnp.bfloat16) for m in maps_to]
-    load_hit = (out_ids[:, None] == maps_from[None, :]).astype(jnp.bfloat16)
+    tag = jnp.concatenate([wall_local // 32, wall_local % 32]).astype(jnp.bfloat16)
+    tag = jnp.zeros((16, NV * width), jnp.bfloat16).at[0, : 2 * wall_count].set(tag)
     fluid = jnp.einsum(
         "abmn,abnr->abmr", diag_inv, adj_rhs, preferred_element_type=jnp.float32
     ).astype(jnp.bfloat16)
@@ -106,6 +104,21 @@
         sent = jnp.einsum("abdmn,abnr->abdmr", face_jac, fluid, preferred_element_type=jnp.float32)
         sent = (sent * weights).astype(jnp.bfloat16)
         low_span, high_span, low_chord, high_chord = face_terms(sent)
+        wall_rows = fluid.reshape(rows, cols, 4, 4, 4, NV, width)[:, :, :, :, 0].reshape(
+            wall_count, NV * width
+        )
+        if step == 1:
+            arrived = over_y(jnp.concatenate([wall_rows, tag]))
+            maps = [wall_local]
+            for a in arrived[1:]:
+                code = a[wall_count].astype(jnp.float32)
+                maps.append((code[:wall_count] * 32 + code[wall_count : 2 * wall_count]).astype(jnp.int32))
+            row_group = jnp.concatenate([wall_rows] + [a[:wall_count] for a in arrived[1:]])
+            maps_to = [maps[0]] + [maps[CY - k] for k in range(1, CY)]
+            pick_hits = [(m[:, None] == got_ids[None, :]).astype(jnp.bfloat16) for m in maps_to]
+            load_hit = (out_ids[:, None] == jnp.concatenate(maps)[None, :]).astype(jnp.bfloat16)
+        else:
+            row_group = jnp.concatenate(over_y(wall_rows))
         column = jnp.concatenate(over_z(shell.reshape(shell_count, sdof * width)))
         served = [
             jnp.dot(h, column, preferred_element_type=jnp.float32).astype(jnp.bfloat16)
@@ -117,10 +130,6 @@
         wall_in = jnp.einsum(
             "sv,wsr->wvr", couple, picked.reshape(wall_count, sdof, width), precision=high
         )
-        wall_rows = fluid.reshape(rows, cols, 4, 4, 4, NV, width)[:, :, :, :, 0].reshape(
-            wall_count, NV * width
-        )
-        row_group = jnp.concatenate(over_y(wall_rows))
         partial = jnp.dot(load_hit, row_group, preferred_element_type=jnp.float32)
         partial = partial.reshape(cz, shell_count, NV * width)
         summed = partial[0]

time: 284 us -> 276 us (0.972)
  waiting for transfers between devices: 47.5 us -> 79.1 us
  starting transfers between devices: 157 us -> 132 us
  local copies, waits for them, and re-layouts: 43.6 us -> 31.8 us
    ppermute x27 -> x24, waiting for transfers between devices: 40.6 us -> 72.7 us  [chord_shift(): return lax.ppermute(block, 'chord', route)]
    ppermute x27 -> x24, starting transfers between devices: 134 us -> 112 us  [chord_shift(): return lax.ppermute(block, 'chord', route)]
    unnamed x61 -> x77, local copies, waits for them, and re-layouts: 7.96 us -> 6.42 us
  transfers between devices with their start and end apart: 35 -> 32, of which waited for: 8 -> 13; matrix products, arithmetic and copies ran while one was open for 19% -> 12% of each run, Pallas kernels for 0% -> 0%
where the time goes in v7:
time: 276 us; the launch traced here: 275 us
  starting transfers between devices  132 us (48%)
  waiting for transfers between devices  79.1 us (29%)
  local copies, waits for them, and re-layouts  31.8 us (12%)
  matrix products  21.2 us (8%)
  other arithmetic  8.73 us (3%)
    ppermute x24, starting transfers between devices, chord_shift(): return lax.ppermute(block, 'chord', route)  112 us
    ppermute x24, waiting for transfers between devices, chord_shift(): return lax.ppermute(block, 'chord', route)  72.7 us
    ppermute x8, starting transfers between devices, passed_along(): return lax.ppermute(block, axis, route)  20 us
    dot_general x8, matrix products, per_device(): jnp.dot(h, column, preferred_element_type=jnp.float32).astype(jnp.bfloat16)  6.75 us
    unnamed x77, local copies, waits for them, and re-layouts  6.42 us
    ppermute x8, waiting for transfers between devices, passed_along(): return lax.ppermute(block, axis, route)  6.39 us
  transfers between devices with their start and end apart: 32, of which 13 were waited for; matrix products, arithmetic and copies ran while one was open for 12% of the time, Pallas kernels for 0%

profile of v7, /device:TPU:1, one launch (start us, length us, event | category | flops | bytes accessed | tf_op | source)
XLA Modules:
  0.0 274.7 jit_solution(4690045805231501453)
XLA Ops:
  0.6 1.0 copy.51
  1.7 1.3 convolution_convert_fusion.13
  3.6 9.6 %collective-permute-start.4 = (bf16[64,768]{1,0:T(8,128)(2,1)}, bf16[64,768]{1,0:T(8,128)(2,1)}, u32[]{:S(2)}, u32[]{:S(2)}) collective-permute-start(bf16[64,768]{1,0:T(8,128)(2,1)} %get-tuple-element.141), channel_id=1, source_target_pairs={{0,4},{1,5},{2,6},{3,7},{4,8},{5,9},{6,10},{7,11},{8,12},{9,13},{1... | collective-permute-start | bytes 294920 | tf_op jit(solution)/shard_map/ppermute | solution.py:23
  13.3 10.6 %collective-permute-start.5 = (bf16[64,768]{1,0:T(8,128)(2,1)}, bf16[64,768]{1,0:T(8,128)(2,1)}, u32[]{:S(2)}, u32[]{:S(2)}) collective-permute-start(bf16[64,768]{1,0:T(8,128)(2,1)} %get-tuple-element.141), channel_id=1, source_target_pairs={{0,8},{1,9},{2,10},{3,11},{4,12},{5,13},{6,14},{7,15},{8,0},{9,1},... | collective-permute-start | bytes 294920 | tf_op jit(solution)/shard_map/ppermute | solution.py:23
  24.6 1.9 convolution_convert_fusion.2
  27.9 3.8 %collective-permute-start = (bf16[1,4,80,128]{3,2,1,0:T(8,128)(2,1)}, bf16[1,4,80,128]{3,2,1,0:T(8,128)(2,1)}, u32[]{:S(2)}, u32[]{:S(2)}) collective-permute-start(bf16[1,4,80,128]{3,2,1,0:T(8,128)(2,1)} %get-tuple-element.159), channel_id=1, source_target_pairs={{0,16},{16,32},{32,48},{48,64},{64,80},{80,96},{96,112},{112,128},... | collective-permute-start | bytes 245768 | tf_op jit(solution)/shard_map/ppermute | solution.py:14
  32.5 3.8 %collective-permute-start.2 = (bf16[2,1,80,128]{3,2,1,0:T(8,128)(2,1)}, bf16[2,1,80,128]{3,2,1,0:T(8,128)(2,1)}, u32[]{:S(2)}, u32[]{:S(2)}) collective-permute-start(bf16[2,1,80,128]{3,2,1,0:T(8,128)(2,1)} %slice.664), channel_id=1, source_target_pairs={{0,1},{1,2},{2,3},{3,4},{4,5},{5,6},{6,7},{7,8},{8,9},{9,10},{10,1... | collective-permute-start | bytes 122888 | tf_op jit(solution)/shard_map/ppermute | solution.py:14
  36.9 1.3 collective-permute-start.3
  40.5 1.6 copy.38
  42.1 1.1 copy.126
  46.3 1.3 add.261
  47.6 11.5 %collective-permute-start.6 = (bf16[64,768]{1,0:T(8,128)(2,1)}, bf16[64,768]{1,0:T(8,128)(2,1)S(1)}, u32[]{:S(2)}, u32[]{:S(2)}) collective-permute-start(bf16[64,768]{1,0:T(8,128)(2,1)} %get-tuple-element.141), channel_id=1, source_target_pairs={{0,12},{1,13},{2,14},{3,15},{4,0},{5,1},{6,2},{7,3},{8,4},{9,5},{1... | collective-permute-start | bytes 294920 | tf_op jit(solution)/shard_map/ppermute | solution.py:23
  60.0 2.1 collective-permute-start.1
  63.1 1.9 collective-permute-start.11
  65.9 1.1 add_dynamic-update-slice_fusion.1
  67.0 3.2 %collective-permute-done.1 = bf16[1,4,80,128]{3,2,1,0:T(8,128)(2,1)S(1)} collective-permute-done((bf16[1,4,80,128]{3,2,1,0:T(8,128)(2,1)}, bf16[1,4,80,128]{3,2,1,0:T(8,128)(2,1)S(1)}, u32[]{:S(2)}, u32[]{:S(2)}) %collective-permute-start.1) | collective-permute-done | bytes 81952 | tf_op jit(solution)/shard_map/ppermute | solution.py:14
  70.2 1.9 collective-permute-start.9
  73.0 1.9 collective-permute-start.7
  77.8 5.1 %collective-permute-start.12 = (bf16[128,768]{1,0:T(8,128)(2,1)}, bf16[128,768]{1,0:T(8,128)(2,1)}, u32[]{:S(2)}, u32[]{:S(2)}) collective-permute-start(bf16[128,768]{1,0:T(8,128)(2,1)} %convolution_convert_fusion.7), channel_id=1, source_target_pairs={{0,3},{1,0},{2,1},{3,2},{4,7},{5,4},{6,5},{7,6},{8,11},{9,8},{10,9... | collective-permute-start | bytes 589832 | tf_op jit(solution)/shard_map/ppermute | solution.py:23
  83.9 1.9 collective-permute-start.10
  86.5 1.9 collective-permute-start.19
  88.4 5.9 %collective-permute-start.18 = (f32[64,640]{1,0:T(8,128)S(1)}, f32[64,640]{1,0:T(8,128)S(1)}, u32[]{:S(2)}, u32[]{:S(2)}) collective-permute-start(f32[64,640]{1,0:T(8,128)S(1)} %get-tuple-element.147), channel_id=1, source_target_pairs={{0,8},{1,9},{2,10},{3,11},{4,12},{5,13},{6,14},{7,15},{8,0},{9,1},... | collective-permute-start | bytes 491528 | tf_op jit(solution)/shard_map/ppermute | solution.py:23
  94.3 5.0 %collective-permute-start.17 = (f32[64,640]{1,0:T(8,128)S(1)}, f32[64,640]{1,0:T(8,128)S(1)}, u32[]{:S(2)}, u32[]{:S(2)}) collective-permute-start(f32[64,640]{1,0:T(8,128)S(1)} %get-tuple-element.145), channel_id=1, source_target_pairs={{0,4},{1,5},{2,6},{3,7},{4,8},{5,9},{6,10},{7,11},{8,12},{9,13},{1... | collective-permute-start | bytes 491528 | tf_op jit(solution)/shard_map/ppermute | solution.py:23
  100.2 22.4 %collective-permute-done.19 = f32[64,640]{1,0:T(8,128)S(1)} collective-permute-done((f32[64,640]{1,0:T(8,128)S(1)}, f32[64,640]{1,0:T(8,128)S(1)}, u32[]{:S(2)}, u32[]{:S(2)}) %collective-permute-start.19) | collective-permute-done | bytes 163872 | tf_op jit(solution)/shard_map/ppermute | solution.py:23
  122.7 2.6 collective-permute-start.8
  125.3 1.6 collective-permute-done.17
  127.6 1.7 reshape.945
  129.2 3.0 %collective-permute-done.8 = bf16[128,768]{1,0:T(8,128)(2,1)} collective-permute-done((bf16[128,768]{1,0:T(8,128)(2,1)}, bf16[128,768]{1,0:T(8,128)(2,1)}, u32[]{:S(2)}, u32[]{:S(2)}) %collective-permute-start.8) | collective-permute-done | bytes 196640 | tf_op jit(solution)/shard_map/ppermute | solution.py:23
  132.2 2.2 fusion.12
  134.4 1.9 copy.55
  136.3 2.0 copy.56
  138.3 1.7 convolution_negate_fusion.1
  142.9 3.0 %collective-permute-start.13 = (bf16[1,4,80,128]{3,2,1,0:T(8,128)(2,1)S(1)}, bf16[1,4,80,128]{3,2,1,0:T(8,128)(2,1)S(1)}, u32[]{:S(2)}, u32[]{:S(2)}) collective-permute-start(bf16[1,4,80,128]{3,2,1,0:T(8,128)(2,1)S(1)} %get-tuple-element.153), channel_id=1, source_target_pairs={{0,16},{16,32},{32,48},{48,64},{64,80},{80,96},{96,112},{112,128},... | collective-permute-start | bytes 245768 | tf_op jit(solution)/shard_map/ppermute | solution.py:14
  145.9 2.9 %collective-permute-start.15 = (bf16[2,1,80,128]{3,2,1,0:T(8,128)(2,1)S(1)}, bf16[2,1,80,128]{3,2,1,0:T(8,128)(2,1)S(1)}, u32[]{:S(2)}, u32[]{:S(2)}) collective-permute-start(bf16[2,1,80,128]{3,2,1,0:T(8,128)(2,1)S(1)} %slice.688), channel_id=1, source_target_pairs={{0,1},{1,2},{2,3},{3,4},{4,5},{5,6},{6,7},{7,8},{8,9},{9,10},{10,1... | collective-permute-start | bytes 122888 | tf_op jit(solution)/shard_map/ppermute | solution.py:14
  148.8 1.3 collective-permute-start.16
  150.1 1.0 fusion.88
  151.8 4.0 %collective-permute-start.28 = (bf16[128,640]{1,0:T(8,128)(2,1)S(1)}, bf16[128,640]{1,0:T(8,128)(2,1)S(1)}, u32[]{:S(2)}, u32[]{:S(2)}) collective-permute-start(bf16[128,640]{1,0:T(8,128)(2,1)S(1)} %bitcast.160), channel_id=1, source_target_pairs={{0,3},{1,0},{2,1},{3,2},{4,7},{5,4},{6,5},{7,6},{8,11},{9,8},{10,9... | collective-permute-start | bytes 491528 | tf_op jit(solution)/shard_map/ppermute | solution.py:23
  155.9 4.0 %collective-permute-start.27 = (bf16[128,640]{1,0:T(8,128)(2,1)S(1)}, bf16[128,640]{1,0:T(8,128)(2,1)S(1)}, u32[]{:S(2)}, u32[]{:S(2)}) collective-permute-start(bf16[128,640]{1,0:T(8,128)(2,1)S(1)} %bitcast.161), channel_id=1, source_target_pairs={{0,2},{1,3},{2,0},{3,1},{4,6},{5,7},{6,4},{7,5},{8,10},{9,11},{10,... | collective-permute-start | bytes 491528 | tf_op jit(solution)/shard_map/ppermute | solution.py:23
  161.0 1.9 collective-permute-start.26
  163.1 1.9 collective-permute-start.14
  165.9 3.2 %collective-permute-done.14 = bf16[1,4,80,128]{3,2,1,0:T(8,128)(2,1)S(1)} collective-permute-done((bf16[1,4,80,128]{3,2,1,0:T(8,128)(2,1)S(1)}, bf16[1,4,80,128]{3,2,1,0:T(8,128)(2,1)S(1)}, u32[]{:S(2)}, u32[]{:S(2)}) %collective-permute-start.14) | collective-permute-done | bytes 81952 | tf_op jit(solution)/shard_map/ppermute | solution.py:14
  170.1 6.4 %collective-permute-start.31 = (f32[64,640]{1,0:T(8,128)S(1)}, f32[64,640]{1,0:T(8,128)S(1)}, u32[]{:S(2)}, u32[]{:S(2)}) collective-permute-start(f32[64,640]{1,0:T(8,128)S(1)} %get-tuple-element.143), channel_id=1, source_target_pairs={{0,12},{1,13},{2,14},{3,15},{4,0},{5,1},{6,2},{7,3},{8,4},{9,5},{1... | collective-permute-start | bytes 491528 | tf_op jit(solution)/shard_map/ppermute | solution.py:23
  176.6 7.3 %collective-permute-start.30 = (f32[64,640]{1,0:T(8,128)S(1)}, f32[64,640]{1,0:T(8,128)S(1)}, u32[]{:S(2)}, u32[]{:S(2)}) collective-permute-start(f32[64,640]{1,0:T(8,128)S(1)} %get-tuple-element.144), channel_id=1, source_target_pairs={{0,8},{1,9},{2,10},{3,11},{4,12},{5,13},{6,14},{7,15},{8,0},{9,1},... | collective-permute-start | bytes 491528 | tf_op jit(solution)/shard_map/ppermute | solution.py:23
  183.8 4.0 %collective-permute-start.29 = (f32[64,640]{1,0:T(8,128)S(1)}, f32[64,640]{1,0:T(8,128)S(1)}, u32[]{:S(2)}, u32[]{:S(2)}) collective-permute-start(f32[64,640]{1,0:T(8,128)S(1)} %get-tuple-element.142), channel_id=1, source_target_pairs={{0,4},{1,5},{2,6},{3,7},{4,8},{5,9},{6,10},{7,11},{8,12},{9,13},{1... | collective-permute-start | bytes 491528 | tf_op jit(solution)/shard_map/ppermute | solution.py:23
  188.2 10.8 %collective-permute-done.31 = f32[64,640]{1,0:T(8,128)S(1)} collective-permute-done((f32[64,640]{1,0:T(8,128)S(1)}, f32[64,640]{1,0:T(8,128)S(1)}, u32[]{:S(2)}, u32[]{:S(2)}) %collective-permute-start.31) | collective-permute-done | bytes 163872 | tf_op jit(solution)/shard_map/ppermute | solution.py:23
  199.0 2.8 %collective-permute-done.30 = f32[64,640]{1,0:T(8,128)S(1)} collective-permute-done((f32[64,640]{1,0:T(8,128)S(1)}, f32[64,640]{1,0:T(8,128)S(1)}, u32[]{:S(2)}, u32[]{:S(2)}) %collective-permute-start.30) | collective-permute-done | bytes 163872 | tf_op jit(solution)/shard_map/ppermute | solution.py:23
  201.8 7.9 %collective-permute-done.29 = f32[64,640]{1,0:T(8,128)S(1)} collective-permute-done((f32[64,640]{1,0:T(8,128)S(1)}, f32[64,640]{1,0:T(8,128)S(1)}, u32[]{:S(2)}, u32[]{:S(2)}) %collective-permute-start.29) | collective-permute-done | bytes 163872 | tf_op jit(solution)/shard_map/ppermute | solution.py:23
  210.5 1.6 reshape.949
  212.1 1.3 fusion.86
  213.5 1.1 convert_subtract_fusion
  215.3 4.7 %collective-permute-start.20 = (bf16[64,768]{1,0:T(8,128)(2,1)S(1)}, bf16[64,768]{1,0:T(8,128)(2,1)S(1)}, u32[]{:S(2)}, u32[]{:S(2)}) collective-permute-start(bf16[64,768]{1,0:T(8,128)(2,1)S(1)} %get-tuple-element.139), channel_id=1, source_target_pairs={{0,4},{1,5},{2,6},{3,7},{4,8},{5,9},{6,10},{7,11},{8,12},{9,13},{1... | collective-permute-start | bytes 294920 | tf_op jit(solution)/shard_map/ppermute | solution.py:23
  220.3 4.9 %collective-permute-start.21 = (bf16[64,768]{1,0:T(8,128)(2,1)S(1)}, bf16[64,768]{1,0:T(8,128)(2,1)S(1)}, u32[]{:S(2)}, u32[]{:S(2)}) collective-permute-start(bf16[64,768]{1,0:T(8,128)(2,1)S(1)} %get-tuple-element.139), channel_id=1, source_target_pairs={{0,8},{1,9},{2,10},{3,11},{4,12},{5,13},{6,14},{7,15},{8,0},{9,1},... | collective-permute-start | bytes 294920 | tf_op jit(solution)/shard_map/ppermute | solution.py:23
  225.2 6.7 %collective-permute-start.22 = (bf16[64,768]{1,0:T(8,128)(2,1)S(1)}, bf16[64,768]{1,0:T(8,128)(2,1)S(1)}, u32[]{:S(2)}, u32[]{:S(2)}) collective-permute-start(bf16[64,768]{1,0:T(8,128)(2,1)S(1)} %get-tuple-element.139), channel_id=1, source_target_pairs={{0,12},{1,13},{2,14},{3,15},{4,0},{5,1},{6,2},{7,3},{8,4},{9,5},{1... | collective-permute-start | bytes 294920 | tf_op jit(solution)/shard_map/ppermute | solution.py:23
  232.0 4.8 %collective-permute-done.21 = bf16[64,768]{1,0:T(8,128)(2,1)S(1)} collective-permute-done((bf16[64,768]{1,0:T(8,128)(2,1)S(1)}, bf16[64,768]{1,0:T(8,128)(2,1)S(1)}, u32[]{:S(2)}, u32[]{:S(2)}) %collective-permute-start.21) | collective-permute-done | bytes 98336 | tf_op jit(solution)/shard_map/ppermute | solution.py:23
  236.7 10.3 %collective-permute-done.22 = bf16[64,768]{1,0:T(8,128)(2,1)S(1)} collective-permute-done((bf16[64,768]{1,0:T(8,128)(2,1)S(1)}, bf16[64,768]{1,0:T(8,128)(2,1)S(1)}, u32[]{:S(2)}, u32[]{:S(2)}) %collective-permute-start.22) | collective-permute-done | bytes 98336 | tf_op jit(solution)/shard_map/ppermute | solution.py:23
  247.9 3.7 %collective-permute-start.25 = (bf16[128,768]{1,0:T(8,128)(2,1)S(1)}, bf16[128,768]{1,0:T(8,128)(2,1)S(1)}, u32[]{:S(2)}, u32[]{:S(2)}) collective-permute-start(bf16[128,768]{1,0:T(8,128)(2,1)S(1)} %convolution_convert_fusion.3), channel_id=1, source_target_pairs={{0,3},{1,0},{2,1},{3,2},{4,7},{5,4},{6,5},{7,6},{8,11},{9,8},{10,9... | collective-permute-start | bytes 589832 | tf_op jit(solution)/shard_map/ppermute | solution.py:23
  251.6 2.1 collective-permute-start.24
  253.7 2.3 collective-permute-start.23
  257.4 3.3 %collective-permute-done.24 = bf16[128,768]{1,0:T(8,128)(2,1)S(1)} collective-permute-done((bf16[128,768]{1,0:T(8,128)(2,1)S(1)}, bf16[128,768]{1,0:T(8,128)(2,1)S(1)}, u32[]{:S(2)}, u32[]{:S(2)}) %collective-permute-start.24) | collective-permute-done | bytes 196640 | tf_op jit(solution)/shard_map/ppermute | solution.py:23
  260.7 5.3 %collective-permute-done.23 = bf16[128,768]{1,0:T(8,128)(2,1)S(1)} collective-permute-done((bf16[128,768]{1,0:T(8,128)(2,1)S(1)}, bf16[128,768]{1,0:T(8,128)(2,1)S(1)}, u32[]{:S(2)}, u32[]{:S(2)}) %collective-permute-start.23) | collective-permute-done | bytes 196640 | tf_op jit(solution)/shard_map/ppermute | solution.py:23
  267.0 1.9 copy.74
  269.0 2.0 copy.75
  271.0 1.7 convolution_negate_fusion
  273.2 1.5 fusion.2
  (187 shorter events, 31.3 us)
Async XLA Ops:
  0.6 24.0 %copy-start = (bf16[2,4,320,320]{3,2,1,0:T(8,128)(2,1)S(1)}, bf16[2,4,320,320]{3,2,1,0:T(8,128)(2,1)}, u32[]{:S(2)}) copy-start(bf16[2,4,320,320]{3,2,1,0:T(8,128)(2,1)} %param.31) | copy-start | bytes 4915204
  3.6 69.3 %collective-permute-start.4 = (bf16[64,768]{1,0:T(8,128)(2,1)}, bf16[64,768]{1,0:T(8,128)(2,1)}, u32[]{:S(2)}, u32[]{:S(2)}) collective-permute-start(bf16[64,768]{1,0:T(8,128)(2,1)} %get-tuple-element.141), channel_id=1, source_target_pairs={{0,4},{1,5},{2,6},{3,7},{4,8},{5,9},{6,10},{7,11},{8,12},{9,13},{1... | collective-permute-start | bytes 294920 | tf_op jit(solution)/shard_map/ppermute | solution.py:23
  13.3 62.6 %collective-permute-start.5 = (bf16[64,768]{1,0:T(8,128)(2,1)}, bf16[64,768]{1,0:T(8,128)(2,1)}, u32[]{:S(2)}, u32[]{:S(2)}) collective-permute-start(bf16[64,768]{1,0:T(8,128)(2,1)} %get-tuple-element.141), channel_id=1, source_target_pairs={{0,8},{1,9},{2,10},{3,11},{4,12},{5,13},{6,14},{7,15},{8,0},{9,1},... | collective-permute-start | bytes 294920 | tf_op jit(solution)/shard_map/ppermute | solution.py:23
  24.6 1.9 copy-start.2
  27.2 11.6 %copy-start.28 = (s32[2,4,16]{2,1,0:T(4,128)S(1)}, s32[2,4,16]{2,1,0:T(4,128)}, u32[]{:S(2)}) copy-start(s32[2,4,16]{2,1,0:T(4,128)} %param.34) | copy-start | bytes 1540
  27.9 35.1 %collective-permute-start = (bf16[1,4,80,128]{3,2,1,0:T(8,128)(2,1)}, bf16[1,4,80,128]{3,2,1,0:T(8,128)(2,1)}, u32[]{:S(2)}, u32[]{:S(2)}) collective-permute-start(bf16[1,4,80,128]{3,2,1,0:T(8,128)(2,1)} %get-tuple-element.159), channel_id=1, source_target_pairs={{0,16},{16,32},{32,48},{48,64},{64,80},{80,96},{96,112},{112,128},... | collective-permute-start | bytes 245768 | tf_op jit(solution)/shard_map/ppermute | solution.py:14
  31.7 4.5 %copy-start.8 = (bf16[2,4,80,128]{3,2,1,0:T(8,128)(2,1)}, bf16[2,4,80,128]{3,2,1,0:T(8,128)(2,1)S(1)}, u32[]{:S(2)}) copy-start(bf16[2,4,80,128]{3,2,1,0:T(8,128)(2,1)S(1)} %get-tuple-element.154) | copy-start | bytes 491524
  31.8 5.1 %copy-start.10 = (bf16[2,4,80,128]{3,2,1,0:T(8,128)(2,1)}, bf16[2,4,80,128]{3,2,1,0:T(8,128)(2,1)S(1)}, u32[]{:S(2)}) copy-start(bf16[2,4,80,128]{3,2,1,0:T(8,128)(2,1)S(1)} %get-tuple-element.155) | copy-start | bytes 491524
  32.5 15.2 %collective-permute-start.2 = (bf16[2,1,80,128]{3,2,1,0:T(8,128)(2,1)}, bf16[2,1,80,128]{3,2,1,0:T(8,128)(2,1)}, u32[]{:S(2)}, u32[]{:S(2)}) collective-permute-start(bf16[2,1,80,128]{3,2,1,0:T(8,128)(2,1)} %slice.664), channel_id=1, source_target_pairs={{0,1},{1,2},{2,3},{3,4},{4,5},{5,6},{6,7},{7,8},{8,9},{9,10},{10,1... | collective-permute-start | bytes 122888 | tf_op jit(solution)/shard_map/ppermute | solution.py:14
  36.9 23.1 %collective-permute-start.3 = (bf16[2,1,80,128]{3,2,1,0:T(8,128)(2,1)}, bf16[2,1,80,128]{3,2,1,0:T(8,128)(2,1)}, u32[]{:S(2)}, u32[]{:S(2)}) collective-permute-start(bf16[2,1,80,128]{3,2,1,0:T(8,128)(2,1)} %slice.669), channel_id=1, source_target_pairs={{1,0},{2,1},{3,2},{4,3},{5,4},{6,5},{7,6},{8,7},{9,8},{10,9},{11,1... | collective-permute-start | bytes 122888 | tf_op jit(solution)/shard_map/ppermute | solution.py:14
  39.1 3.0 %copy-start.11 = (bf16[2,4,80,128]{3,2,1,0:T(8,128)(2,1)S(1)}, bf16[2,4,80,128]{3,2,1,0:T(8,128)(2,1)}, u32[]{:S(2)}) copy-start(bf16[2,4,80,128]{3,2,1,0:T(8,128)(2,1)} %copy-done.10) | copy-start | bytes 491524
  39.1 0.7 copy-start.14
  39.1 3.0 %copy-start.9 = (bf16[2,4,80,128]{3,2,1,0:T(8,128)(2,1)S(1)}, bf16[2,4,80,128]{3,2,1,0:T(8,128)(2,1)}, u32[]{:S(2)}) copy-start(bf16[2,4,80,128]{3,2,1,0:T(8,128)(2,1)} %copy-done.8) | copy-start | bytes 491524
  42.1 1.1 copy-start.17
  42.1 1.7 copy-start.16
  47.6 22.6 %copy-start.20 = (bf16[144,640]{1,0:T(8,128)(2,1)S(1)}, bf16[144,640]{1,0:T(8,128)(2,1)}, u32[]{:S(2)}) copy-start(bf16[144,640]{1,0:T(8,128)(2,1)} %pad_maximum_fusion) | copy-start | bytes 552964
  47.6 24.5 %copy-start.18 = (bf16[1,4,1,80,128]{4,1,3,2,0:T(4,128)(2,1)S(1)}, bf16[1,4,1,80,128]{4,1,3,2,0:T(4,128)(2,1)}, u32[]{:S(2)}) copy-start(bf16[1,4,1,80,128]{4,1,3,2,0:T(4,128)(2,1)} %copy.41) | copy-start | bytes 245764
  47.6 24.7 %copy-start.12 = (bf16[2,3,4,1,4,5,128]{6,1,5,4,3,2,0:T(4,128)(2,1)S(1)}, bf16[2,3,4,1,4,5,128]{6,1,5,4,3,2,0:T(4,128)(2,1)}, u32[]{:S(2)}) copy-start(bf16[2,3,4,1,4,5,128]{6,1,5,4,3,2,0:T(4,128)(2,1)} %copy.46) | copy-start | bytes 368644
  47.6 29.2 %collective-permute-start.6 = (bf16[64,768]{1,0:T(8,128)(2,1)}, bf16[64,768]{1,0:T(8,128)(2,1)S(1)}, u32[]{:S(2)}, u32[]{:S(2)}) collective-permute-start(bf16[64,768]{1,0:T(8,128)(2,1)} %get-tuple-element.141), channel_id=1, source_target_pairs={{0,12},{1,13},{2,14},{3,15},{4,0},{5,1},{6,2},{7,3},{8,4},{9,5},{1... | collective-permute-start | bytes 294920 | tf_op jit(solution)/shard_map/ppermute | solution.py:23
  60.0 10.2 %collective-permute-start.1 = (bf16[1,4,80,128]{3,2,1,0:T(8,128)(2,1)}, bf16[1,4,80,128]{3,2,1,0:T(8,128)(2,1)S(1)}, u32[]{:S(2)}, u32[]{:S(2)}) collective-permute-start(bf16[1,4,80,128]{3,2,1,0:T(8,128)(2,1)} %get-tuple-element.157), channel_id=1, source_target_pairs={{16,0},{32,16},{48,32},{64,48},{80,64},{96,80},{112,96},{128,112},... | collective-permute-start | bytes 245768 | tf_op jit(solution)/shard_map/ppermute | solution.py:14
  63.1 13.8 %collective-permute-start.11 = (bf16[144,640]{1,0:T(8,128)(2,1)}, bf16[144,640]{1,0:T(8,128)(2,1)S(1)}, u32[]{:S(2)}, u32[]{:S(2)}) collective-permute-start(bf16[144,640]{1,0:T(8,128)(2,1)} %pad_maximum_fusion), channel_id=1, source_target_pairs={{0,1},{1,2},{2,3},{3,0},{4,5},{5,6},{6,7},{7,4},{8,9},{9,10},{10,1... | collective-permute-start | bytes 552968 | tf_op jit(solution)/shard_map/ppermute | solution.py:23
  65.9 6.8 %copy-start.13 = (bf16[2,3,4,1,4,5,128]{6,1,5,4,3,2,0:T(4,128)(2,1)S(1)}, bf16[2,3,4,1,4,5,128]{6,1,5,4,3,2,0:T(4,128)(2,1)}, u32[]{:S(2)}) copy-start(bf16[2,3,4,1,4,5,128]{6,1,5,4,3,2,0:T(4,128)(2,1)} %copy.49) | copy-start | bytes 368644
  70.2 12.8 %collective-permute-start.9 = (bf16[144,640]{1,0:T(8,128)(2,1)S(1)}, bf16[144,640]{1,0:T(8,128)(2,1)S(1)}, u32[]{:S(2)}, u32[]{:S(2)}) collective-permute-start(bf16[144,640]{1,0:T(8,128)(2,1)S(1)} %copy-done.20), channel_id=1, source_target_pairs={{0,2},{1,3},{2,0},{3,1},{4,6},{5,7},{6,4},{7,5},{8,10},{9,11},{10,... | collective-permute-start | bytes 552968 | tf_op jit(solution)/shard_map/ppermute | solution.py:23
  72.2 2.8 %copy-start.4 = (bf16[256,768]{1,0:T(8,128)(2,1)S(1)}, bf16[256,768]{1,0:T(8,128)(2,1)}, u32[]{:S(2)}) copy-start(bf16[256,768]{1,0:T(8,128)(2,1)} %get-tuple-element.140) | copy-start | bytes 1179652
  73.0 12.8 %collective-permute-start.7 = (bf16[144,640]{1,0:T(8,128)(2,1)S(1)}, bf16[144,640]{1,0:T(8,128)(2,1)S(1)}, u32[]{:S(2)}, u32[]{:S(2)}) collective-permute-start(bf16[144,640]{1,0:T(8,128)(2,1)S(1)} %copy-done.20), channel_id=1, source_target_pairs={{0,3},{1,0},{2,1},{3,2},{4,7},{5,4},{6,5},{7,6},{8,11},{9,8},{10,9... | collective-permute-start | bytes 552968 | tf_op jit(solution)/shard_map/ppermute | solution.py:23
  75.8 10.2 %copy-start.15 = (bf16[16,8,5,128]{3,1,2,0:T(8,128)(2,1)S(1)}, bf16[16,8,5,128]{3,1,2,0:T(8,128)(2,1)}, u32[]{:S(2)}) copy-start(bf16[16,8,5,128]{3,1,2,0:T(8,128)(2,1)} %copy-done.14) | copy-start | bytes 491524
  75.8 10.2 %copy-start.31 = (s32[256]{0:T(256)S(1)}, s32[256]{0:T(256)}, u32[]{:S(2)}) copy-start(s32[256]{0:T(256)} %add.261) | copy-start | bytes 3076
  76.8 22.5 %copy-start.5 = (bf16[256,768]{1,0:T(8,128)(2,1)}, bf16[256,768]{1,0:T(8,128)(2,1)S(1)}, u32[]{:S(2)}) copy-start(bf16[256,768]{1,0:T(8,128)(2,1)S(1)} %constant_dynamic-update-slice_fusion) | copy-start | bytes 1179652
  76.9 9.6 %copy-start.22 = (s32[128]{0:T(128)}, s32[128]{0:T(128)S(1)}, u32[]{:S(2)}) copy-start(s32[128]{0:T(128)S(1)} %fusion.102) | copy-start | bytes 1540
  77.8 51.4 %collective-permute-start.12 = (bf16[128,768]{1,0:T(8,128)(2,1)}, bf16[128,768]{1,0:T(8,128)(2,1)}, u32[]{:S(2)}, u32[]{:S(2)}) collective-permute-start(bf16[128,768]{1,0:T(8,128)(2,1)} %convolution_convert_fusion.7), channel_id=1, source_target_pairs={{0,3},{1,0},{2,1},{3,2},{4,7},{5,4},{6,5},{7,6},{8,11},{9,8},{10,9... | collective-permute-start | bytes 589832 | tf_op jit(solution)/shard_map/ppermute | solution.py:23
  83.0 3.0 %copy-start.24 = (s32[128]{0:T(128)}, s32[128]{0:T(128)S(1)}, u32[]{:S(2)}) copy-start(s32[128]{0:T(128)S(1)} %fusion.104) | copy-start | bytes 1540
  83.9 45.3 %collective-permute-start.10 = (bf16[128,768]{1,0:T(8,128)(2,1)}, bf16[128,768]{1,0:T(8,128)(2,1)}, u32[]{:S(2)}, u32[]{:S(2)}) collective-permute-start(bf16[128,768]{1,0:T(8,128)(2,1)} %convolution_convert_fusion.8), channel_id=1, source_target_pairs={{0,2},{1,3},{2,0},{3,1},{4,6},{5,7},{6,4},{7,5},{8,10},{9,11},{10,... | collective-permute-start | bytes 589832 | tf_op jit(solution)/shard_map/ppermute | solution.py:23
  85.9 13.4 %copy-start.26 = (s32[128]{0:T(128)}, s32[128]{0:T(128)S(1)}, u32[]{:S(2)}) copy-start(s32[128]{0:T(128)S(1)} %fusion.106) | copy-start | bytes 1540
  86.5 36.2 %collective-permute-start.19 = (f32[64,640]{1,0:T(8,128)S(1)}, f32[64,640]{1,0:T(8,128)S(1)}, u32[]{:S(2)}, u32[]{:S(2)}) collective-permute-start(f32[64,640]{1,0:T(8,128)S(1)} %get-tuple-element.146), channel_id=1, source_target_pairs={{0,12},{1,13},{2,14},{3,15},{4,0},{5,1},{6,2},{7,3},{8,4},{9,5},{1... | collective-permute-start | bytes 491528 | tf_op jit(solution)/shard_map/ppermute | solution.py:23
  88.4 36.8 %collective-permute-start.18 = (f32[64,640]{1,0:T(8,128)S(1)}, f32[64,640]{1,0:T(8,128)S(1)}, u32[]{:S(2)}, u32[]{:S(2)}) collective-permute-start(f32[64,640]{1,0:T(8,128)S(1)} %get-tuple-element.147), channel_id=1, source_target_pairs={{0,8},{1,9},{2,10},{3,11},{4,12},{5,13},{6,14},{7,15},{8,0},{9,1},... | collective-permute-start | bytes 491528 | tf_op jit(solution)/shard_map/ppermute | solution.py:23
  94.3 32.5 %collective-permute-start.17 = (f32[64,640]{1,0:T(8,128)S(1)}, f32[64,640]{1,0:T(8,128)S(1)}, u32[]{:S(2)}, u32[]{:S(2)}) collective-permute-start(f32[64,640]{1,0:T(8,128)S(1)} %get-tuple-element.145), channel_id=1, source_target_pairs={{0,4},{1,5},{2,6},{3,7},{4,8},{5,9},{6,10},{7,11},{8,12},{9,13},{1... | collective-permute-start | bytes 491528 | tf_op jit(solution)/shard_map/ppermute | solution.py:23
  122.7 9.5 %collective-permute-start.8 = (bf16[128,768]{1,0:T(8,128)(2,1)}, bf16[128,768]{1,0:T(8,128)(2,1)}, u32[]{:S(2)}, u32[]{:S(2)}) collective-permute-start(bf16[128,768]{1,0:T(8,128)(2,1)} %convolution_convert_fusion.9), channel_id=1, source_target_pairs={{0,1},{1,2},{2,3},{3,0},{4,5},{5,6},{6,7},{7,4},{8,9},{9,10},{10,1... | collective-permute-start | bytes 589832 | tf_op jit(solution)/shard_map/ppermute | solution.py:23
  129.2 9.1 %copy-start.21 = (f32[6,5]{1,0:T(8,128)S(1)}, f32[6,5]{1,0:T(8,128)}, u32[]{:S(2)}) copy-start(f32[6,5]{1,0:T(8,128)} %param.35) | copy-start | bytes 364
  140.6 1.5 copy-start.3
  142.8 7.3 %copy-start.6 = (f32[64,5,128]{2,1,0:T(8,128)S(1)}, f32[64,5,128]{2,1,0:T(8,128)}, u32[]{:S(2)}) copy-start(f32[64,5,128]{2,1,0:T(8,128)} %reshape.945) | copy-start | bytes 491524
  142.9 22.8 %collective-permute-start.13 = (bf16[1,4,80,128]{3,2,1,0:T(8,128)(2,1)S(1)}, bf16[1,4,80,128]{3,2,1,0:T(8,128)(2,1)S(1)}, u32[]{:S(2)}, u32[]{:S(2)}) collective-permute-start(bf16[1,4,80,128]{3,2,1,0:T(8,128)(2,1)S(1)} %get-tuple-element.153), channel_id=1, source_target_pairs={{0,16},{16,32},{32,48},{48,64},{64,80},{80,96},{96,112},{112,128},... | collective-permute-start | bytes 245768 | tf_op jit(solution)/shard_map/ppermute | solution.py:14
  145.9 15.1 %collective-permute-start.15 = (bf16[2,1,80,128]{3,2,1,0:T(8,128)(2,1)S(1)}, bf16[2,1,80,128]{3,2,1,0:T(8,128)(2,1)S(1)}, u32[]{:S(2)}, u32[]{:S(2)}) collective-permute-start(bf16[2,1,80,128]{3,2,1,0:T(8,128)(2,1)S(1)} %slice.688), channel_id=1, source_target_pairs={{0,1},{1,2},{2,3},{3,4},{4,5},{5,6},{6,7},{7,8},{8,9},{9,10},{10,1... | collective-permute-start | bytes 122888 | tf_op jit(solution)/shard_map/ppermute | solution.py:14
  148.8 14.3 %collective-permute-start.16 = (bf16[2,1,80,128]{3,2,1,0:T(8,128)(2,1)S(1)}, bf16[2,1,80,128]{3,2,1,0:T(8,128)(2,1)S(1)}, u32[]{:S(2)}, u32[]{:S(2)}) collective-permute-start(bf16[2,1,80,128]{3,2,1,0:T(8,128)(2,1)S(1)} %slice.693), channel_id=1, source_target_pairs={{1,0},{2,1},{3,2},{4,3},{5,4},{6,5},{7,6},{8,7},{9,8},{10,9},{11,1... | collective-permute-start | bytes 122888 | tf_op jit(solution)/shard_map/ppermute | solution.py:14
  151.8 14.0 %copy-start.1 = (f32[2,4,4,4,4,5,128]{6,1,5,4,3,2,0:T(4,128)S(1)}, f32[2,4,4,4,4,5,128]{6,1,5,4,3,2,0:T(4,128)}, u32[]{:S(2)}) copy-start(f32[2,4,4,4,4,5,128]{6,1,5,4,3,2,0:T(4,128)} %copy.126) | copy-start | bytes 3932164
  151.8 17.5 %collective-permute-start.28 = (bf16[128,640]{1,0:T(8,128)(2,1)S(1)}, bf16[128,640]{1,0:T(8,128)(2,1)S(1)}, u32[]{:S(2)}, u32[]{:S(2)}) collective-permute-start(bf16[128,640]{1,0:T(8,128)(2,1)S(1)} %bitcast.160), channel_id=1, source_target_pairs={{0,3},{1,0},{2,1},{3,2},{4,7},{5,4},{6,5},{7,6},{8,11},{9,8},{10,9... | collective-permute-start | bytes 491528 | tf_op jit(solution)/shard_map/ppermute | solution.py:23
  155.9 13.4 %collective-permute-start.27 = (bf16[128,640]{1,0:T(8,128)(2,1)S(1)}, bf16[128,640]{1,0:T(8,128)(2,1)S(1)}, u32[]{:S(2)}, u32[]{:S(2)}) collective-permute-start(bf16[128,640]{1,0:T(8,128)(2,1)S(1)} %bitcast.161), channel_id=1, source_target_pairs={{0,2},{1,3},{2,0},{3,1},{4,6},{5,7},{6,4},{7,5},{8,10},{9,11},{10,... | collective-permute-start | bytes 491528 | tf_op jit(solution)/shard_map/ppermute | solution.py:23
  160.2 9.4 %copy-start.30 = (s32[512]{0:T(512)S(1)}, s32[512]{0:T(512)}, u32[]{:S(2)}) copy-start(s32[512]{0:T(512)} %copy-done.29) | copy-start | bytes 6148
  160.3 9.4 %copy-start.32 = (s32[256]{0:T(256)S(1)}, s32[256]{0:T(256)}, u32[]{:S(2)}) copy-start(s32[256]{0:T(256)} %add.261) | copy-start | bytes 3076
  161.0 8.6 %collective-permute-start.26 = (bf16[128,640]{1,0:T(8,128)(2,1)S(1)}, bf16[128,640]{1,0:T(8,128)(2,1)S(1)}, u32[]{:S(2)}, u32[]{:S(2)}) collective-permute-start(bf16[128,640]{1,0:T(8,128)(2,1)S(1)} %bitcast.162), channel_id=1, source_target_pairs={{0,1},{1,2},{2,3},{3,0},{4,5},{5,6},{6,7},{7,4},{8,9},{9,10},{10,1... | collective-permute-start | bytes 491528 | tf_op jit(solution)/shard_map/ppermute | solution.py:23
  163.1 6.1 %collective-permute-start.14 = (bf16[1,4,80,128]{3,2,1,0:T(8,128)(2,1)S(1)}, bf16[1,4,80,128]{3,2,1,0:T(8,128)(2,1)S(1)}, u32[]{:S(2)}, u32[]{:S(2)}) collective-permute-start(bf16[1,4,80,128]{3,2,1,0:T(8,128)(2,1)S(1)} %get-tuple-element.151), channel_id=1, source_target_pairs={{16,0},{32,16},{48,32},{64,48},{80,64},{96,80},{112,96},{128,112},... | collective-permute-start | bytes 245768 | tf_op jit(solution)/shard_map/ppermute | solution.py:14
  170.1 28.9 %collective-permute-start.31 = (f32[64,640]{1,0:T(8,128)S(1)}, f32[64,640]{1,0:T(8,128)S(1)}, u32[]{:S(2)}, u32[]{:S(2)}) collective-permute-start(f32[64,640]{1,0:T(8,128)S(1)} %get-tuple-element.143), channel_id=1, source_target_pairs={{0,12},{1,13},{2,14},{3,15},{4,0},{5,1},{6,2},{7,3},{8,4},{9,5},{1... | collective-permute-start | bytes 491528 | tf_op jit(solution)/shard_map/ppermute | solution.py:23
  176.6 25.3 %collective-permute-start.30 = (f32[64,640]{1,0:T(8,128)S(1)}, f32[64,640]{1,0:T(8,128)S(1)}, u32[]{:S(2)}, u32[]{:S(2)}) collective-permute-start(f32[64,640]{1,0:T(8,128)S(1)} %get-tuple-element.144), channel_id=1, source_target_pairs={{0,8},{1,9},{2,10},{3,11},{4,12},{5,13},{6,14},{7,15},{8,0},{9,1},... | collective-permute-start | bytes 491528 | tf_op jit(solution)/shard_map/ppermute | solution.py:23
  183.8 25.9 %collective-permute-start.29 = (f32[64,640]{1,0:T(8,128)S(1)}, f32[64,640]{1,0:T(8,128)S(1)}, u32[]{:S(2)}, u32[]{:S(2)}) collective-permute-start(f32[64,640]{1,0:T(8,128)S(1)} %get-tuple-element.142), channel_id=1, source_target_pairs={{0,4},{1,5},{2,6},{3,7},{4,8},{5,9},{6,10},{7,11},{8,12},{9,13},{1... | collective-permute-start | bytes 491528 | tf_op jit(solution)/shard_map/ppermute | solution.py:23
  212.1 7.9 %copy-start.7 = (bf16[2,3,4,1,4,5,128]{6,1,5,4,3,2,0:T(4,128)(2,1)S(1)}, bf16[2,3,4,1,4,5,128]{6,1,5,4,3,2,0:T(4,128)(2,1)}, u32[]{:S(2)}) copy-start(bf16[2,3,4,1,4,5,128]{6,1,5,4,3,2,0:T(4,128)(2,1)} %copy.70) | copy-start | bytes 368644
  212.1 7.9 %copy-start.19 = (bf16[2,1,4,1,4,5,128]{6,1,5,4,3,2,0:T(2,128)(2,1)S(1)}, bf16[2,1,4,1,4,5,128]{6,1,5,4,3,2,0:T(2,128)(2,1)}, u32[]{:S(2)}) copy-start(bf16[2,1,4,1,4,5,128]{6,1,5,4,3,2,0:T(2,128)(2,1)} %copy.71) | copy-start | bytes 122884
  214.6 32.5 %copy-start.23 = (s32[128]{0:T(128)S(1)}, s32[128]{0:T(128)}, u32[]{:S(2)}) copy-start(s32[128]{0:T(128)} %copy-done.22) | copy-start | bytes 1540
  215.2 32.1 %copy-start.25 = (s32[128]{0:T(128)S(1)}, s32[128]{0:T(128)}, u32[]{:S(2)}) copy-start(s32[128]{0:T(128)} %copy-done.24) | copy-start | bytes 1540
  215.3 32.4 %copy-start.27 = (s32[128]{0:T(128)S(1)}, s32[128]{0:T(128)}, u32[]{:S(2)}) copy-start(s32[128]{0:T(128)} %copy-done.26) | copy-start | bytes 1540
  215.3 16.7 %collective-permute-start.20 = (bf16[64,768]{1,0:T(8,128)(2,1)S(1)}, bf16[64,768]{1,0:T(8,128)(2,1)S(1)}, u32[]{:S(2)}, u32[]{:S(2)}) collective-permute-start(bf16[64,768]{1,0:T(8,128)(2,1)S(1)} %get-tuple-element.139), channel_id=1, source_target_pairs={{0,4},{1,5},{2,6},{3,7},{4,8},{5,9},{6,10},{7,11},{8,12},{9,13},{1... | collective-permute-start | bytes 294920 | tf_op jit(solution)/shard_map/ppermute | solution.py:23
  220.3 16.4 %collective-permute-start.21 = (bf16[64,768]{1,0:T(8,128)(2,1)S(1)}, bf16[64,768]{1,0:T(8,128)(2,1)S(1)}, u32[]{:S(2)}, u32[]{:S(2)}) collective-permute-start(bf16[64,768]{1,0:T(8,128)(2,1)S(1)} %get-tuple-element.139), channel_id=1, source_target_pairs={{0,8},{1,9},{2,10},{3,11},{4,12},{5,13},{6,14},{7,15},{8,0},{9,1},... | collective-permute-start | bytes 294920 | tf_op jit(solution)/shard_map/ppermute | solution.py:23
  225.2 21.9 %collective-permute-start.22 = (bf16[64,768]{1,0:T(8,128)(2,1)S(1)}, bf16[64,768]{1,0:T(8,128)(2,1)S(1)}, u32[]{:S(2)}, u32[]{:S(2)}) collective-permute-start(bf16[64,768]{1,0:T(8,128)(2,1)S(1)} %get-tuple-element.139), channel_id=1, source_target_pairs={{0,12},{1,13},{2,14},{3,15},{4,0},{5,1},{6,2},{7,3},{8,4},{9,5},{1... | collective-permute-start | bytes 294920 | tf_op jit(solution)/shard_map/ppermute | solution.py:23
  247.9 9.5 %collective-permute-start.25 = (bf16[128,768]{1,0:T(8,128)(2,1)S(1)}, bf16[128,768]{1,0:T(8,128)(2,1)S(1)}, u32[]{:S(2)}, u32[]{:S(2)}) collective-permute-start(bf16[128,768]{1,0:T(8,128)(2,1)S(1)} %convolution_convert_fusion.3), channel_id=1, source_target_pairs={{0,3},{1,0},{2,1},{3,2},{4,7},{5,4},{6,5},{7,6},{8,11},{9,8},{10,9... | collective-permute-start | bytes 589832 | tf_op jit(solution)/shard_map/ppermute | solution.py:23
  251.6 9.1 %collective-permute-start.24 = (bf16[128,768]{1,0:T(8,128)(2,1)S(1)}, bf16[128,768]{1,0:T(8,128)(2,1)S(1)}, u32[]{:S(2)}, u32[]{:S(2)}) collective-permute-start(bf16[128,768]{1,0:T(8,128)(2,1)S(1)} %convolution_convert_fusion.4), channel_id=1, source_target_pairs={{0,2},{1,3},{2,0},{3,1},{4,6},{5,7},{6,4},{7,5},{8,10},{9,11},{10,... | collective-permute-start | bytes 589832 | tf_op jit(solution)/shard_map/ppermute | solution.py:23
  253.7 12.3 %collective-permute-start.23 = (bf16[128,768]{1,0:T(8,128)(2,1)S(1)}, bf16[128,768]{1,0:T(8,128)(2,1)S(1)}, u32[]{:S(2)}, u32[]{:S(2)}) collective-permute-start(bf16[128,768]{1,0:T(8,128)(2,1)S(1)} %convolution_convert_fusion.5), channel_id=1, source_target_pairs={{0,1},{1,2},{2,3},{3,0},{4,5},{5,6},{6,7},{7,4},{8,9},{9,10},{10,1... | collective-permute-start | bytes 589832 | tf_op jit(solution)/shard_map/ppermute | solution.py:23
  (1 other events, 0.6 us)
